TPU v7x, 32 devices: a whole 2x2x4 slice. The times are simulated.
32 devices in a mesh: section: 2 (over core), dp: 4 (over y, x), mp: 4 (over z).
Axes of the slice: x: 2, y: 2, z: 4, core: 2. Of those that a mesh axis runs over, the one named last changes fastest.
Arguments:
- student_hidden: bfloat16 [768, 2432], P('mp'), may hold values from -20 to 20
- student_weight: float32 [2432, 64], P(('section', 'mp'), 'dp'), may hold values from -6 to 6
- student_ema: float32 [2432, 64], P(('section', 'mp'), 'dp'), may hold values from -6 to 6
- noise: bfloat16 [768, 64], P('mp'), may hold values from -6 to 6
- timesteps: int32 [8], P('mp'), may hold values from 0 to 7
- patch_embed: bfloat16 [64, 2432], replicated, may hold values from -0.75 to 0.75
- teacher_weight: bfloat16 [2, 4, 2432, 2432], P('section', None, 'mp', 'dp'), may hold values from -0.125 to 0.125
- modulation: bfloat16 [2, 4, 8, 2, 2432], P('section'), may hold values from -3 to 3
- layer_counts: int32 [2], P('section'), may hold values from 1 to 4, as said below
- feature_layers: int32 [2], replicated, may hold values from 0 to 7, as said below
- head_routes: int32 [2, 768, 1], P(None, 'mp'), may hold values from 0 to 3; in each aligned block of 192 rows (0 to 191, 192 to 383, ..., all dimensions but the last counted through in order) at most 60 rows name the same one
- head_owner: int32 [2, 4], replicated, may hold values from 0 to 3, each once within a row
- head_in: bfloat16 [2, 4, 2432, 256], P(None, 'mp'), may hold values from -0.125 to 0.125
- head_out: bfloat16 [2, 4, 256], P(None, 'mp'), may hold values from -0.375 to 0.375
Outputs:
- student_update: float32 [2432, 64], P(('section', 'mp'), 'dp')
- ema_new: float32 [2432, 64], P(('section', 'mp'), 'dp')
Inputs may be any that keep to these rules, and one draw needn't show every extreme that they name: Each section runs its first layer_counts slots; some section runs all 4, some other section fewer. `feature_layers`: the first names a slot of the first section, the second a slot of the last section. `head_routes`: within the rows of one device no head is named by more than 60 rows of one tapped slot. `head_owner`: each row names every owner once.
All inputs are finite; a program needn't handle non-finite values.
Results may differ from a plain program's by a relative error of at most 0.015.
Values may be sent and summed in bfloat16 or wider, within the bound.
No kernel may reach another device: no remote copies, remote signals or barrier semaphores. Data moves between devices by JAX's collectives and lax.ppermute only.
A program may use at most 192 MiB of HBM per device.

v0:
```python
import math

import jax
import jax.numpy as jnp
from jax import lax
from jax.sharding import PartitionSpec as P

D = 2432
LAT = 64


norm_eps = 1e-06
ema_decay = 0.99
step_size = 0.05


def passed_along(block, axis, distance):
    devices = range(lax.axis_size(axis))
    route = [(i - distance, i) for i in devices if i - distance in devices]
    return lax.ppermute(block, axis, route)


def spread(value, axis, root):
    mine = lax.axis_index(axis) == root
    return lax.psum(jnp.where(mine, value, jnp.zeros_like(value)), axis)


def gelu_slope(values):
    return jax.vjp(jax.nn.gelu, values)[1](jnp.ones_like(values))[0]


def norm_back(normed, inverse, upstream):
    return inverse * (upstream - normed * jnp.mean(upstream * normed, axis=-1, keepdims=True))


def head_grads(features, w_first, w_second, live_mask, loss_scale):
    feat_wide = features.astype(jnp.float32)
    inverse = lax.rsqrt(jnp.mean(feat_wide * feat_wide, axis=-1, keepdims=True) + norm_eps)
    normed = feat_wide * inverse
    hidden_pre = jnp.dot(normed.astype(jnp.bfloat16), w_first, preferred_element_type=jnp.float32)
    hidden_act = jax.nn.gelu(hidden_pre).astype(jnp.bfloat16)
    logits = jnp.dot(hidden_act, w_second, preferred_element_type=jnp.float32)
    logit_grad = -loss_scale * jax.nn.sigmoid(-logits) * live_mask
    act_grad = logit_grad[:, None] * w_second.astype(jnp.float32)[None, :]
    pre_grad = (act_grad * gelu_slope(hidden_pre)).astype(jnp.bfloat16)
    normed_grad = jnp.dot(pre_grad, w_first.T, preferred_element_type=jnp.float32)
    return norm_back(normed, inverse, normed_grad).astype(jnp.bfloat16)


def put_rows(buffer, slot_index, offset, values, condition):
    zero_at = jnp.int32(0)
    start_at = (jnp.int32(slot_index), offset, zero_at)
    previous = lax.dynamic_slice(buffer, start_at, (1, values.shape[0], values.shape[1]))[0]
    merged = jnp.where(condition, values, previous)
    return lax.dynamic_update_slice(buffer, merged[None], start_at)


def take_rows(buffer, slot_index, offset, row_total):
    zero_at = jnp.int32(0)
    return lax.dynamic_slice(
        buffer, (jnp.int32(slot_index), offset, zero_at), (1, row_total, buffer.shape[2])
    )[0]


def on_device(
    student_hidden,
    student_weight,
    student_ema,
    noise,
    timesteps,
    patch_embed,
    teacher_weight,
    modulation,
    layer_counts,
    feature_layers,
    head_routes,
    head_owner,
    head_in,
    head_out,
):
    row_count = student_hidden.shape[0]
    width = student_hidden.shape[1]
    segments = lax.axis_size("section")
    data_size = lax.axis_size("mp")
    model_size = lax.axis_size("dp")
    segment_at = lax.axis_index("section")
    model_at = lax.axis_index("dp")
    slot_count = teacher_weight.shape[1]
    levels = modulation.shape[2]
    col_width = width // model_size
    t_rows = jnp.repeat(timesteps, row_count // timesteps.shape[0])
    noise_level = ((t_rows + 1).astype(jnp.float32) / (levels + 1))[:, None]
    student_rows = lax.all_gather(
        student_weight.astype(jnp.bfloat16), ("section", "mp"), axis=0, tiled=True
    )
    latent_part = (
        jnp.dot(student_hidden, student_rows, preferred_element_type=jnp.float32) * width ** (-0.5)
    ).astype(jnp.bfloat16)
    latents = lax.all_gather(latent_part, "dp", axis=1, tiled=True)
    noisy_input = (
        (1.0 - noise_level) * latents.astype(jnp.float32) + noise_level * noise.astype(jnp.float32)
    ).astype(jnp.bfloat16)
    start_stream = jnp.dot(noisy_input, patch_embed, preferred_element_type=jnp.float32)
    weights = lax.all_gather(teacher_weight, "mp", axis=2, tiled=True)[0]
    level_hot = (t_rows[:, None] == jnp.arange(levels, dtype=jnp.int32)[None, :]).astype(
        jnp.bfloat16
    )
    mod_rows = jnp.einsum(
        "rn,lnd->lrd",
        level_hot,
        modulation[0].reshape(slot_count, levels, 2 * width),
        preferred_element_type=jnp.float32,
    )
    active = (jnp.arange(slot_count, dtype=jnp.int32) < layer_counts[0]).astype(jnp.float32)
    blocks = 4
    block_rows = row_count // blocks
    ticks = blocks + segments - 1
    stream_store = jnp.zeros((slot_count, row_count, width), jnp.float32)
    pre_store = jnp.zeros((slot_count, row_count, col_width), jnp.float32)
    tap_store = jnp.zeros((row_count, width), jnp.bfloat16)
    incoming = jnp.zeros((block_rows, width), jnp.bfloat16)
    for tick_no in range(ticks):
        block_no = tick_no - segment_at
        is_live = (block_no >= 0) & (block_no < blocks)
        offset = jnp.clip(block_no, 0, blocks - 1) * block_rows
        first_block = lax.dynamic_slice_in_dim(start_stream, offset, block_rows, 0)
        stream = jnp.where(segment_at == 0, first_block, incoming.astype(jnp.float32))
        for slot_no in range(slot_count):
            scale_rows = lax.dynamic_slice(
                mod_rows[slot_no], (offset, jnp.int32(0)), (block_rows, width)
            )
            gate_cols = lax.dynamic_slice(
                mod_rows[slot_no], (offset, width + model_at * col_width), (block_rows, col_width)
            )
            stream_store = put_rows(stream_store, slot_no, offset, stream, is_live)
            inverse = lax.rsqrt(jnp.mean(stream * stream, axis=-1, keepdims=True) + norm_eps)
            normed_in = (stream * inverse * (1.0 + scale_rows)).astype(jnp.bfloat16)
            pre_act = jnp.dot(normed_in, weights[slot_no], preferred_element_type=jnp.float32)
            pre_store = put_rows(pre_store, slot_no, offset, pre_act, is_live)
            part_out = (active[slot_no] * gate_cols * jax.nn.gelu(pre_act)).astype(jnp.bfloat16)
            joined = lax.all_gather(part_out, "dp", axis=1, tiled=True)
            stream = stream + joined.astype(jnp.float32)
            global_slot = segment_at * slot_count + slot_no
            tap_hit = is_live & (
                (global_slot == feature_layers[0]) | (global_slot == feature_layers[1])
            )
            previous_tap = lax.dynamic_slice_in_dim(tap_store, offset, block_rows, 0)
            new_tap = jnp.where(tap_hit, stream.astype(jnp.bfloat16), previous_tap)
            tap_store = lax.dynamic_update_slice_in_dim(tap_store, new_tap, offset, 0)
        if tick_no + 1 < ticks:
            incoming = passed_along(stream.astype(jnp.bfloat16), "section", 1)
    capacity = 5 * row_count // (4 * data_size)
    owner_range = jnp.arange(data_size, dtype=jnp.int32)
    tap_mine = (feature_layers[1] // slot_count == segment_at).astype(jnp.int32)
    holding = (
        (feature_layers[0] // slot_count == segment_at)
        | (feature_layers[1] // slot_count == segment_at)
    ).astype(jnp.float32)
    routes = jnp.where(tap_mine == 1, head_routes[1, :, 0], head_routes[0, :, 0])
    owners_map = jnp.where(tap_mine == 1, head_owner[1], head_owner[0])
    route_hot = (routes[:, None] == owner_range[None, :]).astype(jnp.int32)
    owner_ids = jnp.sum(route_hot * owners_map[None, :], axis=1)
    owner_hot = (owner_ids[:, None] == owner_range[None, :]).astype(jnp.int32)
    position = jnp.sum(owner_hot * (jnp.cumsum(owner_hot, axis=0) - 1), axis=1)
    target = owner_ids * capacity + position
    dispatch = (
        target[:, None] == jnp.arange(data_size * capacity, dtype=jnp.int32)[None, :]
    ).astype(jnp.bfloat16)
    send_feat = (
        jnp.dot(dispatch.T, tap_store, preferred_element_type=jnp.float32)
        .astype(jnp.bfloat16)
        .reshape(data_size, capacity, width)
    )
    send_live = (
        (jnp.sum(dispatch.astype(jnp.float32), axis=0) * holding)
        .reshape(data_size, capacity)
        .astype(jnp.bfloat16)
    )
    loss_scale = width / math.sqrt(row_count * data_size)
    w_first = lax.dynamic_index_in_dim(head_in[:, 0], tap_mine, 0, keepdims=False)
    w_second = lax.dynamic_index_in_dim(head_out[:, 0], tap_mine, 0, keepdims=False)
    recv_feat = lax.all_to_all(send_feat, "mp", split_axis=0, concat_axis=0, tiled=True)
    recv_live = lax.all_to_all(send_live, "mp", split_axis=0, concat_axis=0, tiled=True)
    sources = recv_feat.shape[0]
    item_count = recv_feat.shape[1]
    flat_feat = recv_feat.reshape(sources * item_count, width)
    live_flat = recv_live.reshape(sources * item_count).astype(jnp.float32)
    head_result = head_grads(flat_feat, w_first, w_second, live_flat, loss_scale)
    returned = lax.all_to_all(
        head_result.reshape(sources, item_count, width),
        "mp",
        split_axis=0,
        concat_axis=0,
        tiled=True,
    )
    tap_grads = jnp.dot(
        dispatch, returned.reshape(data_size * capacity, width), preferred_element_type=jnp.float32
    )
    start_grad = jnp.zeros((row_count, width), jnp.float32)
    incoming = jnp.zeros((block_rows, width), jnp.bfloat16)
    for tick_no in range(ticks):
        block_no = tick_no - (segments - 1 - segment_at)
        is_live = (block_no >= 0) & (block_no < blocks)
        offset = jnp.clip(block_no, 0, blocks - 1) * block_rows
        grad_stream = jnp.where(segment_at == segments - 1, 0.0, incoming.astype(jnp.float32))
        for slot_no in reversed(range(slot_count)):
            global_slot = segment_at * slot_count + slot_no
            tap_hit = (global_slot == feature_layers[0]) | (global_slot == feature_layers[1])
            grad_stream = grad_stream + jnp.where(
                tap_hit, lax.dynamic_slice_in_dim(tap_grads, offset, block_rows, 0), 0.0
            )
            stream_in = take_rows(stream_store, slot_no, offset, block_rows)
            pre_act = take_rows(pre_store, slot_no, offset, block_rows)
            scale_rows = lax.dynamic_slice(
                mod_rows[slot_no], (offset, jnp.int32(0)), (block_rows, width)
            )
            gate_cols = lax.dynamic_slice(
                mod_rows[slot_no], (offset, width + model_at * col_width), (block_rows, col_width)
            )
            inverse = lax.rsqrt(jnp.mean(stream_in * stream_in, axis=-1, keepdims=True) + norm_eps)
            grad_cols = lax.dynamic_slice_in_dim(grad_stream, model_at * col_width, col_width, 1)
            pre_grad = (grad_cols * active[slot_no] * gate_cols * gelu_slope(pre_act)).astype(
                jnp.bfloat16
            )
            input_grad = lax.psum(
                jnp.dot(pre_grad, weights[slot_no].T, preferred_element_type=jnp.float32).astype(
                    jnp.bfloat16
                ),
                "dp",
            ).astype(jnp.float32)
            grad_stream = grad_stream + norm_back(
                stream_in * inverse, inverse, input_grad * (1.0 + scale_rows)
            )
        previous = lax.dynamic_slice_in_dim(start_grad, offset, block_rows, 0)
        merged = jnp.where(is_live & (segment_at == 0), grad_stream, previous)
        start_grad = lax.dynamic_update_slice_in_dim(start_grad, merged, offset, 0)
        if tick_no + 1 < ticks:
            incoming = passed_along(grad_stream.astype(jnp.bfloat16), "section", -1)
    latent_pre = jnp.dot(
        start_grad.astype(jnp.bfloat16), patch_embed.T, preferred_element_type=jnp.float32
    )
    latent_grad = ((1.0 - noise_level) * latent_pre).astype(jnp.bfloat16)
    latent_grad = spread(latent_grad, "section", 0)
    lat_part = student_weight.shape[1]
    my_latent = lax.dynamic_slice_in_dim(latent_grad, model_at * lat_part, lat_part, 1)
    segment_block = width // segments
    own_rows = student_weight.shape[0]
    hidden_cols = lax.dynamic_slice_in_dim(
        student_hidden, segment_at * segment_block, segment_block, 1
    )
    whole_grad = lax.psum(
        lax.dot_general(
            hidden_cols, my_latent, (((0,), (0,)), ((), ())), preferred_element_type=jnp.float32
        )
        * width ** (-0.5),
        "mp",
    )
    student_grad = lax.dynamic_slice_in_dim(
        whole_grad, lax.axis_index("mp") * own_rows, own_rows, 0
    )
    total_sq = lax.psum(jnp.sum(student_grad * student_grad), ("section", "dp", "mp"))
    mean_square = total_sq / (D * LAT)
    student_update = student_grad * lax.rsqrt(mean_square + norm_eps)
    ema_new = ema_decay * student_ema + (1.0 - ema_decay) * (
        student_weight - step_size * student_update
    )
    return (student_update, ema_new)


def solution(mesh):
    in_specs = (
        P("mp", None),
        P(("section", "mp"), "dp"),
        P(("section", "mp"), "dp"),
        P("mp", None),
        P("mp"),
        P(),
        P("section", None, "mp", "dp"),
        P("section", None, None, None, None),
        P("section"),
        P(),
        P(None, "mp", None),
        P(),
        P(None, "mp", None, None),
        P(None, "mp", None),
    )
    out_specs = (P(("section", "mp"), "dp"), P(("section", "mp"), "dp"))
    return jax.shard_map(
        on_device, mesh=mesh, in_specs=in_specs, out_specs=out_specs, check_vma=False
    )
```

profile of v0, /device:TPU:0, one launch (start us, length us, event | category | flops | bytes accessed | tf_op | source)
XLA Modules:
  0.0 1887.5 jit_solution(5833604745598814442)
XLA Ops:
  32.6 33.9 %all-gather = bf16[8,304,16]{1,2,0:T(8,128)(2,1)S(1)} all-gather(bf16[1,304,16]{1,2,0:T(8,128)(2,1)S(1)} %convert_bitcast_fusion), channel_id=1, replica_groups=mesh['section'=2,'dp'=4,'mp'=4] {'section','mp'}, dimensions={0}, use_global_device_ids=true | all-gather | bytes 87552 | tf_op jit(solution)/shard_map/all_gather | solution.py:93
  71.0 9.0 all_gather.70
  94.3 11.0 fusion.908
  105.3 125.0 %all-gather.23.cloned.1.call-done = bf16[1,4,2432,608]{3,2,1,0:T(8,128)(2,1)} async-done(((bf16[1,4,608,608]{3,2,1,0:T(8,128)(2,1)}), bf16[1,4,2432,608]{3,2,1,0:T(8,128)(2,1)}) %all-gather.23.cloned.1.call-update) | async-done | bytes 11829264 | tf_op jit(solution)/shard_map/all_gather | solution.py:104
  236.8 8.9 all-gather.1
  255.0 8.9 all-gather.2
  405.3 8.9 all-gather.9
  495.7 8.9 all-gather.13
  675.3 20.5 %all-to-all-done = bf16[4,60,2432]{2,1,0:T(8,128)(2,1)} async-done(((bf16[4,60,2432]{2,1,0:T(8,128)(2,1)}), bf16[4,60,2432]{2,1,0:T(8,128)(2,1)}, u32[]{:S(2)}, u32[]{:S(2)}) %all-to-all-start) | async-done | bytes 1167392 | tf_op jit(solution)/shard_map/all_to_all | solution.py:182
  717.5 25.8 %all-to-all-done.2 = bf16[4,60,2432]{2,1,0:T(8,128)(2,1)} async-done(((bf16[4,60,2432]{2,1,0:T(8,128)(2,1)}), bf16[4,60,2432]{2,1,0:T(8,128)(2,1)}, u32[]{:S(2)}, u32[]{:S(2)}) %all-to-all-start.2) | async-done | bytes 1167392 | tf_op jit(solution)/shard_map/all_to_all | solution.py:189
  754.2 39.7 %all-reduce.23.cloned.1.call-done = bf16[48,2432]{1,0:T(8,128)(2,1)} async-done(((bf16[48,2432]{1,0:T(8,128)(2,1)}), bf16[48,2432]{1,0:T(8,128)(2,1)}) %all-reduce.23.cloned.1.call-update) | async-done | bytes 233488 | tf_op jit(solution)/shard_map/psum | solution.py:225
  805.2 43.0 %all-reduce.25.cloned.1.call-done = bf16[48,2432]{1,0:T(8,128)(2,1)} async-done(((bf16[48,2432]{1,0:T(8,128)(2,1)}), bf16[48,2432]{1,0:T(8,128)(2,1)}) %all-reduce.25.cloned.1.call-update) | async-done | bytes 233488 | tf_op jit(solution)/shard_map/psum | solution.py:225
  855.7 43.0 %all-reduce.27.cloned.1.call-done = bf16[48,2432]{1,0:T(8,128)(2,1)} async-done(((bf16[48,2432]{1,0:T(8,128)(2,1)}), bf16[48,2432]{1,0:T(8,128)(2,1)}) %all-reduce.27.cloned.1.call-update) | async-done | bytes 233488 | tf_op jit(solution)/shard_map/psum | solution.py:225
  907.0 43.0 %all-reduce.29.cloned.1.call-done = bf16[48,2432]{1,0:T(8,128)(2,1)} async-done(((bf16[48,2432]{1,0:T(8,128)(2,1)}), bf16[48,2432]{1,0:T(8,128)(2,1)}) %all-reduce.29.cloned.1.call-update) | async-done | bytes 233488 | tf_op jit(solution)/shard_map/psum | solution.py:225
  964.3 42.8 %all-reduce.31.cloned.1.call-done = bf16[48,2432]{1,0:T(8,128)(2,1)} async-done(((bf16[48,2432]{1,0:T(8,128)(2,1)}), bf16[48,2432]{1,0:T(8,128)(2,1)}) %all-reduce.31.cloned.1.call-update) | async-done | bytes 233488 | tf_op jit(solution)/shard_map/psum | solution.py:225
  1015.6 43.0 %all-reduce.33.cloned.1.call-done = bf16[48,2432]{1,0:T(8,128)(2,1)} async-done(((bf16[48,2432]{1,0:T(8,128)(2,1)}), bf16[48,2432]{1,0:T(8,128)(2,1)}) %all-reduce.33.cloned.1.call-update) | async-done | bytes 233488 | tf_op jit(solution)/shard_map/psum | solution.py:225
  1067.0 43.0 %all-reduce.35.cloned.1.call-done = bf16[48,2432]{1,0:T(8,128)(2,1)} async-done(((bf16[48,2432]{1,0:T(8,128)(2,1)}), bf16[48,2432]{1,0:T(8,128)(2,1)}) %all-reduce.35.cloned.1.call-update) | async-done | bytes 233488 | tf_op jit(solution)/shard_map/psum | solution.py:225
  1118.4 43.0 %all-reduce.37.cloned.1.call-done = bf16[48,2432]{1,0:T(8,128)(2,1)} async-done(((bf16[48,2432]{1,0:T(8,128)(2,1)}), bf16[48,2432]{1,0:T(8,128)(2,1)}) %all-reduce.37.cloned.1.call-update) | async-done | bytes 233488 | tf_op jit(solution)/shard_map/psum | solution.py:225
  1174.2 43.0 %all-reduce.39.cloned.1.call-done = bf16[48,2432]{1,0:T(8,128)(2,1)} async-done(((bf16[48,2432]{1,0:T(8,128)(2,1)}), bf16[48,2432]{1,0:T(8,128)(2,1)}) %all-reduce.39.cloned.1.call-update) | async-done | bytes 233488 | tf_op jit(solution)/shard_map/psum | solution.py:225
  1225.7 43.0 %all-reduce.41.cloned.1.call-done = bf16[48,2432]{1,0:T(8,128)(2,1)} async-done(((bf16[48,2432]{1,0:T(8,128)(2,1)}), bf16[48,2432]{1,0:T(8,128)(2,1)}) %all-reduce.41.cloned.1.call-update) | async-done | bytes 233488 | tf_op jit(solution)/shard_map/psum | solution.py:225
  1277.2 43.0 %all-reduce.43.cloned.1.call-done = bf16[48,2432]{1,0:T(8,128)(2,1)} async-done(((bf16[48,2432]{1,0:T(8,128)(2,1)}), bf16[48,2432]{1,0:T(8,128)(2,1)}) %all-reduce.43.cloned.1.call-update) | async-done | bytes 233488 | tf_op jit(solution)/shard_map/psum | solution.py:225
  1328.6 43.0 %all-reduce.45.cloned.1.call-done = bf16[48,2432]{1,0:T(8,128)(2,1)} async-done(((bf16[48,2432]{1,0:T(8,128)(2,1)}), bf16[48,2432]{1,0:T(8,128)(2,1)}) %all-reduce.45.cloned.1.call-update) | async-done | bytes 233488 | tf_op jit(solution)/shard_map/psum | solution.py:225
  1384.4 42.9 %all-reduce.47.cloned.1.call-done = bf16[48,2432]{1,0:T(8,128)(2,1)} async-done(((bf16[48,2432]{1,0:T(8,128)(2,1)}), bf16[48,2432]{1,0:T(8,128)(2,1)}) %all-reduce.47.cloned.1.call-update) | async-done | bytes 233488 | tf_op jit(solution)/shard_map/psum | solution.py:225
  1435.9 43.0 %all-reduce.49.cloned.1.call-done = bf16[48,2432]{1,0:T(8,128)(2,1)} async-done(((bf16[48,2432]{1,0:T(8,128)(2,1)}), bf16[48,2432]{1,0:T(8,128)(2,1)}) %all-reduce.49.cloned.1.call-update) | async-done | bytes 233488 | tf_op jit(solution)/shard_map/psum | solution.py:225
  1487.6 42.7 %all-reduce.51.cloned.1.call-done = bf16[48,2432]{1,0:T(8,128)(2,1)} async-done(((bf16[48,2432]{1,0:T(8,128)(2,1)}), bf16[48,2432]{1,0:T(8,128)(2,1)}) %all-reduce.51.cloned.1.call-update) | async-done | bytes 233488 | tf_op jit(solution)/shard_map/psum | solution.py:225
  1538.7 43.0 %all-reduce.53.cloned.1.call-done = bf16[48,2432]{1,0:T(8,128)(2,1)} async-done(((bf16[48,2432]{1,0:T(8,128)(2,1)}), bf16[48,2432]{1,0:T(8,128)(2,1)}) %all-reduce.53.cloned.1.call-update) | async-done | bytes 233488 | tf_op jit(solution)/shard_map/psum | solution.py:225
  1594.5 43.0 %all-reduce.55.cloned.1.call-done = bf16[48,2432]{1,0:T(8,128)(2,1)} async-done(((bf16[48,2432]{1,0:T(8,128)(2,1)}), bf16[48,2432]{1,0:T(8,128)(2,1)}) %all-reduce.55.cloned.1.call-update) | async-done | bytes 233488 | tf_op jit(solution)/shard_map/psum | solution.py:225
  1646.1 43.0 %all-reduce.57.cloned.1.call-done = bf16[48,2432]{1,0:T(8,128)(2,1)} async-done(((bf16[48,2432]{1,0:T(8,128)(2,1)}), bf16[48,2432]{1,0:T(8,128)(2,1)}) %all-reduce.57.cloned.1.call-update) | async-done | bytes 233488 | tf_op jit(solution)/shard_map/psum | solution.py:225
  1697.5 43.0 %all-reduce.59.cloned.1.call-done = bf16[48,2432]{1,0:T(8,128)(2,1)} async-done(((bf16[48,2432]{1,0:T(8,128)(2,1)}), bf16[48,2432]{1,0:T(8,128)(2,1)}) %all-reduce.59.cloned.1.call-update) | async-done | bytes 233488 | tf_op jit(solution)/shard_map/psum | solution.py:225
  1748.9 43.0 %all-reduce.61.cloned.1.call-done = bf16[48,2432]{1,0:T(8,128)(2,1)} async-done(((bf16[48,2432]{1,0:T(8,128)(2,1)}), bf16[48,2432]{1,0:T(8,128)(2,1)}) %all-reduce.61.cloned.1.call-update) | async-done | bytes 233488 | tf_op jit(solution)/shard_map/psum | solution.py:225
  1801.7 34.4 %all-reduce.63.cloned.1.call-done = f32[1216,16]{0,1:T(8,128)} async-done(((f32[1216,16]{0,1:T(8,128)}), f32[1216,16]{0,1:T(8,128)}) %all-reduce.63.cloned.1.call-update) | async-done | bytes 77840 | tf_op jit(solution)/shard_map/psum | solution.py:251
  1837.6 40.5 %psum.183 = f32[]{:T(128)} all-reduce(f32[]{:T(128)} %multiply_reduce_fusion.42), channel_id=1, replica_groups=mesh['section'=2,'dp'=4,'mp'=4] {'section','dp','mp'}, use_global_device_ids=true, to_apply=%region_90.91 | all-reduce | flops 1 | bytes 8 | tf_op jit(solution)/shard_map/psum | solution.py:261
  (560 shorter events, 667.9 us)
Async XLA Ops:
  7.2 223.1 %all-gather.23.cloned.1.call-start = ((), (), s32[]{:S(2)}) async-start(), calls=%async_computation.3 | async-start | bytes 15564800 | tf_op jit(solution)/shard_map/all_gather | solution.py:104
  18.8 651.5 %all-to-all-start.1 = ((bf16[4,1,60]{2,1,0:T(2,128)(2,1)}), bf16[4,1,60]{2,1,0:T(2,128)(2,1)}, u32[]{:S(2)}, u32[]{:S(2)}) async-start(bf16[4,1,60]{2,1,0:T(2,128)(2,1)} %convert_element_type.788), calls=%async_computation.1 | async-start | bytes 4096 | tf_op jit(solution)/shard_map/all_to_all | solution.py:183
  306.2 4.3 collective-permute-start
  396.0 4.1 collective-permute-start.1
  486.0 4.5 collective-permute-start.2
  576.4 4.1 collective-permute-start.3
  670.2 25.6 %all-to-all-start = ((bf16[4,60,2432]{2,1,0:T(8,128)(2,1)}), bf16[4,60,2432]{2,1,0:T(8,128)(2,1)}, u32[]{:S(2)}, u32[]{:S(2)}) async-start(bf16[4,60,2432]{2,1,0:T(8,128)(2,1)} %reshape.733), calls=%async_computation | async-start | bytes 2490368 | tf_op jit(solution)/shard_map/all_to_all | solution.py:182
  713.2 30.1 %all-to-all-start.2 = ((bf16[4,60,2432]{2,1,0:T(8,128)(2,1)}), bf16[4,60,2432]{2,1,0:T(8,128)(2,1)}, u32[]{:S(2)}, u32[]{:S(2)}) async-start(bf16[4,60,2432]{2,1,0:T(8,128)(2,1)} %reshape.734), calls=%async_computation.2 | async-start | bytes 2490368 | tf_op jit(solution)/shard_map/all_to_all | solution.py:189
  717.5 76.4 %all-reduce.23.cloned.1.call-start = ((), (), s32[]{:S(2)}) async-start(), calls=%async_computation.4 | async-start | bytes 466944 | tf_op jit(solution)/shard_map/psum | solution.py:225
  753.0 95.2 %all-reduce.25.cloned.1.call-start = ((), (), s32[]{:S(2)}) async-start(), calls=%async_computation.5 | async-start | bytes 466944 | tf_op jit(solution)/shard_map/psum | solution.py:225
  805.2 93.6 %all-reduce.27.cloned.1.call-start = ((), (), s32[]{:S(2)}) async-start(), calls=%async_computation.6 | async-start | bytes 466944 | tf_op jit(solution)/shard_map/psum | solution.py:225
  855.7 94.3 %all-reduce.29.cloned.1.call-start = ((), (), s32[]{:S(2)}) async-start(), calls=%async_computation.7 | async-start | bytes 466944 | tf_op jit(solution)/shard_map/psum | solution.py:225
  906.9 100.1 %all-reduce.31.cloned.1.call-start = ((), (), s32[]{:S(2)}) async-start(), calls=%async_computation.8 | async-start | bytes 466944 | tf_op jit(solution)/shard_map/psum | solution.py:225
  953.8 3.7 collective-permute-start.4
  964.0 94.6 %all-reduce.33.cloned.1.call-start = ((), (), s32[]{:S(2)}) async-start(), calls=%async_computation.9 | async-start | bytes 466944 | tf_op jit(solution)/shard_map/psum | solution.py:225
  1015.5 94.5 %all-reduce.35.cloned.1.call-start = ((), (), s32[]{:S(2)}) async-start(), calls=%async_computation.10 | async-start | bytes 466944 | tf_op jit(solution)/shard_map/psum | solution.py:225
  1066.9 94.4 %all-reduce.37.cloned.1.call-start = ((), (), s32[]{:S(2)}) async-start(), calls=%async_computation.11 | async-start | bytes 466944 | tf_op jit(solution)/shard_map/psum | solution.py:225
  1118.3 98.9 %all-reduce.39.cloned.1.call-start = ((), (), s32[]{:S(2)}) async-start(), calls=%async_computation.12 | async-start | bytes 466944 | tf_op jit(solution)/shard_map/psum | solution.py:225
  1164.4 3.4 collective-permute-start.5
  1174.2 94.6 %all-reduce.41.cloned.1.call-start = ((), (), s32[]{:S(2)}) async-start(), calls=%async_computation.13 | async-start | bytes 466944 | tf_op jit(solution)/shard_map/psum | solution.py:225
  1225.7 94.5 %all-reduce.43.cloned.1.call-start = ((), (), s32[]{:S(2)}) async-start(), calls=%async_computation.14 | async-start | bytes 466944 | tf_op jit(solution)/shard_map/psum | solution.py:225
  1277.1 94.4 %all-reduce.45.cloned.1.call-start = ((), (), s32[]{:S(2)}) async-start(), calls=%async_computation.15 | async-start | bytes 466944 | tf_op jit(solution)/shard_map/psum | solution.py:225
  1328.5 98.8 %all-reduce.47.cloned.1.call-start = ((), (), s32[]{:S(2)}) async-start(), calls=%async_computation.16 | async-start | bytes 466944 | tf_op jit(solution)/shard_map/psum | solution.py:225
  1374.6 3.4 collective-permute-start.6
  1384.3 94.5 %all-reduce.49.cloned.1.call-start = ((), (), s32[]{:S(2)}) async-start(), calls=%async_computation.17 | async-start | bytes 466944 | tf_op jit(solution)/shard_map/psum | solution.py:225
  1435.8 94.5 %all-reduce.51.cloned.1.call-start = ((), (), s32[]{:S(2)}) async-start(), calls=%async_computation.18 | async-start | bytes 466944 | tf_op jit(solution)/shard_map/psum | solution.py:225
  1487.3 94.4 %all-reduce.53.cloned.1.call-start = ((), (), s32[]{:S(2)}) async-start(), calls=%async_computation.19 | async-start | bytes 466944 | tf_op jit(solution)/shard_map/psum | solution.py:225
  1538.7 98.9 %all-reduce.55.cloned.1.call-start = ((), (), s32[]{:S(2)}) async-start(), calls=%async_computation.20 | async-start | bytes 466944 | tf_op jit(solution)/shard_map/psum | solution.py:225
  1594.5 94.6 %all-reduce.57.cloned.1.call-start = ((), (), s32[]{:S(2)}) async-start(), calls=%async_computation.21 | async-start | bytes 466944 | tf_op jit(solution)/shard_map/psum | solution.py:225
  1646.0 94.5 %all-reduce.59.cloned.1.call-start = ((), (), s32[]{:S(2)}) async-start(), calls=%async_computation.22 | async-start | bytes 466944 | tf_op jit(solution)/shard_map/psum | solution.py:225
  1697.4 94.4 %all-reduce.61.cloned.1.call-start = ((), (), s32[]{:S(2)}) async-start(), calls=%async_computation.23 | async-start | bytes 466944 | tf_op jit(solution)/shard_map/psum | solution.py:225
  1748.8 87.3 %all-reduce.63.cloned.1.call-start = ((), (), s32[]{:S(2)}) async-start(), calls=%async_computation.24 | async-start | bytes 163840 | tf_op jit(solution)/shard_map/psum | solution.py:251
  (58 other events, 1274.4 us)
Sparse Core Ops, SparseCore 0:
  9.6 220.6 all-gather.22
  753.1 40.7 all-reduce.22
  805.3 42.8 all-reduce.24
  855.8 42.8 all-reduce.26
  907.0 42.8 all-reduce.28
  964.1 42.8 all-reduce.30
  1015.6 42.8 all-reduce.32
  1067.1 42.8 all-reduce.34
  1118.5 42.8 all-reduce.36
  1174.3 42.8 all-reduce.38
  1225.8 42.8 all-reduce.40
  1277.2 42.8 all-reduce.42
  1328.6 42.8 all-reduce.44
  1384.5 42.8 all-reduce.46
  1435.9 42.8 all-reduce.48
  1487.4 42.8 all-reduce.50
  1538.8 42.8 all-reduce.52
  1594.6 42.8 all-reduce.54
  1646.1 42.8 all-reduce.56
  1697.6 42.8 all-reduce.58
  1748.9 42.8 all-reduce.60
  1801.8 34.2 all-reduce.62
where the time goes:
time: 1900 us; the launch traced here: 1890 us
  waiting for transfers between devices  1070 us (56%)
  blocking collectives  259 us (14%)
  other arithmetic  182 us (10%)
  matrix products  178 us (9%)
  local copies, waits for them, and re-layouts  142 us (7%)
  between operations  28.2 us (1%)
  starting transfers between devices  27.2 us (1%)
    psum x20, waiting for transfers between devices, on_device(): lax.psum(jnp.dot(pre_grad, weights[slot_no].T, preferred_element_type=jnp...  856 us
    all_gather x20, blocking collectives, on_device(): joined = lax.all_gather(part_out, 'dp', axis=1, tiled=True)  172 us
    all_gather x1, waiting for transfers between devices, on_device(): weights = lax.all_gather(teacher_weight, 'mp', axis=2, tiled=True)[0]  125 us
    dot_general x20, matrix products, on_device(): jnp.dot(pre_grad, weights[slot_no].T, preferred_element_type=jnp.float32)  88.8 us
    dot_general x20, matrix products, on_device(): jnp.dot(normed_in, weights[slot_no], preferred_element_type=jnp.float32)  68 us
    convert_element_type x40, local copies, waits for them, and re-layouts, on_device(): stream = stream + joined.astype(jnp.float32)  52.5 us
    psum x1, blocking collectives, on_device(): lax.psum(jnp.sum(student_grad * student_grad), ('section', 'dp', 'mp'))  40.5 us
    dynamic_slice x38, local copies, waits for them, and re-layouts, put_rows(): lax.dynamic_slice(buffer, start_at, (1, values.shape[0], values.shape[1]))  39.8 us
  transfers between devices with their start and end apart: 33, of which 28 were waited for; matrix products, arithmetic and copies ran while one was open for 16% of the time, Pallas kernels for 0%

commit v1 on v0

v1 whole, which is shorter than its diff:
```python
import math

import jax
import jax.numpy as jnp
from jax import lax
from jax.sharding import PartitionSpec as P

D = 2432
LAT = 64


norm_eps = 1e-06
ema_decay = 0.99
step_size = 0.05


def xor_pairs(n, d, base=0):
    return [(base + i, base + (i ^ d)) for i in range(n)]


def swap(x, axis, n, d, base=0):
    return lax.ppermute(x, axis, xor_pairs(n, d, base))


def gather_in_order(x, axis, n, me, base=0):
    parts = [x] + [swap(x, axis, n, d, base) for d in range(1, n)]
    stacked = jnp.stack(parts)
    return jnp.take(stacked, me ^ jnp.arange(n, dtype=jnp.int32), axis=0)


def gelu_slope(values):
    return jax.vjp(jax.nn.gelu, values)[1](jnp.ones_like(values))[0]


def norm_back(normed, inverse, upstream):
    return inverse * (upstream - normed * jnp.mean(upstream * normed, axis=-1, keepdims=True))


def head_grads(features, w_first, w_second, loss_scale):
    feat_wide = features.astype(jnp.float32)
    inverse = lax.rsqrt(jnp.mean(feat_wide * feat_wide, axis=-1, keepdims=True) + norm_eps)
    normed = feat_wide * inverse
    hidden_pre = jnp.dot(normed.astype(jnp.bfloat16), w_first, preferred_element_type=jnp.float32)
    hidden_act = jax.nn.gelu(hidden_pre).astype(jnp.bfloat16)
    logits = jnp.dot(hidden_act, w_second, preferred_element_type=jnp.float32)
    logit_grad = -loss_scale * jax.nn.sigmoid(-logits)
    act_grad = logit_grad[:, None] * w_second.astype(jnp.float32)[None, :]
    pre_grad = (act_grad * gelu_slope(hidden_pre)).astype(jnp.bfloat16)
    normed_grad = jnp.dot(pre_grad, w_first.T, preferred_element_type=jnp.float32)
    return norm_back(normed, inverse, normed_grad).astype(jnp.bfloat16)


def on_device(
    student_hidden,
    student_weight,
    student_ema,
    noise,
    timesteps,
    patch_embed,
    teacher_weight,
    modulation,
    layer_counts,
    feature_layers,
    head_routes,
    head_owner,
    head_in,
    head_out,
):
    row_count, width = student_hidden.shape
    n_sec = lax.axis_size("section")
    n_mp = lax.axis_size("mp")
    n_dp = lax.axis_size("dp")
    sec = lax.axis_index("section")
    me_dp = lax.axis_index("dp")
    me_mp = lax.axis_index("mp")
    slot_count = teacher_weight.shape[1]
    levels = modulation.shape[2]
    col_width = width // n_dp
    samples = timesteps.shape[0]
    per_sample = row_count // samples

    t_rows = jnp.repeat(timesteps, per_sample)
    noise_level = ((t_rows + 1).astype(jnp.float32) / (levels + 1))[:, None]

    w_cols = gather_in_order(student_weight.astype(jnp.bfloat16), "dp", n_dp, me_dp)
    w_cols = jnp.concatenate(list(w_cols), axis=1)
    row_axes = ("section", "mp")
    row_me = sec * n_mp + me_mp
    w_rows = gather_in_order(w_cols, row_axes, n_sec * n_mp, row_me)
    student_full = w_rows.reshape(width, -1)
    latents = (
        jnp.dot(student_hidden, student_full, preferred_element_type=jnp.float32) * width ** (-0.5)
    ).astype(jnp.bfloat16)
    noisy_input = (
        (1.0 - noise_level) * latents.astype(jnp.float32) + noise_level * noise.astype(jnp.float32)
    ).astype(jnp.bfloat16)
    start_stream = jnp.dot(noisy_input, patch_embed, preferred_element_type=jnp.float32)

    weights = lax.all_gather(teacher_weight[0], "mp", axis=1, tiled=True)

    mod_pick = jnp.take(modulation[0], timesteps, axis=1).astype(jnp.float32)
    mod_rows = jnp.repeat(mod_pick, per_sample, axis=1)
    scale_rows = mod_rows[:, :, 0, :]
    gate_cols = lax.dynamic_slice_in_dim(mod_rows[:, :, 1, :], me_dp * col_width, col_width, 2)
    active = (jnp.arange(slot_count, dtype=jnp.int32) < layer_counts[0]).astype(jnp.float32)

    saved = []
    taps = []
    stream = start_stream
    for tick in range(n_sec):
        tick_saved = []
        tap = jnp.zeros((row_count, width), jnp.bfloat16)
        for slot_no in range(slot_count):
            inverse = lax.rsqrt(jnp.mean(stream * stream, axis=-1, keepdims=True) + norm_eps)
            normed = stream * inverse
            normed_in = (normed * (1.0 + scale_rows[slot_no])).astype(jnp.bfloat16)
            pre_act = jnp.dot(normed_in, weights[slot_no], preferred_element_type=jnp.float32)
            tick_saved.append((normed, inverse, pre_act))
            part_out = (active[slot_no] * gate_cols[slot_no] * jax.nn.gelu(pre_act)).astype(
                jnp.bfloat16
            )
            joined = gather_in_order(
                part_out, ("section", "dp"), n_dp, me_dp, base=tick * n_dp
            )
            joined = jnp.concatenate(list(joined), axis=1)
            stream = stream + joined.astype(jnp.float32)
            hit = feature_layers[tick] == tick * slot_count + slot_no
            tap = jnp.where(hit, stream.astype(jnp.bfloat16), tap)
        saved.append(tick_saved)
        taps.append(tap)
        if tick + 1 < n_sec:
            sent = lax.ppermute(stream.astype(jnp.bfloat16), "section", [(tick, tick + 1)])
            stream = sent.astype(jnp.float32)

    tap_store = taps[0]
    for tick in range(1, n_sec):
        tap_store = jnp.where(sec == tick, taps[tick], tap_store)
    capacity = 5 * row_count // (4 * n_mp)
    owner_range = jnp.arange(n_mp, dtype=jnp.int32)
    routes = lax.dynamic_index_in_dim(head_routes[:, :, 0], sec, 0, keepdims=False)
    owners_map = lax.dynamic_index_in_dim(head_owner, sec, 0, keepdims=False)
    route_hot = (routes[:, None] == owner_range[None, :]).astype(jnp.int32)
    owner_ids = jnp.sum(route_hot * owners_map[None, :], axis=1)
    owner_hot = (owner_ids[:, None] == owner_range[None, :]).astype(jnp.int32)
    position = jnp.sum(owner_hot * (jnp.cumsum(owner_hot, axis=0) - 1), axis=1)
    target = owner_ids * capacity + position
    dispatch = (
        target[:, None] == jnp.arange(n_mp * capacity, dtype=jnp.int32)[None, :]
    ).astype(jnp.bfloat16)
    send_feat = (
        jnp.dot(dispatch.T, tap_store, preferred_element_type=jnp.float32)
        .astype(jnp.bfloat16)
        .reshape(n_mp, capacity, width)
    )
    items = [lax.dynamic_index_in_dim(send_feat, me_mp, 0, keepdims=False)]
    for d in range(1, n_mp):
        outgoing = lax.dynamic_index_in_dim(send_feat, me_mp ^ d, 0, keepdims=False)
        items.append(swap(outgoing, "mp", n_mp, d))
    loss_scale = width / math.sqrt(row_count * n_mp)
    w_first = lax.dynamic_index_in_dim(head_in[:, 0], sec, 0, keepdims=False)
    w_second = lax.dynamic_index_in_dim(head_out[:, 0], sec, 0, keepdims=False)
    head_result = head_grads(
        jnp.concatenate(items, axis=0), w_first, w_second, loss_scale
    ).reshape(n_mp, capacity, width)
    head_cols = lax.dynamic_slice_in_dim(head_result, me_dp * col_width, col_width, 2)
    back = [head_cols[0]] + [swap(head_cols[d], "mp", n_mp, d) for d in range(1, n_mp)]
    by_owner = jnp.take(jnp.stack(back), me_mp ^ owner_range, axis=0)
    tap_grads = jnp.dot(
        dispatch, by_owner.reshape(n_mp * capacity, col_width), preferred_element_type=jnp.float32
    )

    my_cols = lambda x: lax.dynamic_slice_in_dim(x, me_dp * col_width, col_width, x.ndim - 1)
    grad_stream = jnp.zeros((row_count, col_width), jnp.float32)
    for tick in range(n_sec):
        live = n_sec - 1 - tick
        tick_saved = saved[live]
        for slot_no in reversed(range(slot_count)):
            hit = feature_layers[live] == live * slot_count + slot_no
            grad_stream = grad_stream + jnp.where(hit, tap_grads, 0.0)
            normed, inverse, pre_act = tick_saved[slot_no]
            pre_grad = (
                grad_stream * active[slot_no] * gate_cols[slot_no] * gelu_slope(pre_act)
            ).astype(jnp.bfloat16)
            partial = jnp.dot(
                pre_grad, weights[slot_no].T, preferred_element_type=jnp.float32
            ).astype(jnp.bfloat16)
            partial = lax.optimization_barrier(partial)
            scaled = 1.0 + scale_rows[slot_no]
            row_term = jnp.sum(partial.astype(jnp.float32) * scaled * normed, axis=-1)
            pieces = [my_cols(partial)]
            terms = [row_term[None, :]]
            for d in range(1, n_dp):
                block = lax.dynamic_slice_in_dim(partial, (me_dp ^ d) * col_width, col_width, 1)
                pairs = xor_pairs(n_dp, d, live * n_dp)
                pieces.append(lax.ppermute(block, ("section", "dp"), pairs))
                terms.append(lax.ppermute(row_term[None, :], ("section", "dp"), pairs))
            order = me_dp ^ jnp.arange(n_dp, dtype=jnp.int32)
            ordered = jnp.take(jnp.stack(pieces), order, axis=0).astype(jnp.float32)
            term_rows = jnp.take(jnp.concatenate(terms, axis=0), order, axis=0)
            input_grad = jnp.zeros((row_count, col_width), jnp.float32)
            row_sum = jnp.zeros((row_count,), jnp.float32)
            for src in range(n_dp):
                input_grad = input_grad + ordered[src]
                row_sum = row_sum + term_rows[src]
            row_mean = (row_sum / width)[:, None]
            grad_stream = grad_stream + inverse * (
                input_grad * my_cols(scaled) - my_cols(normed) * row_mean
            )
        if tick + 1 < n_sec:
            sent = lax.ppermute(
                grad_stream.astype(jnp.bfloat16), "section", [(live, live - 1)]
            )
            grad_stream = sent.astype(jnp.float32)

    lat_part = student_weight.shape[1]
    latent_pre = jnp.dot(
        grad_stream.astype(jnp.bfloat16), my_cols(patch_embed).T, preferred_element_type=jnp.float32
    )
    got = [lax.dynamic_slice_in_dim(latent_pre, me_dp * lat_part, lat_part, 1)]
    for d in range(1, n_dp):
        block = lax.dynamic_slice_in_dim(latent_pre, (me_dp ^ d) * lat_part, lat_part, 1)
        got.append(lax.ppermute(block, ("section", "dp"), xor_pairs(n_dp, d, 0)))
    got = jnp.take(jnp.stack(got), me_dp ^ jnp.arange(n_dp, dtype=jnp.int32), axis=0)
    lat_sum = got[0]
    for src in range(1, n_dp):
        lat_sum = lat_sum + got[src]
    my_latent = ((1.0 - noise_level) * lat_sum).astype(jnp.bfloat16)
    if n_sec > 1:
        spread = lax.ppermute(my_latent, "section", [(0, s) for s in range(1, n_sec)])
        my_latent = jnp.where(sec == 0, my_latent, spread)

    own_rows = student_weight.shape[0]
    segment_block = width // n_sec
    hidden_cols = lax.dynamic_slice_in_dim(student_hidden, sec * segment_block, segment_block, 1)
    part_grad = lax.dot_general(
        hidden_cols, my_latent, (((0,), (0,)), ((), ())), preferred_element_type=jnp.float32
    ).reshape(n_mp, own_rows, lat_part)
    got = [lax.dynamic_index_in_dim(part_grad, me_mp, 0, keepdims=False)]
    for d in range(1, n_mp):
        outgoing = lax.dynamic_index_in_dim(part_grad, me_mp ^ d, 0, keepdims=False)
        got.append(swap(outgoing, "mp", n_mp, d))
    got = jnp.take(jnp.stack(got), me_mp ^ jnp.arange(n_mp, dtype=jnp.int32), axis=0)
    grad_sum = got[0]
    for src in range(1, n_mp):
        grad_sum = grad_sum + got[src]
    student_grad = grad_sum * width ** (-0.5)

    local_sq = jnp.sum(student_grad * student_grad).reshape(1)
    sq = gather_in_order(local_sq, "section", n_sec, sec).reshape(-1)
    sq = gather_in_order(sq, "dp", n_dp, me_dp).reshape(-1)
    sq = gather_in_order(sq, "mp", n_mp, me_mp).reshape(-1)
    total_sq = jnp.sum(sq)
    mean_square = total_sq / (width * LAT)
    student_update = student_grad * lax.rsqrt(mean_square + norm_eps)
    ema_new = ema_decay * student_ema + (1.0 - ema_decay) * (
        student_weight - step_size * student_update
    )
    return (student_update, ema_new)


def solution(mesh):
    in_specs = (
        P("mp", None),
        P(("section", "mp"), "dp"),
        P(("section", "mp"), "dp"),
        P("mp", None),
        P("mp"),
        P(),
        P("section", None, "mp", "dp"),
        P("section", None, None, None, None),
        P("section"),
        P(),
        P(None, "mp", None),
        P(),
        P(None, "mp", None, None),
        P(None, "mp", None),
    )
    out_specs = (P(("section", "mp"), "dp"), P(("section", "mp"), "dp"))
    return jax.shard_map(
        on_device, mesh=mesh, in_specs=in_specs, out_specs=out_specs, check_vma=False
    )
```

time: 1900 us -> 893 us (0.47)
  waiting for transfers between devices: 1070 us -> 354 us
  blocking collectives: 259 us -> 0 us
  starting transfers between devices: 27.2 us -> 196 us
  matrix products: 178 us -> 92.5 us
  other arithmetic: 182 us -> 110 us
  local copies, waits for them, and re-layouts: 142 us -> 106 us
    psum x21 -> x0, waiting for transfers between devices: 890 us -> none  [the longest x20 856 us: on_device(): lax.psum(jnp.dot(pre_grad, weights[slot_no].T, preferred_element_type=jnp...]
    all_gather x22 -> x0, blocking collectives: 215 us -> none  [the longest x20 172 us: on_device(): joined = lax.all_gather(part_out, 'dp', axis=1, tiled=True)]
    ppermute x8 -> x104, starting transfers between devices: 11 us -> 196 us  [the longest x50 86 us: swap(): return lax.ppermute(x, axis, xor_pairs(n, d, base))]
    ppermute x8 -> x104, waiting for transfers between devices: 8.71 us -> 171 us  [the longest x1 95 us: on_device(): lax.ppermute(grad_stream.astype(jnp.bfloat16), 'section', [(live, live -...]
    dynamic_update_slice x45 -> x0, other arithmetic: 68.9 us -> none  [the longest x20 38.2 us: put_rows(): return lax.dynamic_update_slice(buffer, merged[None], start_at)]
    convert_element_type x44 -> x1, local copies, waits for them, and re-layouts: 58.1 us -> 0.08 us  [on_device(): mod_pick = jnp.take(modulation[0], timesteps, axis=1).astype(jnp.float32)]
    all_gather x1, waiting for transfers between devices: 125 us -> 182 us  [on_device(): weights = lax.all_gather(teacher_weight[0], 'mp', axis=1, tiled=True)]
    dot_general x20 -> x8, matrix products: 88.8 us -> 33.7 us  [on_device(): jnp.dot(pre_grad, weights[slot_no].T, preferred_element_type=jnp.float32)]
  transfers between devices with their start and end apart: 33 -> 105, of which waited for: 28 -> 34; matrix products, arithmetic and copies ran while one was open for 16% -> 4% of each run, Pallas kernels for 0% -> 0%
where the time goes in v1:
time: 893 us; the launch traced here: 881 us
  waiting for transfers between devices  354 us (40%)
  starting transfers between devices  196 us (22%)
  other arithmetic  110 us (12%)
  local copies, waits for them, and re-layouts  106 us (12%)
  matrix products  92.5 us (10%)
  between operations  22.8 us (3%)
    all_gather x1, waiting for transfers between devices, on_device(): weights = lax.all_gather(teacher_weight[0], 'mp', axis=1, tiled=True)  182 us
    ppermute x1, waiting for transfers between devices, on_device(): lax.ppermute(grad_stream.astype(jnp.bfloat16), 'section', [(live, live -...  95 us
    ppermute x50, starting transfers between devices, swap(): return lax.ppermute(x, axis, xor_pairs(n, d, base))  86 us
    ppermute x24, starting transfers between devices, on_device(): pieces.append(lax.ppermute(block, ('section', 'dp'), pairs))  51.4 us
    ppermute x50, waiting for transfers between devices, swap(): return lax.ppermute(x, axis, xor_pairs(n, d, base))  51.1 us
    ppermute x24, starting transfers between devices, on_device(): terms.append(lax.ppermute(row_term[None, :], ('section', 'dp'), pairs))  44.7 us
    dot_general x8, matrix products, on_device(): jnp.dot(normed_in, weights[slot_no], preferred_element_type=jnp.float32)  40.5 us
    dot_general x8, matrix products, on_device(): jnp.dot(pre_grad, weights[slot_no].T, preferred_element_type=jnp.float32)  33.7 us
  transfers between devices with their start and end apart: 105, of which 34 were waited for; matrix products, arithmetic and copies ran while one was open for 4% of the time, Pallas kernels for 0%

profile of v1, /device:TPU:0, one launch (start us, length us, event | category | flops | bytes accessed | tf_op | source)
XLA Modules:
  0.0 880.8 jit_solution(4976252293237050197)
XLA Ops:
  17.7 7.1 copy-done.2
  55.2 181.6 %all-gather.3.cloned.1.call-done = bf16[1,4,2432,608]{3,2,1,0:T(8,128)(2,1)} async-done(((bf16[1,4,608,608]{3,2,1,0:T(8,128)(2,1)}), bf16[1,4,2432,608]{3,2,1,0:T(8,128)(2,1)}) %all-gather.3.cloned.1.call-update) | async-done | bytes 11829264 | tf_op jit(solution)/shard_map/all_gather | solution.py:99
  236.8 5.4 multiply_convert_fusion.7
  253.6 4.3 collective-permute-done.12
  268.7 5.1 multiply_convert_fusion.6
  278.7 4.3 collective-permute-start.15
  301.6 5.0 multiply_convert_fusion.5
  318.0 4.2 collective-permute-done.18
  332.9 5.0 multiply_convert_fusion.4
  342.8 4.3 collective-permute-start.21
  367.5 4.9 multiply_convert_fusion.3
  385.4 5.0 multiply_convert_fusion.2
  408.8 5.0 multiply_convert_fusion.1
  428.1 5.1 multiply_convert_fusion
  453.1 7.5 convolution_convert_fusion
  469.5 6.3 slice_add_fusion.3
  475.9 4.0 collective-permute-done.36
  488.0 4.0 collective-permute-start.38
  494.4 4.2 collective-permute-done.39
  499.7 4.4 convolution_convert_fusion.8
  522.7 4.2 convolution_convert_fusion.7
  545.6 4.2 convolution_convert_fusion.6
  568.3 4.1 convolution_convert_fusion.5
  586.2 95.0 %collective-permute-done.65 = bf16[192,608]{1,0:T(8,128)(2,1)S(1)} collective-permute-done((bf16[192,608]{1,0:T(8,128)(2,1)S(1)}, bf16[192,608]{1,0:T(8,128)(2,1)S(1)}, u32[]{:S(2)}, u32[]{:S(2)}) %collective-permute-start.65) | collective-permute-done | bytes 233504 | tf_op jit(solution)/shard_map/ppermute | solution.py:210
  681.3 4.2 convolution_convert_fusion.4
  718.7 4.2 convolution_convert_fusion.3
  746.0 4.0 collective-permute-done.74
  753.7 4.2 convolution_convert_fusion.2
  775.7 4.0 collective-permute-start.80
  791.1 4.2 convolution_convert_fusion.1
  818.3 4.0 collective-permute-done.86
  831.4 3.9 collective-permute-start.92
  (595 shorter events, 441.2 us)
Async XLA Ops:
  7.2 229.6 %all-gather.3.cloned.1.call-start = ((), (), s32[]{:S(2)}) async-start(), calls=%async_computation | async-start | bytes 15564800 | tf_op jit(solution)/shard_map/all_gather | solution.py:99
  8.1 20.5 %collective-permute-start = (bf16[304,16]{0,1:T(8,128)(2,1)S(1)}, bf16[304,16]{0,1:T(8,128)(2,1)S(1)}, u32[]{:S(2)}, u32[]{:S(2)}) collective-permute-start(bf16[304,16]{0,1:T(8,128)(2,1)S(1)} %convert_element_type.273), channel_id=1, source_target_pairs={{0,4},{4,0},{8,12},{12,8},{1,5},{5,1},{9,13},{13,9},{2,6},{6,2},{1... | collective-permute-start | bytes 29192 | tf_op jit(solution)/shard_map/ppermute | solution.py:22
  11.0 17.5 %collective-permute-start.1 = (bf16[304,16]{0,1:T(8,128)(2,1)S(1)}, bf16[304,16]{0,1:T(8,128)(2,1)S(1)}, u32[]{:S(2)}, u32[]{:S(2)}) collective-permute-start(bf16[304,16]{0,1:T(8,128)(2,1)S(1)} %convert_element_type.273), channel_id=1, source_target_pairs={{0,8},{4,12},{8,0},{12,4},{1,9},{5,13},{9,1},{13,5},{2,10},{6,14},... | collective-permute-start | bytes 29192 | tf_op jit(solution)/shard_map/ppermute | solution.py:22
  12.5 16.0 %collective-permute-start.2 = (bf16[304,16]{0,1:T(8,128)(2,1)S(1)}, bf16[304,16]{0,1:T(8,128)(2,1)S(1)}, u32[]{:S(2)}, u32[]{:S(2)}) collective-permute-start(bf16[304,16]{0,1:T(8,128)(2,1)S(1)} %convert_element_type.273), channel_id=1, source_target_pairs={{0,12},{4,8},{8,4},{12,0},{1,13},{5,9},{9,5},{13,1},{2,14},{6,10},... | collective-permute-start | bytes 29192 | tf_op jit(solution)/shard_map/ppermute | solution.py:22
  35.1 9.8 %collective-permute-start.8 = (bf16[304,64]{0,1:T(8,128)(2,1)S(1)}, bf16[304,64]{0,1:T(8,128)(2,1)S(1)}, u32[]{:S(2)}, u32[]{:S(2)}) collective-permute-start(bf16[304,64]{0,1:T(8,128)(2,1)S(1)} %pad_maximum_fusion.21), channel_id=1, source_target_pairs={{0,18},{1,19},{2,16},{3,17},{16,2},{17,3},{18,0},{19,1},{4,22},{5,... | collective-permute-start | bytes 116744 | tf_op jit(solution)/shard_map/ppermute | solution.py:22
  242.2 9.3 %collective-permute-start.10 = (bf16[192,608]{1,0:T(8,128)(2,1)S(1)}, bf16[192,608]{1,0:T(8,128)(2,1)S(1)}, u32[]{:S(2)}, u32[]{:S(2)}) collective-permute-start(bf16[192,608]{1,0:T(8,128)(2,1)S(1)} %get-tuple-element.108), channel_id=1, source_target_pairs={{0,4},{4,0},{8,12},{12,8},{1,5},{5,1},{9,13},{13,9},{2,6},{6,2},{1... | collective-permute-start | bytes 700424 | tf_op jit(solution)/shard_map/ppermute | solution.py:22
  273.7 9.2 %collective-permute-start.13 = (bf16[192,608]{1,0:T(8,128)(2,1)}, bf16[192,608]{1,0:T(8,128)(2,1)}, u32[]{:S(2)}, u32[]{:S(2)}) collective-permute-start(bf16[192,608]{1,0:T(8,128)(2,1)} %get-tuple-element.110), channel_id=1, source_target_pairs={{0,4},{4,0},{8,12},{12,8},{1,5},{5,1},{9,13},{13,9},{2,6},{6,2},{1... | collective-permute-start | bytes 700424 | tf_op jit(solution)/shard_map/ppermute | solution.py:22
  278.7 9.3 %collective-permute-start.15 = (bf16[192,608]{1,0:T(8,128)(2,1)}, bf16[192,608]{1,0:T(8,128)(2,1)}, u32[]{:S(2)}, u32[]{:S(2)}) collective-permute-start(bf16[192,608]{1,0:T(8,128)(2,1)} %get-tuple-element.110), channel_id=1, source_target_pairs={{0,12},{4,8},{8,4},{12,0},{1,13},{5,9},{9,5},{13,1},{2,14},{6,10},... | collective-permute-start | bytes 700424 | tf_op jit(solution)/shard_map/ppermute | solution.py:22
  306.5 9.7 %collective-permute-start.16 = (bf16[192,608]{1,0:T(8,128)(2,1)S(1)}, bf16[192,608]{1,0:T(8,128)(2,1)S(1)}, u32[]{:S(2)}, u32[]{:S(2)}) collective-permute-start(bf16[192,608]{1,0:T(8,128)(2,1)S(1)} %get-tuple-element.112), channel_id=1, source_target_pairs={{0,4},{4,0},{8,12},{12,8},{1,5},{5,1},{9,13},{13,9},{2,6},{6,2},{1... | collective-permute-start | bytes 700424 | tf_op jit(solution)/shard_map/ppermute | solution.py:22
  337.9 9.2 %collective-permute-start.19 = (bf16[192,608]{1,0:T(8,128)(2,1)S(1)}, bf16[192,608]{1,0:T(8,128)(2,1)S(1)}, u32[]{:S(2)}, u32[]{:S(2)}) collective-permute-start(bf16[192,608]{1,0:T(8,128)(2,1)S(1)} %get-tuple-element.114), channel_id=1, source_target_pairs={{0,4},{4,0},{8,12},{12,8},{1,5},{5,1},{9,13},{13,9},{2,6},{6,2},{1... | collective-permute-start | bytes 700424 | tf_op jit(solution)/shard_map/ppermute | solution.py:22
  433.2 9.7 %collective-permute-start.32 = (bf16[192,608]{1,0:T(8,128)(2,1)}, bf16[192,608]{1,0:T(8,128)(2,1)}, u32[]{:S(2)}, u32[]{:S(2)}) collective-permute-start(bf16[192,608]{1,0:T(8,128)(2,1)} %get-tuple-element.122), channel_id=1, source_target_pairs={{16,20},{20,16},{24,28},{28,24},{17,21},{21,17},{25,29},{29,25},{1... | collective-permute-start | bytes 700424 | tf_op jit(solution)/shard_map/ppermute | solution.py:22
  465.1 10.9 %collective-permute-start.35 = (bf16[60,2432]{1,0:T(8,128)(2,1)}, bf16[60,2432]{1,0:T(8,128)(2,1)}, u32[]{:S(2)}, u32[]{:S(2)}) collective-permute-start(bf16[60,2432]{1,0:T(8,128)(2,1)} %get-tuple-element.21), channel_id=1, source_target_pairs={{0,1},{1,0},{2,3},{3,2},{4,5},{5,4},{6,7},{7,6},{8,9},{9,8},{10,11... | collective-permute-start | bytes 875528 | tf_op jit(solution)/shard_map/ppermute | solution.py:22
  465.1 14.8 %collective-permute-start.36 = (bf16[60,2432]{1,0:T(8,128)(2,1)}, bf16[60,2432]{1,0:T(8,128)(2,1)}, u32[]{:S(2)}, u32[]{:S(2)}) collective-permute-start(bf16[60,2432]{1,0:T(8,128)(2,1)} %get-tuple-element.20), channel_id=1, source_target_pairs={{0,2},{1,3},{2,0},{3,1},{4,6},{5,7},{6,4},{7,5},{8,10},{9,11},{10,... | collective-permute-start | bytes 875528 | tf_op jit(solution)/shard_map/ppermute | solution.py:22
  465.9 14.1 %collective-permute-start.37 = (bf16[60,2432]{1,0:T(8,128)(2,1)}, bf16[60,2432]{1,0:T(8,128)(2,1)}, u32[]{:S(2)}, u32[]{:S(2)}) collective-permute-start(bf16[60,2432]{1,0:T(8,128)(2,1)} %get-tuple-element.19), channel_id=1, source_target_pairs={{0,3},{1,2},{2,1},{3,0},{4,7},{5,6},{6,5},{7,4},{8,11},{9,10},{10,... | collective-permute-start | bytes 875528 | tf_op jit(solution)/shard_map/ppermute | solution.py:22
  584.5 96.8 %collective-permute-start.65 = (bf16[192,608]{1,0:T(8,128)(2,1)S(1)}, bf16[192,608]{1,0:T(8,128)(2,1)S(1)}, u32[]{:S(2)}, u32[]{:S(2)}) collective-permute-start(bf16[192,608]{1,0:T(8,128)(2,1)S(1)} %fusion.184), channel_id=1, source_target_pairs={{16,0},{17,1},{18,2},{19,3},{20,4},{21,5},{22,6},{23,7},{24,8},{25... | collective-permute-start | bytes 700424 | tf_op jit(solution)/shard_map/ppermute | solution.py:210
  687.5 15.9 %collective-permute-start.69 = (f32[1,192]{1,0:T(1,128)S(1)}, f32[1,192]{1,0:T(1,128)S(1)}, u32[]{:S(2)}, u32[]{:S(2)}) collective-permute-start(f32[1,192]{1,0:T(1,128)S(1)} %bitcast.684), channel_id=1, source_target_pairs={{0,4},{4,0},{8,12},{12,8},{1,5},{5,1},{9,13},{13,9},{2,6},{6,2},{1... | collective-permute-start | bytes 2312 | tf_op jit(solution)/shard_map/ppermute | solution.py:196
  690.2 17.0 %collective-permute-start.70 = (f32[1,192]{1,0:T(1,128)S(1)}, f32[1,192]{1,0:T(1,128)S(1)}, u32[]{:S(2)}, u32[]{:S(2)}) collective-permute-start(f32[1,192]{1,0:T(1,128)S(1)} %bitcast.685), channel_id=1, source_target_pairs={{0,8},{4,12},{8,0},{12,4},{1,9},{5,13},{9,1},{13,5},{2,10},{6,14},... | collective-permute-start | bytes 2312 | tf_op jit(solution)/shard_map/ppermute | solution.py:196
  692.9 14.4 %collective-permute-start.71 = (f32[1,192]{1,0:T(1,128)S(1)}, f32[1,192]{1,0:T(1,128)S(1)}, u32[]{:S(2)}, u32[]{:S(2)}) collective-permute-start(f32[1,192]{1,0:T(1,128)S(1)} %bitcast.686), channel_id=1, source_target_pairs={{0,12},{4,8},{8,4},{12,0},{1,13},{5,9},{9,5},{13,1},{2,14},{6,10},... | collective-permute-start | bytes 2312 | tf_op jit(solution)/shard_map/ppermute | solution.py:196
  698.0 9.9 %collective-permute-start.66 = (bf16[192,608]{1,0:T(8,128)(2,1)}, bf16[192,608]{1,0:T(8,128)(2,1)S(1)}, u32[]{:S(2)}, u32[]{:S(2)}) collective-permute-start(bf16[192,608]{1,0:T(8,128)(2,1)} %get-tuple-element.71), channel_id=1, source_target_pairs={{0,4},{4,0},{8,12},{12,8},{1,5},{5,1},{9,13},{13,9},{2,6},{6,2},{1... | collective-permute-start | bytes 700424 | tf_op jit(solution)/shard_map/ppermute | solution.py:195
  725.0 16.0 %collective-permute-start.75 = (f32[1,192]{1,0:T(1,128)S(1)}, f32[1,192]{1,0:T(1,128)S(1)}, u32[]{:S(2)}, u32[]{:S(2)}) collective-permute-start(f32[1,192]{1,0:T(1,128)S(1)} %bitcast.698), channel_id=1, source_target_pairs={{0,4},{4,0},{8,12},{12,8},{1,5},{5,1},{9,13},{13,9},{2,6},{6,2},{1... | collective-permute-start | bytes 2312 | tf_op jit(solution)/shard_map/ppermute | solution.py:196
  728.1 15.8 %collective-permute-start.76 = (f32[1,192]{1,0:T(1,128)S(1)}, f32[1,192]{1,0:T(1,128)S(1)}, u32[]{:S(2)}, u32[]{:S(2)}) collective-permute-start(f32[1,192]{1,0:T(1,128)S(1)} %bitcast.699), channel_id=1, source_target_pairs={{0,8},{4,12},{8,0},{12,4},{1,9},{5,13},{9,1},{13,5},{2,10},{6,14},... | collective-permute-start | bytes 2312 | tf_op jit(solution)/shard_map/ppermute | solution.py:196
  731.3 12.7 %collective-permute-start.77 = (f32[1,192]{1,0:T(1,128)S(1)}, f32[1,192]{1,0:T(1,128)S(1)}, u32[]{:S(2)}, u32[]{:S(2)}) collective-permute-start(f32[1,192]{1,0:T(1,128)S(1)} %bitcast.700), channel_id=1, source_target_pairs={{0,12},{4,8},{8,4},{12,0},{1,13},{5,9},{9,5},{13,1},{2,14},{6,10},... | collective-permute-start | bytes 2312 | tf_op jit(solution)/shard_map/ppermute | solution.py:196
  734.7 9.9 %collective-permute-start.72 = (bf16[192,608]{1,0:T(8,128)(2,1)S(1)}, bf16[192,608]{1,0:T(8,128)(2,1)S(1)}, u32[]{:S(2)}, u32[]{:S(2)}) collective-permute-start(bf16[192,608]{1,0:T(8,128)(2,1)S(1)} %get-tuple-element.67), channel_id=1, source_target_pairs={{0,4},{4,0},{8,12},{12,8},{1,5},{5,1},{9,13},{13,9},{2,6},{6,2},{1... | collective-permute-start | bytes 700424 | tf_op jit(solution)/shard_map/ppermute | solution.py:195
  759.9 15.8 %collective-permute-start.81 = (f32[1,192]{1,0:T(1,128)S(1)}, f32[1,192]{1,0:T(1,128)S(1)}, u32[]{:S(2)}, u32[]{:S(2)}) collective-permute-start(f32[1,192]{1,0:T(1,128)S(1)} %bitcast.688), channel_id=1, source_target_pairs={{0,4},{4,0},{8,12},{12,8},{1,5},{5,1},{9,13},{13,9},{2,6},{6,2},{1... | collective-permute-start | bytes 2312 | tf_op jit(solution)/shard_map/ppermute | solution.py:196
  762.7 17.1 %collective-permute-start.82 = (f32[1,192]{1,0:T(1,128)S(1)}, f32[1,192]{1,0:T(1,128)S(1)}, u32[]{:S(2)}, u32[]{:S(2)}) collective-permute-start(f32[1,192]{1,0:T(1,128)S(1)} %bitcast.689), channel_id=1, source_target_pairs={{0,8},{4,12},{8,0},{12,4},{1,9},{5,13},{9,1},{13,5},{2,10},{6,14},... | collective-permute-start | bytes 2312 | tf_op jit(solution)/shard_map/ppermute | solution.py:196
  765.2 14.6 %collective-permute-start.83 = (f32[1,192]{1,0:T(1,128)S(1)}, f32[1,192]{1,0:T(1,128)S(1)}, u32[]{:S(2)}, u32[]{:S(2)}) collective-permute-start(f32[1,192]{1,0:T(1,128)S(1)} %bitcast.690), channel_id=1, source_target_pairs={{0,12},{4,8},{8,4},{12,0},{1,13},{5,9},{9,5},{13,1},{2,14},{6,10},... | collective-permute-start | bytes 2312 | tf_op jit(solution)/shard_map/ppermute | solution.py:196
  770.4 10.1 %collective-permute-start.78 = (bf16[192,608]{1,0:T(8,128)(2,1)}, bf16[192,608]{1,0:T(8,128)(2,1)S(1)}, u32[]{:S(2)}, u32[]{:S(2)}) collective-permute-start(bf16[192,608]{1,0:T(8,128)(2,1)} %get-tuple-element.63), channel_id=1, source_target_pairs={{0,4},{4,0},{8,12},{12,8},{1,5},{5,1},{9,13},{13,9},{2,6},{6,2},{1... | collective-permute-start | bytes 700424 | tf_op jit(solution)/shard_map/ppermute | solution.py:195
  797.3 16.0 %collective-permute-start.87 = (f32[1,192]{1,0:T(1,128)S(1)}, f32[1,192]{1,0:T(1,128)S(1)}, u32[]{:S(2)}, u32[]{:S(2)}) collective-permute-start(f32[1,192]{1,0:T(1,128)S(1)} %bitcast.694), channel_id=1, source_target_pairs={{0,4},{4,0},{8,12},{12,8},{1,5},{5,1},{9,13},{13,9},{2,6},{6,2},{1... | collective-permute-start | bytes 2312 | tf_op jit(solution)/shard_map/ppermute | solution.py:196
  800.5 15.8 %collective-permute-start.88 = (f32[1,192]{1,0:T(1,128)S(1)}, f32[1,192]{1,0:T(1,128)S(1)}, u32[]{:S(2)}, u32[]{:S(2)}) collective-permute-start(f32[1,192]{1,0:T(1,128)S(1)} %bitcast.695), channel_id=1, source_target_pairs={{0,8},{4,12},{8,0},{12,4},{1,9},{5,13},{9,1},{13,5},{2,10},{6,14},... | collective-permute-start | bytes 2312 | tf_op jit(solution)/shard_map/ppermute | solution.py:196
  803.6 12.7 %collective-permute-start.89 = (f32[1,192]{1,0:T(1,128)S(1)}, f32[1,192]{1,0:T(1,128)S(1)}, u32[]{:S(2)}, u32[]{:S(2)}) collective-permute-start(f32[1,192]{1,0:T(1,128)S(1)} %bitcast.696), channel_id=1, source_target_pairs={{0,12},{4,8},{8,4},{12,0},{1,13},{5,9},{9,5},{13,1},{2,14},{6,10},... | collective-permute-start | bytes 2312 | tf_op jit(solution)/shard_map/ppermute | solution.py:196
  807.0 9.9 %collective-permute-start.84 = (bf16[192,608]{1,0:T(8,128)(2,1)S(1)}, bf16[192,608]{1,0:T(8,128)(2,1)S(1)}, u32[]{:S(2)}, u32[]{:S(2)}) collective-permute-start(bf16[192,608]{1,0:T(8,128)(2,1)S(1)} %get-tuple-element.59), channel_id=1, source_target_pairs={{0,4},{4,0},{8,12},{12,8},{1,5},{5,1},{9,13},{13,9},{2,6},{6,2},{1... | collective-permute-start | bytes 700424 | tf_op jit(solution)/shard_map/ppermute | solution.py:195
  826.1 9.2 %collective-permute-start.90 = (f32[192,16]{0,1:T(8,128)S(1)}, f32[192,16]{0,1:T(8,128)S(1)}, u32[]{:S(2)}, u32[]{:S(2)}) collective-permute-start(f32[192,16]{0,1:T(8,128)S(1)} %get-tuple-element.95), channel_id=1, source_target_pairs={{0,4},{4,0},{8,12},{12,8},{1,5},{5,1},{9,13},{13,9},{2,6},{6,2},{1... | collective-permute-start | bytes 36872 | tf_op jit(solution)/shard_map/ppermute | solution.py:222
  (144 other events, 1396.7 us)
Sparse Core Ops, SparseCore 0:
  9.6 227.1 all-gather.2

commit v2 on v1

--- a/solution.py
+++ b/solution.py
@@ -26,6 +26,13 @@
     parts = [x] + [swap(x, axis, n, d, base) for d in range(1, n)]
     stacked = jnp.stack(parts)
     return jnp.take(stacked, me ^ jnp.arange(n, dtype=jnp.int32), axis=0)
+
+
+def relative_blocks(x, axis, n, me):
+    width = x.shape[axis] // n
+    return jnp.concatenate(
+        [lax.dynamic_slice_in_dim(x, (me ^ d) * width, width, axis) for d in range(n)], axis=axis
+    )
 
 
 def gelu_slope(values):
@@ -94,13 +101,19 @@
     noisy_input = (
         (1.0 - noise_level) * latents.astype(jnp.float32) + noise_level * noise.astype(jnp.float32)
     ).astype(jnp.bfloat16)
-    start_stream = jnp.dot(noisy_input, patch_embed, preferred_element_type=jnp.float32)
-
-    weights = lax.all_gather(teacher_weight[0], "mp", axis=1, tiled=True)
+    embed_rel = relative_blocks(patch_embed, 1, n_dp, me_dp)
+    start_stream = jnp.dot(noisy_input, embed_rel, preferred_element_type=jnp.float32)
+
+    weights = [
+        relative_blocks(
+            lax.all_gather(teacher_weight[0, slot_no], "mp", axis=0, tiled=True), 0, n_dp, me_dp
+        )
+        for slot_no in range(teacher_weight.shape[1])
+    ]
 
     mod_pick = jnp.take(modulation[0], timesteps, axis=1).astype(jnp.float32)
     mod_rows = jnp.repeat(mod_pick, per_sample, axis=1)
-    scale_rows = mod_rows[:, :, 0, :]
+    scale_rows = relative_blocks(mod_rows[:, :, 0, :], 2, n_dp, me_dp)
     gate_cols = lax.dynamic_slice_in_dim(mod_rows[:, :, 1, :], me_dp * col_width, col_width, 2)
     active = (jnp.arange(slot_count, dtype=jnp.int32) < layer_counts[0]).astype(jnp.float32)
 
@@ -119,10 +132,10 @@
             part_out = (active[slot_no] * gate_cols[slot_no] * jax.nn.gelu(pre_act)).astype(
                 jnp.bfloat16
             )
-            joined = gather_in_order(
-                part_out, ("section", "dp"), n_dp, me_dp, base=tick * n_dp
-            )
-            joined = jnp.concatenate(list(joined), axis=1)
+            joined = [part_out] + [
+                swap(part_out, ("section", "dp"), n_dp, d, base=tick * n_dp) for d in range(1, n_dp)
+            ]
+            joined = jnp.concatenate(joined, axis=1)
             stream = stream + joined.astype(jnp.float32)
             hit = feature_layers[tick] == tick * slot_count + slot_no
             tap = jnp.where(hit, stream.astype(jnp.bfloat16), tap)
@@ -157,19 +170,21 @@
         outgoing = lax.dynamic_index_in_dim(send_feat, me_mp ^ d, 0, keepdims=False)
         items.append(swap(outgoing, "mp", n_mp, d))
     loss_scale = width / math.sqrt(row_count * n_mp)
-    w_first = lax.dynamic_index_in_dim(head_in[:, 0], sec, 0, keepdims=False)
+    w_first = relative_blocks(
+        lax.dynamic_index_in_dim(head_in[:, 0], sec, 0, keepdims=False), 0, n_dp, me_dp
+    )
     w_second = lax.dynamic_index_in_dim(head_out[:, 0], sec, 0, keepdims=False)
     head_result = head_grads(
         jnp.concatenate(items, axis=0), w_first, w_second, loss_scale
     ).reshape(n_mp, capacity, width)
-    head_cols = lax.dynamic_slice_in_dim(head_result, me_dp * col_width, col_width, 2)
+    head_cols = head_result[:, :, :col_width]
     back = [head_cols[0]] + [swap(head_cols[d], "mp", n_mp, d) for d in range(1, n_mp)]
     by_owner = jnp.take(jnp.stack(back), me_mp ^ owner_range, axis=0)
     tap_grads = jnp.dot(
         dispatch, by_owner.reshape(n_mp * capacity, col_width), preferred_element_type=jnp.float32
     )
 
-    my_cols = lambda x: lax.dynamic_slice_in_dim(x, me_dp * col_width, col_width, x.ndim - 1)
+    my_cols = lambda x: x[..., :col_width]
     grad_stream = jnp.zeros((row_count, col_width), jnp.float32)
     for tick in range(n_sec):
         live = n_sec - 1 - tick
@@ -190,13 +205,12 @@
             pieces = [my_cols(partial)]
             terms = [row_term[None, :]]
             for d in range(1, n_dp):
-                block = lax.dynamic_slice_in_dim(partial, (me_dp ^ d) * col_width, col_width, 1)
+                block = partial[:, d * col_width:(d + 1) * col_width]
                 pairs = xor_pairs(n_dp, d, live * n_dp)
                 pieces.append(lax.ppermute(block, ("section", "dp"), pairs))
                 terms.append(lax.ppermute(row_term[None, :], ("section", "dp"), pairs))
-            order = me_dp ^ jnp.arange(n_dp, dtype=jnp.int32)
-            ordered = jnp.take(jnp.stack(pieces), order, axis=0).astype(jnp.float32)
-            term_rows = jnp.take(jnp.concatenate(terms, axis=0), order, axis=0)
+            ordered = jnp.stack(pieces).astype(jnp.float32)
+            term_rows = jnp.concatenate(terms, axis=0)
             input_grad = jnp.zeros((row_count, col_width), jnp.float32)
             row_sum = jnp.zeros((row_count,), jnp.float32)
             for src in range(n_dp):
@@ -214,7 +228,9 @@
 
     lat_part = student_weight.shape[1]
     latent_pre = jnp.dot(
-        grad_stream.astype(jnp.bfloat16), my_cols(patch_embed).T, preferred_element_type=jnp.float32
+        grad_stream.astype(jnp.bfloat16),
+        lax.dynamic_slice_in_dim(patch_embed, me_dp * col_width, col_width, 1).T,
+        preferred_element_type=jnp.float32,
     )
     got = [lax.dynamic_slice_in_dim(latent_pre, me_dp * lat_part, lat_part, 1)]
     for d in range(1, n_dp):

time: 893 us -> 744 us (0.83)
  waiting for transfers between devices: 354 us -> 282 us
  other arithmetic: 110 us -> 51 us
  matrix products: 92.5 us -> 74.9 us
    all_gather x1 -> x4, waiting for transfers between devices: 182 us -> 127 us  [on_device(): lax.all_gather(teacher_weight[0, slot_no], 'mp', axis=0, tiled=True)]
    dynamic_slice x0 -> x7, local copies, waits for them, and re-layouts: none -> 23.8 us  [relative_blocks(): lax.dynamic_slice_in_dim(x, (me ^ d) * width, width, axis)]
    gather x15 -> x7, local copies, waits for them, and re-layouts: 23.7 us -> 3.6 us  [gather_in_order(): return jnp.take(stacked, me ^ jnp.arange(n, dtype=jnp.int32), axis=0)]
    ppermute x24, waiting for transfers between devices: 19.6 us -> 0.06 us  [on_device(): pieces.append(lax.ppermute(block, ('section', 'dp'), pairs))]
    gather x16 -> x0, local copies, waits for them, and re-layouts: 18.5 us -> none  [the longest x8 14 us: on_device(): ordered = jnp.take(jnp.stack(pieces), order, axis=0).astype(jnp.float32)]
    another operation x13 -> x5, other arithmetic: 15.2 us -> 1.38 us  [gather_in_order(): stacked = jnp.stack(parts)]
    ppermute x24, waiting for transfers between devices: 0.06 us -> 11.9 us  [on_device(): terms.append(lax.ppermute(row_term[None, :], ('section', 'dp'), pairs))]
    select_n x14 -> x6, other arithmetic: 11.2 us -> 0.18 us  [gather_in_order(): return jnp.take(stacked, me ^ jnp.arange(n, dtype=jnp.int32), axis=0)]
  transfers between devices with their start and end apart: 105 -> 108, of which waited for: 34 -> 28; matrix products, arithmetic and copies ran while one was open for 4% -> 13% of each run, Pallas kernels for 0% -> 0%
where the time goes in v2:
time: 744 us; the launch traced here: 733 us
  waiting for transfers between devices  282 us (38%)
  starting transfers between devices  188 us (25%)
  local copies, waits for them, and re-layouts  114 us (15%)
  matrix products  74.9 us (10%)
  other arithmetic  51 us (7%)
  between operations  22.8 us (3%)
    all_gather x4, waiting for transfers between devices, on_device(): lax.all_gather(teacher_weight[0, slot_no], 'mp', axis=0, tiled=True)  127 us
    ppermute x1, waiting for transfers between devices, on_device(): lax.ppermute(grad_stream.astype(jnp.bfloat16), 'section', [(live, live -...  91.5 us
    ppermute x50, starting transfers between devices, swap(): return lax.ppermute(x, axis, xor_pairs(n, d, base))  82.7 us
    ppermute x24, starting transfers between devices, on_device(): pieces.append(lax.ppermute(block, ('section', 'dp'), pairs))  46.2 us
    ppermute x24, starting transfers between devices, on_device(): terms.append(lax.ppermute(row_term[None, :], ('section', 'dp'), pairs))  44.9 us
    ppermute x50, waiting for transfers between devices, swap(): return lax.ppermute(x, axis, xor_pairs(n, d, base))  44.6 us
    dot_general x8, matrix products, on_device(): jnp.dot(normed_in, weights[slot_no], preferred_element_type=jnp.float32)  34.6 us
    dot_general x8, matrix products, on_device(): jnp.dot(pre_grad, weights[slot_no].T, preferred_element_type=jnp.float32)  26.1 us
  transfers between devices with their start and end apart: 108, of which 28 were waited for; matrix products, arithmetic and copies ran while one was open for 13% of the time, Pallas kernels for 0%

profile of v2, /device:TPU:0, one launch (start us, length us, event | category | flops | bytes accessed | tf_op | source)
XLA Modules:
  0.0 733.0 jit_solution(18048394085575075909)
XLA Ops:
  7.2 3.6 fusion.378
  19.7 6.4 broadcast_in_dim.190
  26.1 11.7 %fusion.377 = (f32[4,192,1,2432]{3,1,2,0:T(8,128)}, f32[4,192,1,2432]{3,1,2,0:T(8,128)}) fusion(f32[4,192,2,2432]{3,1,2,0:T(8,128)} %bitcast.427), kind=kLoop, calls=%fused_computation.640 | loop fusion | bytes 29884416 | tf_op jit(solution)/shard_map/slice | solution.py:117
  38.0 9.0 %dynamic-slice_bitcast_fusion = (f32[4,192,608]{2,1,0:T(8,128)}, f32[4,192,608]{2,1,0:T(8,128)}, f32[4,192,608]{2,1,0:T(8,128)}, f32[4,192,608]{2,1,0:T(8,128)}) fusion(f32[4,192,1,2432]{3,1,2,0:T(8,128)} %get-tuple-element.9, s32[]{:T(128)S(6)} %select_n.373, s32[]{:T(128)S(6)} %select_n.372, s32[]{:T(128)S(6)} %select_n.371, s32[]{:T(128)S(6)} %select_n.370), kind=kLoop, calls=%fused_computation.35 | loop fusion | bytes 14942224 | tf_op jit(solution)/shard_map/dynamic_slice | solution.py:34
  48.8 9.6 %concatenate.53 = f32[4,192,2432]{2,1,0:T(8,128)} concatenate(f32[4,192,608]{2,1,0:T(8,128)} %get-tuple-element.17, f32[4,192,608]{2,1,0:T(8,128)} %get-tuple-element.16, f32[4,192,608]{2,1,0:T(8,128)} %get-tuple-element.15, f32[4,192,608]{2,1,0:T(8,128)} %get-tuple-element.14), dimensions={2} | concatenate | bytes 14942208 | tf_op jit(solution)/shard_map/concatenate | solution.py:33
  71.5 6.5 collective-permute-done.8
  87.5 4.3 multiply_convert_fusion.23
  101.6 46.6 %all-gather.11.cloned.1.call-done = bf16[1,1,2432,608]{3,2,1,0:T(8,128)(2,1)} async-done(((bf16[1,1,608,608]{3,2,1,0:T(8,128)(2,1)}), bf16[1,1,2432,608]{3,2,1,0:T(8,128)(2,1)}) %all-gather.11.cloned.1.call-update) | async-done | bytes 2957328 | tf_op jit(solution)/shard_map/all_gather | solution.py:109
  148.2 3.6 dynamic-slice_bitcast_fusion.15
  158.4 4.2 multiply_convert_fusion.22
  171.9 39.5 %all-gather.13.cloned.1.call-done = bf16[1,1,2432,608]{3,2,1,0:T(8,128)(2,1)} async-done(((bf16[1,1,608,608]{3,2,1,0:T(8,128)(2,1)}), bf16[1,1,2432,608]{3,2,1,0:T(8,128)(2,1)}) %all-gather.13.cloned.1.call-update) | async-done | bytes 2957328 | tf_op jit(solution)/shard_map/all_gather | solution.py:109
  211.4 3.6 dynamic-slice_bitcast_fusion.11
  222.7 4.1 multiply_convert_fusion.21
  236.0 38.5 %all-gather.15.cloned.1.call-done = bf16[1,1,2432,608]{3,2,1,0:T(8,128)(2,1)} async-done(((bf16[1,1,608,608]{3,2,1,0:T(8,128)(2,1)}), bf16[1,1,2432,608]{3,2,1,0:T(8,128)(2,1)}) %all-gather.15.cloned.1.call-update) | async-done | bytes 2957328 | tf_op jit(solution)/shard_map/all_gather | solution.py:109
  274.4 3.5 dynamic-slice_bitcast_fusion.7
  285.4 4.1 multiply_convert_fusion.20
  301.0 4.4 collective-permute-done.21
  316.1 5.4 multiply_convert_fusion.19
  331.1 4.2 multiply_convert_fusion.18
  349.6 4.1 multiply_convert_fusion.17
  364.4 4.1 multiply_convert_fusion.16
  380.2 7.0 convolution_convert_fusion
  397.9 3.9 collective-permute-done.35
  401.8 4.7 collective-permute-done.36
  417.9 4.0 collective-permute-start.38
  424.4 3.7 collective-permute-done.39
  431.3 4.7 convolution_convert_fusion.8
  477.8 91.5 %collective-permute-done.65 = bf16[192,608]{1,0:T(8,128)(2,1)S(1)} collective-permute-done((bf16[192,608]{1,0:T(8,128)(2,1)S(1)}, bf16[192,608]{1,0:T(8,128)(2,1)S(1)}, u32[]{:S(2)}, u32[]{:S(2)}) %collective-permute-start.65) | collective-permute-done | bytes 233504 | tf_op jit(solution)/shard_map/ppermute | solution.py:224
  572.8 3.6 collective-permute-start.66
  627.0 3.6 collective-permute-start.78
  636.8 3.5 collective-permute-start.81
  679.7 3.5 collective-permute-start.90
  (617 shorter events, 355.5 us)
Async XLA Ops:
  7.2 77.9 %all-gather.9.cloned.1.call-start = ((), (), s32[]{:S(2)}) async-start(), calls=%async_computation | async-start | bytes 3891200 | tf_op jit(solution)/shard_map/all_gather | solution.py:109
  10.9 137.3 %all-gather.11.cloned.1.call-start = ((), (), s32[]{:S(2)}) async-start(), calls=%async_computation.1 | async-start | bytes 3891200 | tf_op jit(solution)/shard_map/all_gather | solution.py:109
  11.6 199.7 %all-gather.13.cloned.1.call-start = ((), (), s32[]{:S(2)}) async-start(), calls=%async_computation.2 | async-start | bytes 3891200 | tf_op jit(solution)/shard_map/all_gather | solution.py:109
  12.4 262.1 %all-gather.15.cloned.1.call-start = ((), (), s32[]{:S(2)}) async-start(), calls=%async_computation.3 | async-start | bytes 3891200 | tf_op jit(solution)/shard_map/all_gather | solution.py:109
  12.5 45.9 %collective-permute-start = (bf16[304,16]{0,1:T(8,128)(2,1)S(1)}, bf16[304,16]{0,1:T(8,128)(2,1)S(1)}, u32[]{:S(2)}, u32[]{:S(2)}) collective-permute-start(bf16[304,16]{0,1:T(8,128)(2,1)S(1)} %convert_element_type.273), channel_id=1, source_target_pairs={{0,4},{4,0},{8,12},{12,8},{1,5},{5,1},{9,13},{13,9},{2,6},{6,2},{1... | collective-permute-start | bytes 29192 | tf_op jit(solution)/shard_map/ppermute | solution.py:22
  15.5 42.9 %collective-permute-start.1 = (bf16[304,16]{0,1:T(8,128)(2,1)S(1)}, bf16[304,16]{0,1:T(8,128)(2,1)S(1)}, u32[]{:S(2)}, u32[]{:S(2)}) collective-permute-start(bf16[304,16]{0,1:T(8,128)(2,1)S(1)} %convert_element_type.273), channel_id=1, source_target_pairs={{0,8},{4,12},{8,0},{12,4},{1,9},{5,13},{9,1},{13,5},{2,10},{6,14},... | collective-permute-start | bytes 29192 | tf_op jit(solution)/shard_map/ppermute | solution.py:22
  17.0 41.4 %collective-permute-start.2 = (bf16[304,16]{0,1:T(8,128)(2,1)S(1)}, bf16[304,16]{0,1:T(8,128)(2,1)S(1)}, u32[]{:S(2)}, u32[]{:S(2)}) collective-permute-start(bf16[304,16]{0,1:T(8,128)(2,1)S(1)} %convert_element_type.273), channel_id=1, source_target_pairs={{0,12},{4,8},{8,4},{12,0},{1,13},{5,9},{9,5},{13,1},{2,14},{6,10},... | collective-permute-start | bytes 29192 | tf_op jit(solution)/shard_map/ppermute | solution.py:22
  67.1 10.9 %collective-permute-start.8 = (bf16[304,64]{0,1:T(8,128)(2,1)S(1)}, bf16[304,64]{0,1:T(8,128)(2,1)S(1)}, u32[]{:S(2)}, u32[]{:S(2)}) collective-permute-start(bf16[304,64]{0,1:T(8,128)(2,1)S(1)} %pad_maximum_fusion.12), channel_id=1, source_target_pairs={{0,18},{1,19},{2,16},{3,17},{16,2},{17,3},{18,0},{19,1},{4,22},{5,... | collective-permute-start | bytes 116744 | tf_op jit(solution)/shard_map/ppermute | solution.py:22
  91.9 59.9 %collective-permute-start.10 = (bf16[192,608]{1,0:T(8,128)(2,1)S(1)}, bf16[192,608]{1,0:T(8,128)(2,1)S(1)}, u32[]{:S(2)}, u32[]{:S(2)}) collective-permute-start(bf16[192,608]{1,0:T(8,128)(2,1)S(1)} %get-tuple-element.108), channel_id=1, source_target_pairs={{0,4},{4,0},{8,12},{12,8},{1,5},{5,1},{9,13},{13,9},{2,6},{6,2},{1... | collective-permute-start | bytes 700424 | tf_op jit(solution)/shard_map/ppermute | solution.py:22
  95.2 56.5 %collective-permute-start.11 = (bf16[192,608]{1,0:T(8,128)(2,1)S(1)}, bf16[192,608]{1,0:T(8,128)(2,1)S(1)}, u32[]{:S(2)}, u32[]{:S(2)}) collective-permute-start(bf16[192,608]{1,0:T(8,128)(2,1)S(1)} %get-tuple-element.108), channel_id=1, source_target_pairs={{0,8},{4,12},{8,0},{12,4},{1,9},{5,13},{9,1},{13,5},{2,10},{6,14},... | collective-permute-start | bytes 700424 | tf_op jit(solution)/shard_map/ppermute | solution.py:22
  98.6 53.2 %collective-permute-start.12 = (bf16[192,608]{1,0:T(8,128)(2,1)S(1)}, bf16[192,608]{1,0:T(8,128)(2,1)}, u32[]{:S(2)}, u32[]{:S(2)}) collective-permute-start(bf16[192,608]{1,0:T(8,128)(2,1)S(1)} %get-tuple-element.108), channel_id=1, source_target_pairs={{0,12},{4,8},{8,4},{12,0},{1,13},{5,9},{9,5},{13,1},{2,14},{6,10},... | collective-permute-start | bytes 700424 | tf_op jit(solution)/shard_map/ppermute | solution.py:22
  162.6 52.4 %collective-permute-start.13 = (bf16[192,608]{1,0:T(8,128)(2,1)S(1)}, bf16[192,608]{1,0:T(8,128)(2,1)S(1)}, u32[]{:S(2)}, u32[]{:S(2)}) collective-permute-start(bf16[192,608]{1,0:T(8,128)(2,1)S(1)} %get-tuple-element.110), channel_id=1, source_target_pairs={{0,4},{4,0},{8,12},{12,8},{1,5},{5,1},{9,13},{13,9},{2,6},{6,2},{1... | collective-permute-start | bytes 700424 | tf_op jit(solution)/shard_map/ppermute | solution.py:22
  166.1 48.9 %collective-permute-start.14 = (bf16[192,608]{1,0:T(8,128)(2,1)S(1)}, bf16[192,608]{1,0:T(8,128)(2,1)S(1)}, u32[]{:S(2)}, u32[]{:S(2)}) collective-permute-start(bf16[192,608]{1,0:T(8,128)(2,1)S(1)} %get-tuple-element.110), channel_id=1, source_target_pairs={{0,8},{4,12},{8,0},{12,4},{1,9},{5,13},{9,1},{13,5},{2,10},{6,14},... | collective-permute-start | bytes 700424 | tf_op jit(solution)/shard_map/ppermute | solution.py:22
  169.4 45.6 %collective-permute-start.15 = (bf16[192,608]{1,0:T(8,128)(2,1)S(1)}, bf16[192,608]{1,0:T(8,128)(2,1)}, u32[]{:S(2)}, u32[]{:S(2)}) collective-permute-start(bf16[192,608]{1,0:T(8,128)(2,1)S(1)} %get-tuple-element.110), channel_id=1, source_target_pairs={{0,12},{4,8},{8,4},{12,0},{1,13},{5,9},{9,5},{13,1},{2,14},{6,10},... | collective-permute-start | bytes 700424 | tf_op jit(solution)/shard_map/ppermute | solution.py:22
  226.7 51.2 %collective-permute-start.16 = (bf16[192,608]{1,0:T(8,128)(2,1)S(1)}, bf16[192,608]{1,0:T(8,128)(2,1)S(1)}, u32[]{:S(2)}, u32[]{:S(2)}) collective-permute-start(bf16[192,608]{1,0:T(8,128)(2,1)S(1)} %get-tuple-element.112), channel_id=1, source_target_pairs={{0,4},{4,0},{8,12},{12,8},{1,5},{5,1},{9,13},{13,9},{2,6},{6,2},{1... | collective-permute-start | bytes 700424 | tf_op jit(solution)/shard_map/ppermute | solution.py:22
  230.2 47.8 %collective-permute-start.17 = (bf16[192,608]{1,0:T(8,128)(2,1)S(1)}, bf16[192,608]{1,0:T(8,128)(2,1)S(1)}, u32[]{:S(2)}, u32[]{:S(2)}) collective-permute-start(bf16[192,608]{1,0:T(8,128)(2,1)S(1)} %get-tuple-element.112), channel_id=1, source_target_pairs={{0,8},{4,12},{8,0},{12,4},{1,9},{5,13},{9,1},{13,5},{2,10},{6,14},... | collective-permute-start | bytes 700424 | tf_op jit(solution)/shard_map/ppermute | solution.py:22
  233.5 44.5 %collective-permute-start.18 = (bf16[192,608]{1,0:T(8,128)(2,1)S(1)}, bf16[192,608]{1,0:T(8,128)(2,1)}, u32[]{:S(2)}, u32[]{:S(2)}) collective-permute-start(bf16[192,608]{1,0:T(8,128)(2,1)S(1)} %get-tuple-element.112), channel_id=1, source_target_pairs={{0,12},{4,8},{8,4},{12,0},{1,13},{5,9},{9,5},{13,1},{2,14},{6,10},... | collective-permute-start | bytes 700424 | tf_op jit(solution)/shard_map/ppermute | solution.py:22
  391.7 14.8 %collective-permute-start.36 = (bf16[60,2432]{1,0:T(8,128)(2,1)}, bf16[60,2432]{1,0:T(8,128)(2,1)}, u32[]{:S(2)}, u32[]{:S(2)}) collective-permute-start(bf16[60,2432]{1,0:T(8,128)(2,1)} %get-tuple-element.48), channel_id=1, source_target_pairs={{0,2},{1,3},{2,0},{3,1},{4,6},{5,7},{6,4},{7,5},{8,10},{9,11},{10,... | collective-permute-start | bytes 875528 | tf_op jit(solution)/shard_map/ppermute | solution.py:22
  393.2 13.3 %collective-permute-start.37 = (bf16[60,2432]{1,0:T(8,128)(2,1)}, bf16[60,2432]{1,0:T(8,128)(2,1)}, u32[]{:S(2)}, u32[]{:S(2)}) collective-permute-start(bf16[60,2432]{1,0:T(8,128)(2,1)} %get-tuple-element.47), channel_id=1, source_target_pairs={{0,3},{1,2},{2,1},{3,0},{4,7},{5,6},{6,5},{7,4},{8,11},{9,10},{10,... | collective-permute-start | bytes 875528 | tf_op jit(solution)/shard_map/ppermute | solution.py:22
  476.4 93.0 %collective-permute-start.65 = (bf16[192,608]{1,0:T(8,128)(2,1)S(1)}, bf16[192,608]{1,0:T(8,128)(2,1)S(1)}, u32[]{:S(2)}, u32[]{:S(2)}) collective-permute-start(bf16[192,608]{1,0:T(8,128)(2,1)S(1)} %fusion.149), channel_id=1, source_target_pairs={{16,0},{17,1},{18,2},{19,3},{20,4},{21,5},{22,6},{23,7},{24,8},{25... | collective-permute-start | bytes 700424 | tf_op jit(solution)/shard_map/ppermute | solution.py:224
  572.8 22.0 %collective-permute-start.66 = (bf16[192,608]{1,0:T(8,128)(2,1)S(1)}, bf16[192,608]{1,0:T(8,128)(2,1)S(1)}, u32[]{:S(2)}, u32[]{:S(2)}) collective-permute-start(bf16[192,608]{1,0:T(8,128)(2,1)S(1)} %get-tuple-element.67), channel_id=1, source_target_pairs={{0,4},{4,0},{8,12},{12,8},{1,5},{5,1},{9,13},{13,9},{2,6},{6,2},{1... | collective-permute-start | bytes 700424 | tf_op jit(solution)/shard_map/ppermute | solution.py:210
  576.4 18.5 %collective-permute-start.67 = (bf16[192,608]{1,0:T(8,128)(2,1)S(1)}, bf16[192,608]{1,0:T(8,128)(2,1)S(1)}, u32[]{:S(2)}, u32[]{:S(2)}) collective-permute-start(bf16[192,608]{1,0:T(8,128)(2,1)S(1)} %get-tuple-element.66), channel_id=1, source_target_pairs={{0,8},{4,12},{8,0},{12,4},{1,9},{5,13},{9,1},{13,5},{2,10},{6,14},... | collective-permute-start | bytes 700424 | tf_op jit(solution)/shard_map/ppermute | solution.py:210
  578.7 16.1 %collective-permute-start.68 = (bf16[192,608]{1,0:T(8,128)(2,1)S(1)}, bf16[192,608]{1,0:T(8,128)(2,1)S(1)}, u32[]{:S(2)}, u32[]{:S(2)}) collective-permute-start(bf16[192,608]{1,0:T(8,128)(2,1)S(1)} %get-tuple-element.65), channel_id=1, source_target_pairs={{0,12},{4,8},{8,4},{12,0},{1,13},{5,9},{9,5},{13,1},{2,14},{6,10},... | collective-permute-start | bytes 700424 | tf_op jit(solution)/shard_map/ppermute | solution.py:210
  599.5 22.3 %collective-permute-start.72 = (bf16[192,608]{1,0:T(8,128)(2,1)S(1)}, bf16[192,608]{1,0:T(8,128)(2,1)S(1)}, u32[]{:S(2)}, u32[]{:S(2)}) collective-permute-start(bf16[192,608]{1,0:T(8,128)(2,1)S(1)} %get-tuple-element.63), channel_id=1, source_target_pairs={{0,4},{4,0},{8,12},{12,8},{1,5},{5,1},{9,13},{13,9},{2,6},{6,2},{1... | collective-permute-start | bytes 700424 | tf_op jit(solution)/shard_map/ppermute | solution.py:210
  602.9 19.0 %collective-permute-start.73 = (bf16[192,608]{1,0:T(8,128)(2,1)S(1)}, bf16[192,608]{1,0:T(8,128)(2,1)S(1)}, u32[]{:S(2)}, u32[]{:S(2)}) collective-permute-start(bf16[192,608]{1,0:T(8,128)(2,1)S(1)} %get-tuple-element.62), channel_id=1, source_target_pairs={{0,8},{4,12},{8,0},{12,4},{1,9},{5,13},{9,1},{13,5},{2,10},{6,14},... | collective-permute-start | bytes 700424 | tf_op jit(solution)/shard_map/ppermute | solution.py:210
  605.7 16.2 %collective-permute-start.74 = (bf16[192,608]{1,0:T(8,128)(2,1)S(1)}, bf16[192,608]{1,0:T(8,128)(2,1)S(1)}, u32[]{:S(2)}, u32[]{:S(2)}) collective-permute-start(bf16[192,608]{1,0:T(8,128)(2,1)S(1)} %get-tuple-element.61), channel_id=1, source_target_pairs={{0,12},{4,8},{8,4},{12,0},{1,13},{5,9},{9,5},{13,1},{2,14},{6,10},... | collective-permute-start | bytes 700424 | tf_op jit(solution)/shard_map/ppermute | solution.py:210
  627.0 22.0 %collective-permute-start.78 = (bf16[192,608]{1,0:T(8,128)(2,1)S(1)}, bf16[192,608]{1,0:T(8,128)(2,1)S(1)}, u32[]{:S(2)}, u32[]{:S(2)}) collective-permute-start(bf16[192,608]{1,0:T(8,128)(2,1)S(1)} %get-tuple-element.59), channel_id=1, source_target_pairs={{0,4},{4,0},{8,12},{12,8},{1,5},{5,1},{9,13},{13,9},{2,6},{6,2},{1... | collective-permute-start | bytes 700424 | tf_op jit(solution)/shard_map/ppermute | solution.py:210
  630.6 18.4 %collective-permute-start.79 = (bf16[192,608]{1,0:T(8,128)(2,1)S(1)}, bf16[192,608]{1,0:T(8,128)(2,1)S(1)}, u32[]{:S(2)}, u32[]{:S(2)}) collective-permute-start(bf16[192,608]{1,0:T(8,128)(2,1)S(1)} %get-tuple-element.58), channel_id=1, source_target_pairs={{0,8},{4,12},{8,0},{12,4},{1,9},{5,13},{9,1},{13,5},{2,10},{6,14},... | collective-permute-start | bytes 700424 | tf_op jit(solution)/shard_map/ppermute | solution.py:210
  632.9 16.1 %collective-permute-start.80 = (bf16[192,608]{1,0:T(8,128)(2,1)S(1)}, bf16[192,608]{1,0:T(8,128)(2,1)S(1)}, u32[]{:S(2)}, u32[]{:S(2)}) collective-permute-start(bf16[192,608]{1,0:T(8,128)(2,1)S(1)} %get-tuple-element.57), channel_id=1, source_target_pairs={{0,12},{4,8},{8,4},{12,0},{1,13},{5,9},{9,5},{13,1},{2,14},{6,10},... | collective-permute-start | bytes 700424 | tf_op jit(solution)/shard_map/ppermute | solution.py:210
  654.5 22.1 %collective-permute-start.84 = (bf16[192,608]{1,0:T(8,128)(2,1)}, bf16[192,608]{1,0:T(8,128)(2,1)}, u32[]{:S(2)}, u32[]{:S(2)}) collective-permute-start(bf16[192,608]{1,0:T(8,128)(2,1)} %get-tuple-element.55), channel_id=1, source_target_pairs={{0,4},{4,0},{8,12},{12,8},{1,5},{5,1},{9,13},{13,9},{2,6},{6,2},{1... | collective-permute-start | bytes 700424 | tf_op jit(solution)/shard_map/ppermute | solution.py:210
  657.6 19.0 %collective-permute-start.85 = (bf16[192,608]{1,0:T(8,128)(2,1)}, bf16[192,608]{1,0:T(8,128)(2,1)}, u32[]{:S(2)}, u32[]{:S(2)}) collective-permute-start(bf16[192,608]{1,0:T(8,128)(2,1)} %get-tuple-element.54), channel_id=1, source_target_pairs={{0,8},{4,12},{8,0},{12,4},{1,9},{5,13},{9,1},{13,5},{2,10},{6,14},... | collective-permute-start | bytes 700424 | tf_op jit(solution)/shard_map/ppermute | solution.py:210
  660.4 16.3 %collective-permute-start.86 = (bf16[192,608]{1,0:T(8,128)(2,1)}, bf16[192,608]{1,0:T(8,128)(2,1)}, u32[]{:S(2)}, u32[]{:S(2)}) collective-permute-start(bf16[192,608]{1,0:T(8,128)(2,1)} %get-tuple-element.53), channel_id=1, source_target_pairs={{0,12},{4,8},{8,4},{12,0},{1,13},{5,9},{9,5},{13,1},{2,14},{6,10},... | collective-permute-start | bytes 700424 | tf_op jit(solution)/shard_map/ppermute | solution.py:210
  (185 other events, 1610.8 us)
Sparse Core Ops, SparseCore 0:
  11.0 73.9 all-gather.8
  86.6 61.4 all-gather.10
  149.7 61.6 all-gather.12
  212.8 61.6 all-gather.14

commit v3 on v2

--- a/solution.py
+++ b/solution.py
@@ -202,20 +202,21 @@
             partial = lax.optimization_barrier(partial)
             scaled = 1.0 + scale_rows[slot_no]
             row_term = jnp.sum(partial.astype(jnp.float32) * scaled * normed, axis=-1)
-            pieces = [my_cols(partial)]
-            terms = [row_term[None, :]]
+            term_hi = row_term.astype(jnp.bfloat16)
+            term_lo = (row_term - term_hi.astype(jnp.float32)).astype(jnp.bfloat16)
+            terms = jnp.stack([term_hi, term_lo], axis=1)
+            pieces = [jnp.concatenate([my_cols(partial), terms], axis=1)]
             for d in range(1, n_dp):
                 block = partial[:, d * col_width:(d + 1) * col_width]
+                outgoing = jnp.concatenate([block, terms], axis=1)
                 pairs = xor_pairs(n_dp, d, live * n_dp)
-                pieces.append(lax.ppermute(block, ("section", "dp"), pairs))
-                terms.append(lax.ppermute(row_term[None, :], ("section", "dp"), pairs))
-            ordered = jnp.stack(pieces).astype(jnp.float32)
-            term_rows = jnp.concatenate(terms, axis=0)
+                pieces.append(lax.ppermute(outgoing, ("section", "dp"), pairs))
+            wide = jnp.stack(pieces).astype(jnp.float32)
             input_grad = jnp.zeros((row_count, col_width), jnp.float32)
             row_sum = jnp.zeros((row_count,), jnp.float32)
             for src in range(n_dp):
-                input_grad = input_grad + ordered[src]
-                row_sum = row_sum + term_rows[src]
+                input_grad = input_grad + wide[src, :, :col_width]
+                row_sum = row_sum + (wide[src, :, col_width] + wide[src, :, col_width + 1])
             row_mean = (row_sum / width)[:, None]
             grad_stream = grad_stream + inverse * (
                 input_grad * my_cols(scaled) - my_cols(normed) * row_mean

time: 744 us -> 747 us (level)
  starting transfers between devices: 188 us -> 144 us
  other arithmetic: 51 us -> 88.8 us
  local copies, waits for them, and re-layouts: 114 us -> 135 us
  waiting for transfers between devices: 282 us -> 270 us
    ppermute x48 -> x24, starting transfers between devices: 91.1 us -> 46.3 us  [on_device(): pieces.append(lax.ppermute(outgoing, ('section', 'dp'), pairs))]
    ppermute x1, waiting for transfers between devices: 91.5 us -> 69.5 us  [on_device(): lax.ppermute(grad_stream.astype(jnp.bfloat16), 'section', [(live, live -...]
    convert_element_type x0 -> x16, local copies, waits for them, and re-layouts: none -> 12.8 us  [the longest x8 7.36 us: on_device(): term_hi = row_term.astype(jnp.bfloat16)]
    another operation x3 -> x11, other arithmetic: 1.93 us -> 13.5 us  [the longest x8 11.5 us: on_device(): wide = jnp.stack(pieces).astype(jnp.float32)]
    reduce_sum x8, other arithmetic: 6.49 us -> 17.3 us  [on_device(): row_term = jnp.sum(partial.astype(jnp.float32) * scaled * normed, axis=-1)]
    ppermute x48 -> x24, waiting for transfers between devices: 11.9 us -> 22.2 us  [on_device(): pieces.append(lax.ppermute(outgoing, ('section', 'dp'), pairs))]
    slice x2 -> x10, local copies, waits for them, and re-layouts: 0.73 us -> 10.3 us  [the longest x8 9.58 us: on_device(): my_cols = lambda x: x[..., :col_width]]
    unnamed x229 -> x281, local copies, waits for them, and re-layouts: 17 us -> 17.6 us
  transfers between devices with their start and end apart: 108 -> 84, of which waited for: 28 -> 32; matrix products, arithmetic and copies ran while one was open for 13% -> 13% of each run, Pallas kernels for 0% -> 0%
where the time goes in v3:
time: 747 us; the launch traced here: 736 us
  waiting for transfers between devices  270 us (36%)
  starting transfers between devices  144 us (19%)
  local copies, waits for them, and re-layouts  135 us (18%)
  other arithmetic  88.8 us (12%)
  matrix products  75.5 us (10%)
  between operations  23.1 us (3%)
    all_gather x4, waiting for transfers between devices, on_device(): lax.all_gather(teacher_weight[0, slot_no], 'mp', axis=0, tiled=True)  127 us
    ppermute x50, starting transfers between devices, swap(): return lax.ppermute(x, axis, xor_pairs(n, d, base))  82.8 us
    ppermute x1, waiting for transfers between devices, on_device(): lax.ppermute(grad_stream.astype(jnp.bfloat16), 'section', [(live, live -...  69.5 us
    ppermute x24, starting transfers between devices, on_device(): pieces.append(lax.ppermute(outgoing, ('section', 'dp'), pairs))  46.3 us
    ppermute x50, waiting for transfers between devices, swap(): return lax.ppermute(x, axis, xor_pairs(n, d, base))  43.4 us
    dot_general x8, matrix products, on_device(): jnp.dot(normed_in, weights[slot_no], preferred_element_type=jnp.float32)  34.7 us
    dot_general x8, matrix products, on_device(): jnp.dot(pre_grad, weights[slot_no].T, preferred_element_type=jnp.float32)  25.4 us
    dynamic_slice x7, local copies, waits for them, and re-layouts, relative_blocks(): lax.dynamic_slice_in_dim(x, (me ^ d) * width, width, axis)  23.8 us
  transfers between devices with their start and end apart: 84, of which 32 were waited for; matrix products, arithmetic and copies ran while one was open for 13% of the time, Pallas kernels for 0%

profile of v3, /device:TPU:0, one launch (start us, length us, event | category | flops | bytes accessed | tf_op | source)
XLA Modules:
  0.0 735.7 jit_solution(7849638454639009034)
XLA Ops:
  19.7 6.4 broadcast_in_dim.150
  26.1 11.7 %fusion.425 = (f32[4,192,1,2432]{3,1,2,0:T(8,128)}, f32[4,192,1,2432]{3,1,2,0:T(8,128)}) fusion(f32[4,192,2,2432]{3,1,2,0:T(8,128)} %bitcast.401), kind=kLoop, calls=%fused_computation.776 | loop fusion | bytes 29884416 | tf_op jit(solution)/shard_map/slice | solution.py:117
  38.0 9.0 %dynamic-slice_bitcast_fusion = (f32[4,192,608]{2,1,0:T(8,128)}, f32[4,192,608]{2,1,0:T(8,128)}, f32[4,192,608]{2,1,0:T(8,128)}, f32[4,192,608]{2,1,0:T(8,128)}) fusion(f32[4,192,1,2432]{3,1,2,0:T(8,128)} %get-tuple-element.9, s32[]{:T(128)S(6)} %select_n.373, s32[]{:T(128)S(6)} %select_n.372, s32[]{:T(128)S(6)} %select_n.371, s32[]{:T(128)S(6)} %select_n.370), kind=kLoop, calls=%fused_computation.35 | loop fusion | bytes 14942224 | tf_op jit(solution)/shard_map/dynamic_slice | solution.py:34
  48.8 9.5 %concatenate.181 = f32[4,192,2432]{2,1,0:T(8,128)} concatenate(f32[4,192,608]{2,1,0:T(8,128)} %get-tuple-element.17, f32[4,192,608]{2,1,0:T(8,128)} %get-tuple-element.16, f32[4,192,608]{2,1,0:T(8,128)} %get-tuple-element.15, f32[4,192,608]{2,1,0:T(8,128)} %get-tuple-element.14), dimensions={2} | concatenate | bytes 14942208 | tf_op jit(solution)/shard_map/concatenate | solution.py:33
  71.4 6.5 collective-permute-done.8
  87.4 4.4 multiply_convert_fusion.23
  101.5 46.6 %all-gather.11.cloned.1.call-done = bf16[1,1,2432,608]{3,2,1,0:T(8,128)(2,1)} async-done(((bf16[1,1,608,608]{3,2,1,0:T(8,128)(2,1)}), bf16[1,1,2432,608]{3,2,1,0:T(8,128)(2,1)}) %all-gather.11.cloned.1.call-update) | async-done | bytes 2957328 | tf_op jit(solution)/shard_map/all_gather | solution.py:109
  158.4 4.1 multiply_convert_fusion.22
  171.8 39.6 %all-gather.13.cloned.1.call-done = bf16[1,1,2432,608]{3,2,1,0:T(8,128)(2,1)} async-done(((bf16[1,1,608,608]{3,2,1,0:T(8,128)(2,1)}), bf16[1,1,2432,608]{3,2,1,0:T(8,128)(2,1)}) %all-gather.13.cloned.1.call-update) | async-done | bytes 2957328 | tf_op jit(solution)/shard_map/all_gather | solution.py:109
  222.6 4.1 multiply_convert_fusion.21
  235.9 38.5 %all-gather.15.cloned.1.call-done = bf16[1,1,2432,608]{3,2,1,0:T(8,128)(2,1)} async-done(((bf16[1,1,608,608]{3,2,1,0:T(8,128)(2,1)}), bf16[1,1,2432,608]{3,2,1,0:T(8,128)(2,1)}) %all-gather.15.cloned.1.call-update) | async-done | bytes 2957328 | tf_op jit(solution)/shard_map/all_gather | solution.py:109
  274.4 3.7 dynamic-slice_bitcast_fusion.7
  285.5 4.2 multiply_convert_fusion.20
  301.1 4.4 collective-permute-done.21
  316.3 5.4 multiply_convert_fusion.19
  331.3 4.1 multiply_convert_fusion.18
  349.8 4.1 multiply_convert_fusion.17
  365.0 4.2 multiply_convert_fusion.16
  380.7 7.2 convolution_convert_fusion
  398.5 3.9 collective-permute-done.35
  402.4 4.7 collective-permute-done.36
  418.5 4.0 collective-permute-start.38
  433.7 4.2 convolution_convert_fusion.8
  448.0 5.8 fusion.12
  505.0 69.5 %collective-permute-done.53 = bf16[192,608]{1,0:T(8,128)(2,1)S(1)} collective-permute-done((bf16[192,608]{1,0:T(8,128)(2,1)S(1)}, bf16[192,608]{1,0:T(8,128)(2,1)S(1)}, u32[]{:S(2)}, u32[]{:S(2)}) %collective-permute-start.53) | collective-permute-done | bytes 233504 | tf_op jit(solution)/shard_map/ppermute | solution.py:225
  584.3 3.7 collective-permute-start.54
  596.1 4.3 collective-permute-done.56
  617.8 4.5 collective-permute-start.59
  639.2 3.7 collective-permute-start.60
  651.0 4.3 collective-permute-done.62
  671.2 4.5 collective-permute-start.65
  691.6 4.3 collective-permute-done.68
  (660 shorter events, 373.4 us)
Async XLA Ops:
  7.2 77.8 %all-gather.9.cloned.1.call-start = ((), (), s32[]{:S(2)}) async-start(), calls=%async_computation | async-start | bytes 3891200 | tf_op jit(solution)/shard_map/all_gather | solution.py:109
  10.8 137.3 %all-gather.11.cloned.1.call-start = ((), (), s32[]{:S(2)}) async-start(), calls=%async_computation.1 | async-start | bytes 3891200 | tf_op jit(solution)/shard_map/all_gather | solution.py:109
  11.6 199.7 %all-gather.13.cloned.1.call-start = ((), (), s32[]{:S(2)}) async-start(), calls=%async_computation.2 | async-start | bytes 3891200 | tf_op jit(solution)/shard_map/all_gather | solution.py:109
  12.3 262.1 %all-gather.15.cloned.1.call-start = ((), (), s32[]{:S(2)}) async-start(), calls=%async_computation.3 | async-start | bytes 3891200 | tf_op jit(solution)/shard_map/all_gather | solution.py:109
  12.4 45.9 %collective-permute-start = (bf16[304,16]{0,1:T(8,128)(2,1)S(1)}, bf16[304,16]{0,1:T(8,128)(2,1)S(1)}, u32[]{:S(2)}, u32[]{:S(2)}) collective-permute-start(bf16[304,16]{0,1:T(8,128)(2,1)S(1)} %convert_element_type.545), channel_id=1, source_target_pairs={{0,4},{4,0},{8,12},{12,8},{1,5},{5,1},{9,13},{13,9},{2,6},{6,2},{1... | collective-permute-start | bytes 29192 | tf_op jit(solution)/shard_map/ppermute | solution.py:22
  15.4 42.9 %collective-permute-start.1 = (bf16[304,16]{0,1:T(8,128)(2,1)S(1)}, bf16[304,16]{0,1:T(8,128)(2,1)S(1)}, u32[]{:S(2)}, u32[]{:S(2)}) collective-permute-start(bf16[304,16]{0,1:T(8,128)(2,1)S(1)} %convert_element_type.545), channel_id=1, source_target_pairs={{0,8},{4,12},{8,0},{12,4},{1,9},{5,13},{9,1},{13,5},{2,10},{6,14},... | collective-permute-start | bytes 29192 | tf_op jit(solution)/shard_map/ppermute | solution.py:22
  16.9 41.4 %collective-permute-start.2 = (bf16[304,16]{0,1:T(8,128)(2,1)S(1)}, bf16[304,16]{0,1:T(8,128)(2,1)S(1)}, u32[]{:S(2)}, u32[]{:S(2)}) collective-permute-start(bf16[304,16]{0,1:T(8,128)(2,1)S(1)} %convert_element_type.545), channel_id=1, source_target_pairs={{0,12},{4,8},{8,4},{12,0},{1,13},{5,9},{9,5},{13,1},{2,14},{6,10},... | collective-permute-start | bytes 29192 | tf_op jit(solution)/shard_map/ppermute | solution.py:22
  61.2 9.8 %collective-permute-start.4 = (bf16[304,64]{0,1:T(8,128)(2,1)S(1)}, bf16[304,64]{0,1:T(8,128)(2,1)S(1)}, u32[]{:S(2)}, u32[]{:S(2)}) collective-permute-start(bf16[304,64]{0,1:T(8,128)(2,1)S(1)} %pad_maximum_fusion.76), channel_id=1, source_target_pairs={{0,2},{1,3},{2,0},{3,1},{16,18},{17,19},{18,16},{19,17},{4,6},{5,7... | collective-permute-start | bytes 116744 | tf_op jit(solution)/shard_map/ppermute | solution.py:22
  67.0 11.0 %collective-permute-start.8 = (bf16[304,64]{0,1:T(8,128)(2,1)S(1)}, bf16[304,64]{0,1:T(8,128)(2,1)S(1)}, u32[]{:S(2)}, u32[]{:S(2)}) collective-permute-start(bf16[304,64]{0,1:T(8,128)(2,1)S(1)} %pad_maximum_fusion.76), channel_id=1, source_target_pairs={{0,18},{1,19},{2,16},{3,17},{16,2},{17,3},{18,0},{19,1},{4,22},{5,... | collective-permute-start | bytes 116744 | tf_op jit(solution)/shard_map/ppermute | solution.py:22
  91.8 59.9 %collective-permute-start.10 = (bf16[192,608]{1,0:T(8,128)(2,1)S(1)}, bf16[192,608]{1,0:T(8,128)(2,1)S(1)}, u32[]{:S(2)}, u32[]{:S(2)}) collective-permute-start(bf16[192,608]{1,0:T(8,128)(2,1)S(1)} %get-tuple-element.140), channel_id=1, source_target_pairs={{0,4},{4,0},{8,12},{12,8},{1,5},{5,1},{9,13},{13,9},{2,6},{6,2},{1... | collective-permute-start | bytes 700424 | tf_op jit(solution)/shard_map/ppermute | solution.py:22
  95.2 56.5 %collective-permute-start.11 = (bf16[192,608]{1,0:T(8,128)(2,1)S(1)}, bf16[192,608]{1,0:T(8,128)(2,1)S(1)}, u32[]{:S(2)}, u32[]{:S(2)}) collective-permute-start(bf16[192,608]{1,0:T(8,128)(2,1)S(1)} %get-tuple-element.140), channel_id=1, source_target_pairs={{0,8},{4,12},{8,0},{12,4},{1,9},{5,13},{9,1},{13,5},{2,10},{6,14},... | collective-permute-start | bytes 700424 | tf_op jit(solution)/shard_map/ppermute | solution.py:22
  98.6 53.1 %collective-permute-start.12 = (bf16[192,608]{1,0:T(8,128)(2,1)S(1)}, bf16[192,608]{1,0:T(8,128)(2,1)}, u32[]{:S(2)}, u32[]{:S(2)}) collective-permute-start(bf16[192,608]{1,0:T(8,128)(2,1)S(1)} %get-tuple-element.140), channel_id=1, source_target_pairs={{0,12},{4,8},{8,4},{12,0},{1,13},{5,9},{9,5},{13,1},{2,14},{6,10},... | collective-permute-start | bytes 700424 | tf_op jit(solution)/shard_map/ppermute | solution.py:22
  162.5 52.3 %collective-permute-start.13 = (bf16[192,608]{1,0:T(8,128)(2,1)S(1)}, bf16[192,608]{1,0:T(8,128)(2,1)S(1)}, u32[]{:S(2)}, u32[]{:S(2)}) collective-permute-start(bf16[192,608]{1,0:T(8,128)(2,1)S(1)} %get-tuple-element.142), channel_id=1, source_target_pairs={{0,4},{4,0},{8,12},{12,8},{1,5},{5,1},{9,13},{13,9},{2,6},{6,2},{1... | collective-permute-start | bytes 700424 | tf_op jit(solution)/shard_map/ppermute | solution.py:22
  166.0 48.9 %collective-permute-start.14 = (bf16[192,608]{1,0:T(8,128)(2,1)S(1)}, bf16[192,608]{1,0:T(8,128)(2,1)S(1)}, u32[]{:S(2)}, u32[]{:S(2)}) collective-permute-start(bf16[192,608]{1,0:T(8,128)(2,1)S(1)} %get-tuple-element.142), channel_id=1, source_target_pairs={{0,8},{4,12},{8,0},{12,4},{1,9},{5,13},{9,1},{13,5},{2,10},{6,14},... | collective-permute-start | bytes 700424 | tf_op jit(solution)/shard_map/ppermute | solution.py:22
  169.3 45.5 %collective-permute-start.15 = (bf16[192,608]{1,0:T(8,128)(2,1)S(1)}, bf16[192,608]{1,0:T(8,128)(2,1)}, u32[]{:S(2)}, u32[]{:S(2)}) collective-permute-start(bf16[192,608]{1,0:T(8,128)(2,1)S(1)} %get-tuple-element.142), channel_id=1, source_target_pairs={{0,12},{4,8},{8,4},{12,0},{1,13},{5,9},{9,5},{13,1},{2,14},{6,10},... | collective-permute-start | bytes 700424 | tf_op jit(solution)/shard_map/ppermute | solution.py:22
  226.7 51.4 %collective-permute-start.16 = (bf16[192,608]{1,0:T(8,128)(2,1)S(1)}, bf16[192,608]{1,0:T(8,128)(2,1)S(1)}, u32[]{:S(2)}, u32[]{:S(2)}) collective-permute-start(bf16[192,608]{1,0:T(8,128)(2,1)S(1)} %get-tuple-element.144), channel_id=1, source_target_pairs={{0,4},{4,0},{8,12},{12,8},{1,5},{5,1},{9,13},{13,9},{2,6},{6,2},{1... | collective-permute-start | bytes 700424 | tf_op jit(solution)/shard_map/ppermute | solution.py:22
  230.1 48.0 %collective-permute-start.17 = (bf16[192,608]{1,0:T(8,128)(2,1)S(1)}, bf16[192,608]{1,0:T(8,128)(2,1)S(1)}, u32[]{:S(2)}, u32[]{:S(2)}) collective-permute-start(bf16[192,608]{1,0:T(8,128)(2,1)S(1)} %get-tuple-element.144), channel_id=1, source_target_pairs={{0,8},{4,12},{8,0},{12,4},{1,9},{5,13},{9,1},{13,5},{2,10},{6,14},... | collective-permute-start | bytes 700424 | tf_op jit(solution)/shard_map/ppermute | solution.py:22
  233.4 44.6 %collective-permute-start.18 = (bf16[192,608]{1,0:T(8,128)(2,1)S(1)}, bf16[192,608]{1,0:T(8,128)(2,1)}, u32[]{:S(2)}, u32[]{:S(2)}) collective-permute-start(bf16[192,608]{1,0:T(8,128)(2,1)S(1)} %get-tuple-element.144), channel_id=1, source_target_pairs={{0,12},{4,8},{8,4},{12,0},{1,13},{5,9},{9,5},{13,1},{2,14},{6,10},... | collective-permute-start | bytes 700424 | tf_op jit(solution)/shard_map/ppermute | solution.py:22
  289.7 9.2 %collective-permute-start.19 = (bf16[192,608]{1,0:T(8,128)(2,1)S(1)}, bf16[192,608]{1,0:T(8,128)(2,1)S(1)}, u32[]{:S(2)}, u32[]{:S(2)}) collective-permute-start(bf16[192,608]{1,0:T(8,128)(2,1)S(1)} %get-tuple-element.146), channel_id=1, source_target_pairs={{0,4},{4,0},{8,12},{12,8},{1,5},{5,1},{9,13},{13,9},{2,6},{6,2},{1... | collective-permute-start | bytes 700424 | tf_op jit(solution)/shard_map/ppermute | solution.py:22
  296.4 9.1 %collective-permute-start.21 = (bf16[192,608]{1,0:T(8,128)(2,1)S(1)}, bf16[192,608]{1,0:T(8,128)(2,1)}, u32[]{:S(2)}, u32[]{:S(2)}) collective-permute-start(bf16[192,608]{1,0:T(8,128)(2,1)S(1)} %get-tuple-element.146), channel_id=1, source_target_pairs={{0,12},{4,8},{8,4},{12,0},{1,13},{5,9},{9,5},{13,1},{2,14},{6,10},... | collective-permute-start | bytes 700424 | tf_op jit(solution)/shard_map/ppermute | solution.py:22
  369.2 9.1 %collective-permute-start.32 = (bf16[192,608]{1,0:T(8,128)(2,1)S(1)}, bf16[192,608]{1,0:T(8,128)(2,1)S(1)}, u32[]{:S(2)}, u32[]{:S(2)}) collective-permute-start(bf16[192,608]{1,0:T(8,128)(2,1)S(1)} %get-tuple-element.154), channel_id=1, source_target_pairs={{16,20},{20,16},{24,28},{28,24},{17,21},{21,17},{25,29},{29,25},{1... | collective-permute-start | bytes 700424 | tf_op jit(solution)/shard_map/ppermute | solution.py:22
  392.3 10.1 %collective-permute-start.35 = (bf16[60,2432]{1,0:T(8,128)(2,1)}, bf16[60,2432]{1,0:T(8,128)(2,1)S(1)}, u32[]{:S(2)}, u32[]{:S(2)}) collective-permute-start(bf16[60,2432]{1,0:T(8,128)(2,1)} %get-tuple-element.49), channel_id=1, source_target_pairs={{0,1},{1,0},{2,3},{3,2},{4,5},{5,4},{6,7},{7,6},{8,9},{9,8},{10,11... | collective-permute-start | bytes 875528 | tf_op jit(solution)/shard_map/ppermute | solution.py:22
  392.3 14.8 %collective-permute-start.36 = (bf16[60,2432]{1,0:T(8,128)(2,1)}, bf16[60,2432]{1,0:T(8,128)(2,1)}, u32[]{:S(2)}, u32[]{:S(2)}) collective-permute-start(bf16[60,2432]{1,0:T(8,128)(2,1)} %get-tuple-element.48), channel_id=1, source_target_pairs={{0,2},{1,3},{2,0},{3,1},{4,6},{5,7},{6,4},{7,5},{8,10},{9,11},{10,... | collective-permute-start | bytes 875528 | tf_op jit(solution)/shard_map/ppermute | solution.py:22
  393.8 13.3 %collective-permute-start.37 = (bf16[60,2432]{1,0:T(8,128)(2,1)}, bf16[60,2432]{1,0:T(8,128)(2,1)}, u32[]{:S(2)}, u32[]{:S(2)}) collective-permute-start(bf16[60,2432]{1,0:T(8,128)(2,1)} %get-tuple-element.47), channel_id=1, source_target_pairs={{0,3},{1,2},{2,1},{3,0},{4,7},{5,6},{6,5},{7,4},{8,11},{9,10},{10,... | collective-permute-start | bytes 875528 | tf_op jit(solution)/shard_map/ppermute | solution.py:22
  503.3 71.2 %collective-permute-start.53 = (bf16[192,608]{1,0:T(8,128)(2,1)S(1)}, bf16[192,608]{1,0:T(8,128)(2,1)S(1)}, u32[]{:S(2)}, u32[]{:S(2)}) collective-permute-start(bf16[192,608]{1,0:T(8,128)(2,1)S(1)} %fusion.149), channel_id=1, source_target_pairs={{16,0},{17,1},{18,2},{19,3},{20,4},{21,5},{22,6},{23,7},{24,8},{25... | collective-permute-start | bytes 700424 | tf_op jit(solution)/shard_map/ppermute | solution.py:225
  584.3 9.4 %collective-permute-start.54 = (bf16[192,610]{1,0:T(8,128)(2,1)S(1)}, bf16[192,610]{1,0:T(8,128)(2,1)S(1)}, u32[]{:S(2)}, u32[]{:S(2)}) collective-permute-start(bf16[192,610]{1,0:T(8,128)(2,1)S(1)} %get-tuple-element.105), channel_id=1, source_target_pairs={{0,4},{4,0},{8,12},{12,8},{1,5},{5,1},{9,13},{13,9},{2,6},{6,2},{1... | collective-permute-start | bytes 702728 | tf_op jit(solution)/shard_map/ppermute | solution.py:213
  591.5 9.0 %collective-permute-start.56 = (bf16[192,610]{1,0:T(8,128)(2,1)S(1)}, bf16[192,610]{1,0:T(8,128)(2,1)S(1)}, u32[]{:S(2)}, u32[]{:S(2)}) collective-permute-start(bf16[192,610]{1,0:T(8,128)(2,1)S(1)} %get-tuple-element.107), channel_id=1, source_target_pairs={{0,12},{4,8},{8,4},{12,0},{1,13},{5,9},{9,5},{13,1},{2,14},{6,10},... | collective-permute-start | bytes 702728 | tf_op jit(solution)/shard_map/ppermute | solution.py:213
  612.9 9.4 %collective-permute-start.57 = (bf16[192,610]{1,0:T(8,128)(2,1)S(1)}, bf16[192,610]{1,0:T(8,128)(2,1)S(1)}, u32[]{:S(2)}, u32[]{:S(2)}) collective-permute-start(bf16[192,610]{1,0:T(8,128)(2,1)S(1)} %get-tuple-element.101), channel_id=1, source_target_pairs={{0,4},{4,0},{8,12},{12,8},{1,5},{5,1},{9,13},{13,9},{2,6},{6,2},{1... | collective-permute-start | bytes 702728 | tf_op jit(solution)/shard_map/ppermute | solution.py:213
  617.8 9.0 %collective-permute-start.59 = (bf16[192,610]{1,0:T(8,128)(2,1)S(1)}, bf16[192,610]{1,0:T(8,128)(2,1)S(1)}, u32[]{:S(2)}, u32[]{:S(2)}) collective-permute-start(bf16[192,610]{1,0:T(8,128)(2,1)S(1)} %get-tuple-element.103), channel_id=1, source_target_pairs={{0,12},{4,8},{8,4},{12,0},{1,13},{5,9},{9,5},{13,1},{2,14},{6,10},... | collective-permute-start | bytes 702728 | tf_op jit(solution)/shard_map/ppermute | solution.py:213
  639.2 9.5 %collective-permute-start.60 = (bf16[192,610]{1,0:T(8,128)(2,1)S(1)}, bf16[192,610]{1,0:T(8,128)(2,1)S(1)}, u32[]{:S(2)}, u32[]{:S(2)}) collective-permute-start(bf16[192,610]{1,0:T(8,128)(2,1)S(1)} %get-tuple-element.97), channel_id=1, source_target_pairs={{0,4},{4,0},{8,12},{12,8},{1,5},{5,1},{9,13},{13,9},{2,6},{6,2},{1... | collective-permute-start | bytes 702728 | tf_op jit(solution)/shard_map/ppermute | solution.py:213
  666.4 9.4 %collective-permute-start.63 = (bf16[192,610]{1,0:T(8,128)(2,1)}, bf16[192,610]{1,0:T(8,128)(2,1)S(1)}, u32[]{:S(2)}, u32[]{:S(2)}) collective-permute-start(bf16[192,610]{1,0:T(8,128)(2,1)} %get-tuple-element.93), channel_id=1, source_target_pairs={{0,4},{4,0},{8,12},{12,8},{1,5},{5,1},{9,13},{13,9},{2,6},{6,2},{1... | collective-permute-start | bytes 702728 | tf_op jit(solution)/shard_map/ppermute | solution.py:213
  682.3 9.2 %collective-permute-start.66 = (f32[192,16]{0,1:T(8,128)S(1)}, f32[192,16]{0,1:T(8,128)S(1)}, u32[]{:S(2)}, u32[]{:S(2)}) collective-permute-start(f32[192,16]{0,1:T(8,128)S(1)} %get-tuple-element.127), channel_id=1, source_target_pairs={{0,4},{4,0},{8,12},{12,8},{1,5},{5,1},{9,13},{13,9},{2,6},{6,2},{1... | collective-permute-start | bytes 36872 | tf_op jit(solution)/shard_map/ppermute | solution.py:239
  (187 other events, 1435.4 us)
Sparse Core Ops, SparseCore 0:
  11.0 73.9 all-gather.8
  86.6 61.4 all-gather.10
  149.7 61.6 all-gather.12
  212.7 61.6 all-gather.14

commit v4 on v3

--- a/solution.py
+++ b/solution.py
@@ -104,12 +104,28 @@
     embed_rel = relative_blocks(patch_embed, 1, n_dp, me_dp)
     start_stream = jnp.dot(noisy_input, embed_rel, preferred_element_type=jnp.float32)
 
-    weights = [
-        relative_blocks(
-            lax.all_gather(teacher_weight[0, slot_no], "mp", axis=0, tiled=True), 0, n_dp, me_dp
-        )
-        for slot_no in range(teacher_weight.shape[1])
-    ]
+    def gather_set(local, role):
+        pieces, arrived = [], []
+        for slot_no in range(local.shape[0]):
+            parts = [local[slot_no]]
+            for d in range(1, n_mp):
+                got = lax.ppermute(
+                    local[slot_no], ("section", "mp"), xor_pairs(n_mp, d, role * n_mp)
+                )
+                parts.append(got)
+                arrived.append(got[0, 0].astype(jnp.float32))
+            rows = jnp.take(jnp.stack(parts), me_mp ^ jnp.arange(n_mp, dtype=jnp.int32), axis=0)
+            pieces.append(relative_blocks(rows.reshape(width, -1), 0, n_dp, me_dp))
+        return pieces, sum(arrived)
+
+    weight_sets = []
+    local_weights = teacher_weight[0]
+    for role in range(n_sec):
+        pieces, token = gather_set(local_weights, role)
+        weight_sets.append(pieces)
+        if role + 1 < n_sec:
+            passed = lax.ppermute(token, "section", [(role, role + 1)])
+            local_weights, _ = lax.optimization_barrier((teacher_weight[0], passed))
 
     mod_pick = jnp.take(modulation[0], timesteps, axis=1).astype(jnp.float32)
     mod_rows = jnp.repeat(mod_pick, per_sample, axis=1)
@@ -127,7 +143,9 @@
             inverse = lax.rsqrt(jnp.mean(stream * stream, axis=-1, keepdims=True) + norm_eps)
             normed = stream * inverse
             normed_in = (normed * (1.0 + scale_rows[slot_no])).astype(jnp.bfloat16)
-            pre_act = jnp.dot(normed_in, weights[slot_no], preferred_element_type=jnp.float32)
+            pre_act = jnp.dot(
+                normed_in, weight_sets[tick][slot_no], preferred_element_type=jnp.float32
+            )
             tick_saved.append((normed, inverse, pre_act))
             part_out = (active[slot_no] * gate_cols[slot_no] * jax.nn.gelu(pre_act)).astype(
                 jnp.bfloat16
@@ -197,7 +215,7 @@
                 grad_stream * active[slot_no] * gate_cols[slot_no] * gelu_slope(pre_act)
             ).astype(jnp.bfloat16)
             partial = jnp.dot(
-                pre_grad, weights[slot_no].T, preferred_element_type=jnp.float32
+                pre_grad, weight_sets[live][slot_no].T, preferred_element_type=jnp.float32
             ).astype(jnp.bfloat16)
             partial = lax.optimization_barrier(partial)
             scaled = 1.0 + scale_rows[slot_no]

time: 747 us -> 921 us (1.23)
  starting transfers between devices: 144 us -> 244 us
  other arithmetic: 88.8 us -> 135 us
  local copies, waits for them, and re-layouts: 135 us -> 176 us
  between operations: 23.1 us -> 10.6 us
    all_gather x4 -> x0, waiting for transfers between devices: 127 us -> none  [on_device(): lax.all_gather(teacher_weight[0, slot_no], 'mp', axis=0, tiled=True)]
    ppermute x0 -> x24, waiting for transfers between devices: none -> 104 us  [gather_set(): lax.ppermute(local[slot_no], ('section', 'mp'), xor_pairs(n_mp, d, role *...]
    ppermute x0 -> x24, starting transfers between devices: none -> 103 us  [gather_set(): lax.ppermute(local[slot_no], ('section', 'mp'), xor_pairs(n_mp, d, role *...]
    gather x0 -> x8, local copies, waits for them, and re-layouts: none -> 35.6 us  [gather_set(): jnp.take(jnp.stack(parts), me_mp ^ jnp.arange(n_mp, dtype=jnp.int32), axi...]
    ppermute x50, waiting for transfers between devices: 43.4 us -> 77.7 us  [swap(): return lax.ppermute(x, axis, xor_pairs(n, d, base))]
    another operation x3 -> x11, other arithmetic: 1.93 us -> 28 us  [the longest x8 26.1 us: gather_set(): jnp.stack(parts)]
    select_n x0 -> x1, other arithmetic: none -> 17.3 us  [gather_set(): jnp.take(jnp.stack(parts), me_mp ^ jnp.arange(n_mp, dtype=jnp.int32), axi...]
    unnamed x281 -> x295, local copies, waits for them, and re-layouts: 17.6 us -> 6.31 us
  transfers between devices with their start and end apart: 84 -> 104, of which waited for: 32 -> 41; matrix products, arithmetic and copies ran while one was open for 13% -> 15% of each run, Pallas kernels for 0% -> 0%
where the time goes in v4:
time: 921 us; the launch traced here: 908 us
  waiting for transfers between devices  266 us (29%)
  starting transfers between devices  244 us (26%)
  local copies, waits for them, and re-layouts  176 us (19%)
  other arithmetic  135 us (15%)
  matrix products  76.9 us (8%)
  between operations  10.6 us (1%)
    ppermute x24, waiting for transfers between devices, gather_set(): lax.ppermute(local[slot_no], ('section', 'mp'), xor_pairs(n_mp, d, role *...  104 us
    ppermute x24, starting transfers between devices, gather_set(): lax.ppermute(local[slot_no], ('section', 'mp'), xor_pairs(n_mp, d, role *...  103 us
    ppermute x50, starting transfers between devices, swap(): return lax.ppermute(x, axis, xor_pairs(n, d, base))  81.3 us
    ppermute x50, waiting for transfers between devices, swap(): return lax.ppermute(x, axis, xor_pairs(n, d, base))  77.7 us
    ppermute x1, waiting for transfers between devices, on_device(): lax.ppermute(grad_stream.astype(jnp.bfloat16), 'section', [(live, live -...  60.6 us
    ppermute x24, starting transfers between devices, on_device(): pieces.append(lax.ppermute(outgoing, ('section', 'dp'), pairs))  45.4 us
    gather x8, local copies, waits for them, and re-layouts, gather_set(): jnp.take(jnp.stack(parts), me_mp ^ jnp.arange(n_mp, dtype=jnp.int32), axi...  35.6 us
    dot_general x8, matrix products, on_device(): jnp.dot(normed_in, weight_sets[tick][slot_no], preferred_element_type=jnp...  35.6 us
  transfers between devices with their start and end apart: 104, of which 41 were waited for; matrix products, arithmetic and copies ran while one was open for 15% of the time, Pallas kernels for 0%

profile of v4, /device:TPU:0, one launch (start us, length us, event | category | flops | bytes accessed | tf_op | source)
XLA Modules:
  0.0 907.6 jit_solution(8010149687196312429)
XLA Ops:
  0.7 4.7 fusion.442
  12.3 4.6 slice_bitcast_fusion.1
  18.9 6.3 broadcast_in_dim.159
  25.2 11.6 %fusion.441 = (f32[4,192,1,2432]{3,1,2,0:T(8,128)}, f32[4,192,1,2432]{3,1,2,0:T(8,128)}) fusion(f32[4,192,2,2432]{3,1,2,0:T(8,128)} %bitcast.426), kind=kLoop, calls=%fused_computation.849 | loop fusion | bytes 29884416 | tf_op jit(solution)/shard_map/slice | solution.py:133
  38.6 8.8 dynamic-slice_bitcast_fusion
  47.8 9.5 %concatenate.193 = f32[4,192,2432]{2,1,0:T(8,128)} concatenate(f32[4,192,608]{2,1,0:T(8,128)} %get-tuple-element.18, f32[4,192,608]{2,1,0:T(8,128)} %get-tuple-element.17, f32[4,192,608]{2,1,0:T(8,128)} %get-tuple-element.16, f32[4,192,608]{2,1,0:T(8,128)} %get-tuple-element.15), dimensions={2} | concatenate | bytes 14942208 | tf_op jit(solution)/shard_map/concatenate | solution.py:33
  58.8 5.9 collective-permute-start.18
  65.6 16.5 %collective-permute-done.3 = bf16[304,64]{0,1:T(8,128)(2,1)S(1)} collective-permute-done((bf16[304,64]{0,1:T(8,128)(2,1)S(1)}, bf16[304,64]{0,1:T(8,128)(2,1)S(1)}, u32[]{:S(2)}, u32[]{:S(2)}) %collective-permute-start.3) | collective-permute-done | bytes 38944 | tf_op jit(solution)/shard_map/ppermute | solution.py:22
  99.2 4.9 collective-permute-done.8
  111.5 4.5 collective-permute-start.16
  121.7 4.5 collective-permute-start.22
  128.9 41.2 %collective-permute-done.17 = bf16[608,608]{1,0:T(8,128)(2,1)} collective-permute-done((bf16[608,608]{1,0:T(8,128)(2,1)}, bf16[608,608]{1,0:T(8,128)(2,1)}, u32[]{:S(2)}, u32[]{:S(2)}) %collective-permute-start.17) | collective-permute-done | bytes 739360 | tf_op jit(solution)/shard_map/ppermute | solution.py:112
  176.1 46.5 %collective-permute-start.28 = (bf16[608,608]{1,0:T(8,128)(2,1)}, bf16[608,608]{1,0:T(8,128)(2,1)}, u32[]{:S(2)}, u32[]{:S(2)}) collective-permute-start(bf16[608,608]{1,0:T(8,128)(2,1)} %get-tuple-element.51), channel_id=1, source_target_pairs={{0,1},{1,0},{2,3},{3,2},{4,5},{5,4},{6,7},{7,6},{8,9},{9,8},{10,11... | collective-permute-start | bytes 2217992 | tf_op jit(solution)/shard_map/ppermute | solution.py:112
  222.6 22.6 %collective-permute-done.23 = bf16[608,608]{1,0:T(8,128)(2,1)} collective-permute-done((bf16[608,608]{1,0:T(8,128)(2,1)}, bf16[608,608]{1,0:T(8,128)(2,1)}, u32[]{:S(2)}, u32[]{:S(2)}) %collective-permute-start.23) | collective-permute-done | bytes 739360 | tf_op jit(solution)/shard_map/ppermute | solution.py:112
  251.3 35.7 %collective-permute-done.29 = bf16[608,608]{1,0:T(8,128)(2,1)} collective-permute-done((bf16[608,608]{1,0:T(8,128)(2,1)}, bf16[608,608]{1,0:T(8,128)(2,1)}, u32[]{:S(2)}, u32[]{:S(2)}) %collective-permute-start.29) | collective-permute-done | bytes 739360 | tf_op jit(solution)/shard_map/ppermute | solution.py:112
  291.6 4.4 gather_fusion.16
  304.1 4.5 gather_fusion.10
  322.6 4.6 gather_fusion.12
  340.6 4.5 gather_fusion.13
  356.1 4.4 gather_fusion.15
  360.5 4.5 collective-permute-done.11
  368.4 4.4 gather_fusion.9
  372.8 17.3 %broadcast_select_fusion = (bf16[4,608,608]{2,1,0:T(8,128)(2,1)}, bf16[4,608,608]{2,1,0:T(8,128)(2,1)}, bf16[4,608,608]{2,1,0:T(8,128)(2,1)}, bf16[4,608,608]{2,...) fusion(bf16[4,608,608]{2,1,0:T(8,128)(2,1)} %gather_fusion.16, ...), kind=kLoop, calls=%fused_computation.42 | loop fusion | flops 11829248 | bytes 47316996 | tf_op jit(solution)/shard_map/jit(_take)/select_n | solution.py:117
  426.6 4.8 collective-permute-start.21
  499.0 4.5 multiply_convert_fusion.19
  520.6 5.1 multiply_convert_fusion.18
  536.8 5.1 multiply_convert_fusion.17
  570.9 7.0 convolution_convert_fusion
  591.5 6.6 collective-permute-done.60
  616.7 7.8 collective-permute-done.63
  642.2 5.8 fusion.12
  700.2 60.6 %collective-permute-done.77 = bf16[192,608]{1,0:T(8,128)(2,1)S(1)} collective-permute-done((bf16[192,608]{1,0:T(8,128)(2,1)S(1)}, bf16[192,608]{1,0:T(8,128)(2,1)S(1)}, u32[]{:S(2)}, u32[]{:S(2)}) %collective-permute-start.77) | collective-permute-done | bytes 233504 | tf_op jit(solution)/shard_map/ppermute | solution.py:243
  (734 shorter events, 513.3 us)
Async XLA Ops:
  5.4 106.1 %collective-permute-start.55 = (bf16[608,608]{1,0:T(8,128)(2,1)}, bf16[608,608]{1,0:T(8,128)(2,1)S(1)}, u32[]{:S(2)}, u32[]{:S(2)}) collective-permute-start(bf16[608,608]{1,0:T(8,128)(2,1)} %get-tuple-element.27), channel_id=1, source_target_pairs={{16,19},{17,18},{18,17},{19,16},{20,23},{21,22},{22,21},{23,20},{2... | collective-permute-start | bytes 2217992 | tf_op jit(solution)/shard_map/ppermute | solution.py:112
  6.1 110.0 %collective-permute-start.54 = (bf16[608,608]{1,0:T(8,128)(2,1)}, bf16[608,608]{1,0:T(8,128)(2,1)}, u32[]{:S(2)}, u32[]{:S(2)}) collective-permute-start(bf16[608,608]{1,0:T(8,128)(2,1)} %get-tuple-element.27), channel_id=1, source_target_pairs={{16,18},{17,19},{18,16},{19,17},{20,22},{21,23},{22,20},{23,21},{2... | collective-permute-start | bytes 2217992 | tf_op jit(solution)/shard_map/ppermute | solution.py:112
  7.7 49.6 %collective-permute-start.2 = (bf16[304,16]{0,1:T(8,128)(2,1)S(1)}, bf16[304,16]{0,1:T(8,128)(2,1)S(1)}, u32[]{:S(2)}, u32[]{:S(2)}) collective-permute-start(bf16[304,16]{0,1:T(8,128)(2,1)S(1)} %convert_element_type.557), channel_id=1, source_target_pairs={{0,12},{4,8},{8,4},{12,0},{1,13},{5,9},{9,5},{13,1},{2,14},{6,10},... | collective-permute-start | bytes 29192 | tf_op jit(solution)/shard_map/ppermute | solution.py:22
  11.6 47.2 %collective-permute-start.1 = (bf16[304,16]{0,1:T(8,128)(2,1)S(1)}, bf16[304,16]{0,1:T(8,128)(2,1)S(1)}, u32[]{:S(2)}, u32[]{:S(2)}) collective-permute-start(bf16[304,16]{0,1:T(8,128)(2,1)S(1)} %convert_element_type.557), channel_id=1, source_target_pairs={{0,8},{4,12},{8,0},{12,4},{1,9},{5,13},{9,1},{13,5},{2,10},{6,14},... | collective-permute-start | bytes 29192 | tf_op jit(solution)/shard_map/ppermute | solution.py:22
  12.1 52.7 %collective-permute-start = (bf16[304,16]{0,1:T(8,128)(2,1)S(1)}, bf16[304,16]{0,1:T(8,128)(2,1)S(1)}, u32[]{:S(2)}, u32[]{:S(2)}) collective-permute-start(bf16[304,16]{0,1:T(8,128)(2,1)S(1)} %convert_element_type.557), channel_id=1, source_target_pairs={{0,4},{4,0},{8,12},{12,8},{1,5},{5,1},{9,13},{13,9},{2,6},{6,2},{1... | collective-permute-start | bytes 29192 | tf_op jit(solution)/shard_map/ppermute | solution.py:22
  57.3 62.5 %collective-permute-start.53 = (bf16[608,608]{1,0:T(8,128)(2,1)}, bf16[608,608]{1,0:T(8,128)(2,1)}, u32[]{:S(2)}, u32[]{:S(2)}) collective-permute-start(bf16[608,608]{1,0:T(8,128)(2,1)} %get-tuple-element.27), channel_id=1, source_target_pairs={{16,17},{17,16},{18,19},{19,18},{20,21},{21,20},{22,23},{23,22},{2... | collective-permute-start | bytes 2217992 | tf_op jit(solution)/shard_map/ppermute | solution.py:112
  58.8 62.9 %collective-permute-start.18 = (bf16[608,608]{1,0:T(8,128)(2,1)}, bf16[608,608]{1,0:T(8,128)(2,1)}, u32[]{:S(2)}, u32[]{:S(2)}) collective-permute-start(bf16[608,608]{1,0:T(8,128)(2,1)} %get-tuple-element.49), channel_id=1, source_target_pairs={{0,3},{1,2},{2,1},{3,0},{4,7},{5,6},{6,5},{7,4},{8,11},{9,10},{10,... | collective-permute-start | bytes 2217992 | tf_op jit(solution)/shard_map/ppermute | solution.py:112
  65.5 16.6 %collective-permute-start.3 = (bf16[304,64]{0,1:T(8,128)(2,1)S(1)}, bf16[304,64]{0,1:T(8,128)(2,1)S(1)}, u32[]{:S(2)}, u32[]{:S(2)}) collective-permute-start(bf16[304,64]{0,1:T(8,128)(2,1)S(1)} %pad_maximum_fusion.104), channel_id=1, source_target_pairs={{0,1},{1,0},{2,3},{3,2},{16,17},{17,16},{18,19},{19,18},{4,5},{5,4... | collective-permute-start | bytes 116744 | tf_op jit(solution)/shard_map/ppermute | solution.py:22
  109.6 60.5 %collective-permute-start.17 = (bf16[608,608]{1,0:T(8,128)(2,1)}, bf16[608,608]{1,0:T(8,128)(2,1)}, u32[]{:S(2)}, u32[]{:S(2)}) collective-permute-start(bf16[608,608]{1,0:T(8,128)(2,1)} %get-tuple-element.49), channel_id=1, source_target_pairs={{0,2},{1,3},{2,0},{3,1},{4,6},{5,7},{6,4},{7,5},{8,10},{9,11},{10,... | collective-permute-start | bytes 2217992 | tf_op jit(solution)/shard_map/ppermute | solution.py:112
  111.5 62.6 %collective-permute-start.16 = (bf16[608,608]{1,0:T(8,128)(2,1)}, bf16[608,608]{1,0:T(8,128)(2,1)}, u32[]{:S(2)}, u32[]{:S(2)}) collective-permute-start(bf16[608,608]{1,0:T(8,128)(2,1)} %get-tuple-element.49), channel_id=1, source_target_pairs={{0,1},{1,0},{2,3},{3,2},{4,5},{5,4},{6,7},{7,6},{8,9},{9,8},{10,11... | collective-permute-start | bytes 2217992 | tf_op jit(solution)/shard_map/ppermute | solution.py:112
  116.1 60.0 %collective-permute-start.24 = (bf16[608,608]{1,0:T(8,128)(2,1)}, bf16[608,608]{1,0:T(8,128)(2,1)}, u32[]{:S(2)}, u32[]{:S(2)}) collective-permute-start(bf16[608,608]{1,0:T(8,128)(2,1)} %get-tuple-element.50), channel_id=1, source_target_pairs={{0,3},{1,2},{2,1},{3,0},{4,7},{5,6},{6,5},{7,4},{8,11},{9,10},{10,... | collective-permute-start | bytes 2217992 | tf_op jit(solution)/shard_map/ppermute | solution.py:112
  119.8 125.4 %collective-permute-start.23 = (bf16[608,608]{1,0:T(8,128)(2,1)}, bf16[608,608]{1,0:T(8,128)(2,1)}, u32[]{:S(2)}, u32[]{:S(2)}) collective-permute-start(bf16[608,608]{1,0:T(8,128)(2,1)} %get-tuple-element.50), channel_id=1, source_target_pairs={{0,2},{1,3},{2,0},{3,1},{4,6},{5,7},{6,4},{7,5},{8,10},{9,11},{10,... | collective-permute-start | bytes 2217992 | tf_op jit(solution)/shard_map/ppermute | solution.py:112
  121.7 125.0 %collective-permute-start.22 = (bf16[608,608]{1,0:T(8,128)(2,1)}, bf16[608,608]{1,0:T(8,128)(2,1)}, u32[]{:S(2)}, u32[]{:S(2)}) collective-permute-start(bf16[608,608]{1,0:T(8,128)(2,1)} %get-tuple-element.50), channel_id=1, source_target_pairs={{0,1},{1,0},{2,3},{3,2},{4,5},{5,4},{6,7},{7,6},{8,9},{9,8},{10,11... | collective-permute-start | bytes 2217992 | tf_op jit(solution)/shard_map/ppermute | solution.py:112
  170.1 79.6 %collective-permute-start.30 = (bf16[608,608]{1,0:T(8,128)(2,1)}, bf16[608,608]{1,0:T(8,128)(2,1)}, u32[]{:S(2)}, u32[]{:S(2)}) collective-permute-start(bf16[608,608]{1,0:T(8,128)(2,1)} %get-tuple-element.51), channel_id=1, source_target_pairs={{0,3},{1,2},{2,1},{3,0},{4,7},{5,6},{6,5},{7,4},{8,11},{9,10},{10,... | collective-permute-start | bytes 2217992 | tf_op jit(solution)/shard_map/ppermute | solution.py:112
  174.1 112.8 %collective-permute-start.29 = (bf16[608,608]{1,0:T(8,128)(2,1)}, bf16[608,608]{1,0:T(8,128)(2,1)}, u32[]{:S(2)}, u32[]{:S(2)}) collective-permute-start(bf16[608,608]{1,0:T(8,128)(2,1)} %get-tuple-element.51), channel_id=1, source_target_pairs={{0,2},{1,3},{2,0},{3,1},{4,6},{5,7},{6,4},{7,5},{8,10},{9,11},{10,... | collective-permute-start | bytes 2217992 | tf_op jit(solution)/shard_map/ppermute | solution.py:112
  176.1 119.9 %collective-permute-start.28 = (bf16[608,608]{1,0:T(8,128)(2,1)}, bf16[608,608]{1,0:T(8,128)(2,1)}, u32[]{:S(2)}, u32[]{:S(2)}) collective-permute-start(bf16[608,608]{1,0:T(8,128)(2,1)} %get-tuple-element.51), channel_id=1, source_target_pairs={{0,1},{1,0},{2,3},{3,2},{4,5},{5,4},{6,7},{7,6},{8,9},{9,8},{10,11... | collective-permute-start | bytes 2217992 | tf_op jit(solution)/shard_map/ppermute | solution.py:112
  245.2 52.4 %collective-permute-start.37 = (bf16[608,608]{1,0:T(8,128)(2,1)}, bf16[608,608]{1,0:T(8,128)(2,1)}, u32[]{:S(2)}, u32[]{:S(2)}) collective-permute-start(bf16[608,608]{1,0:T(8,128)(2,1)} %get-tuple-element.24), channel_id=1, source_target_pairs={{16,19},{17,18},{18,17},{19,16},{20,23},{21,22},{22,21},{23,20},{2... | collective-permute-start | bytes 2217992 | tf_op jit(solution)/shard_map/ppermute | solution.py:112
  246.7 52.4 %collective-permute-start.36 = (bf16[608,608]{1,0:T(8,128)(2,1)}, bf16[608,608]{1,0:T(8,128)(2,1)}, u32[]{:S(2)}, u32[]{:S(2)}) collective-permute-start(bf16[608,608]{1,0:T(8,128)(2,1)} %get-tuple-element.24), channel_id=1, source_target_pairs={{16,18},{17,19},{18,16},{19,17},{20,22},{21,23},{22,20},{23,21},{2... | collective-permute-start | bytes 2217992 | tf_op jit(solution)/shard_map/ppermute | solution.py:112
  249.7 66.6 %collective-permute-start.35 = (bf16[608,608]{1,0:T(8,128)(2,1)}, bf16[608,608]{1,0:T(8,128)(2,1)}, u32[]{:S(2)}, u32[]{:S(2)}) collective-permute-start(bf16[608,608]{1,0:T(8,128)(2,1)} %get-tuple-element.24), channel_id=1, source_target_pairs={{16,17},{17,16},{18,19},{19,18},{20,21},{21,20},{22,23},{23,22},{2... | collective-permute-start | bytes 2217992 | tf_op jit(solution)/shard_map/ppermute | solution.py:112
  286.9 30.9 %collective-permute-start.43 = (bf16[608,608]{1,0:T(8,128)(2,1)}, bf16[608,608]{1,0:T(8,128)(2,1)}, u32[]{:S(2)}, u32[]{:S(2)}) collective-permute-start(bf16[608,608]{1,0:T(8,128)(2,1)} %get-tuple-element.25), channel_id=1, source_target_pairs={{16,19},{17,18},{18,17},{19,16},{20,23},{21,22},{22,21},{23,20},{2... | collective-permute-start | bytes 2217992 | tf_op jit(solution)/shard_map/ppermute | solution.py:112
  296.0 31.2 %collective-permute-start.42 = (bf16[608,608]{1,0:T(8,128)(2,1)}, bf16[608,608]{1,0:T(8,128)(2,1)}, u32[]{:S(2)}, u32[]{:S(2)}) collective-permute-start(bf16[608,608]{1,0:T(8,128)(2,1)} %get-tuple-element.25), channel_id=1, source_target_pairs={{16,18},{17,19},{18,16},{19,17},{20,22},{21,23},{22,20},{23,21},{2... | collective-permute-start | bytes 2217992 | tf_op jit(solution)/shard_map/ppermute | solution.py:112
  297.5 33.7 %collective-permute-start.41 = (bf16[608,608]{1,0:T(8,128)(2,1)}, bf16[608,608]{1,0:T(8,128)(2,1)}, u32[]{:S(2)}, u32[]{:S(2)}) collective-permute-start(bf16[608,608]{1,0:T(8,128)(2,1)} %get-tuple-element.25), channel_id=1, source_target_pairs={{16,17},{17,16},{18,19},{19,18},{20,21},{21,20},{22,23},{23,22},{2... | collective-permute-start | bytes 2217992 | tf_op jit(solution)/shard_map/ppermute | solution.py:112
  299.1 34.1 %collective-permute-start.49 = (bf16[608,608]{1,0:T(8,128)(2,1)}, bf16[608,608]{1,0:T(8,128)(2,1)}, u32[]{:S(2)}, u32[]{:S(2)}) collective-permute-start(bf16[608,608]{1,0:T(8,128)(2,1)} %get-tuple-element.26), channel_id=1, source_target_pairs={{16,19},{17,18},{18,17},{19,16},{20,23},{21,22},{22,21},{23,20},{2... | collective-permute-start | bytes 2217992 | tf_op jit(solution)/shard_map/ppermute | solution.py:112
  316.3 36.5 %collective-permute-start.48 = (bf16[608,608]{1,0:T(8,128)(2,1)}, bf16[608,608]{1,0:T(8,128)(2,1)}, u32[]{:S(2)}, u32[]{:S(2)}) collective-permute-start(bf16[608,608]{1,0:T(8,128)(2,1)} %get-tuple-element.26), channel_id=1, source_target_pairs={{16,18},{17,19},{18,16},{19,17},{20,22},{21,23},{22,20},{23,21},{2... | collective-permute-start | bytes 2217992 | tf_op jit(solution)/shard_map/ppermute | solution.py:112
  317.9 34.9 %collective-permute-start.47 = (bf16[608,608]{1,0:T(8,128)(2,1)}, bf16[608,608]{1,0:T(8,128)(2,1)}, u32[]{:S(2)}, u32[]{:S(2)}) collective-permute-start(bf16[608,608]{1,0:T(8,128)(2,1)} %get-tuple-element.26), channel_id=1, source_target_pairs={{16,17},{17,16},{18,19},{19,18},{20,21},{21,20},{22,23},{23,22},{2... | collective-permute-start | bytes 2217992 | tf_op jit(solution)/shard_map/ppermute | solution.py:112
  327.2 33.3 %collective-permute-start.12 = (bf16[608,608]{1,0:T(8,128)(2,1)}, bf16[608,608]{1,0:T(8,128)(2,1)}, u32[]{:S(2)}, u32[]{:S(2)}) collective-permute-start(bf16[608,608]{1,0:T(8,128)(2,1)} %get-tuple-element.48), channel_id=1, source_target_pairs={{0,3},{1,2},{2,1},{3,0},{4,7},{5,6},{6,5},{7,4},{8,11},{9,10},{10,... | collective-permute-start | bytes 2217992 | tf_op jit(solution)/shard_map/ppermute | solution.py:112
  331.2 33.8 %collective-permute-start.11 = (bf16[608,608]{1,0:T(8,128)(2,1)}, bf16[608,608]{1,0:T(8,128)(2,1)}, u32[]{:S(2)}, u32[]{:S(2)}) collective-permute-start(bf16[608,608]{1,0:T(8,128)(2,1)} %get-tuple-element.48), channel_id=1, source_target_pairs={{0,2},{1,3},{2,0},{3,1},{4,6},{5,7},{6,4},{7,5},{8,10},{9,11},{10,... | collective-permute-start | bytes 2217992 | tf_op jit(solution)/shard_map/ppermute | solution.py:112
  333.2 31.9 %collective-permute-start.10 = (bf16[608,608]{1,0:T(8,128)(2,1)}, bf16[608,608]{1,0:T(8,128)(2,1)}, u32[]{:S(2)}, u32[]{:S(2)}) collective-permute-start(bf16[608,608]{1,0:T(8,128)(2,1)} %get-tuple-element.48), channel_id=1, source_target_pairs={{0,1},{1,0},{2,3},{3,2},{4,5},{5,4},{6,7},{7,6},{8,9},{9,8},{10,11... | collective-permute-start | bytes 2217992 | tf_op jit(solution)/shard_map/ppermute | solution.py:112
  421.8 13.2 %collective-permute-start.19 = (bf16[192,608]{1,0:T(8,128)(2,1)S(1)}, bf16[192,608]{1,0:T(8,128)(2,1)S(1)}, u32[]{:S(2)}, u32[]{:S(2)}) collective-permute-start(bf16[192,608]{1,0:T(8,128)(2,1)S(1)} %get-tuple-element.179), channel_id=1, source_target_pairs={{0,4},{4,0},{8,12},{12,8},{1,5},{5,1},{9,13},{13,9},{2,6},{6,2},{1... | collective-permute-start | bytes 700424 | tf_op jit(solution)/shard_map/ppermute | solution.py:22
  584.2 13.9 %collective-permute-start.60 = (bf16[60,2432]{1,0:T(8,128)(2,1)}, bf16[60,2432]{1,0:T(8,128)(2,1)}, u32[]{:S(2)}, u32[]{:S(2)}) collective-permute-start(bf16[60,2432]{1,0:T(8,128)(2,1)} %get-tuple-element.77), channel_id=1, source_target_pairs={{0,2},{1,3},{2,0},{3,1},{4,6},{5,7},{6,4},{7,5},{8,10},{9,11},{10,... | collective-permute-start | bytes 875528 | tf_op jit(solution)/shard_map/ppermute | solution.py:22
  584.2 13.9 %collective-permute-start.59 = (bf16[60,2432]{1,0:T(8,128)(2,1)}, bf16[60,2432]{1,0:T(8,128)(2,1)}, u32[]{:S(2)}, u32[]{:S(2)}) collective-permute-start(bf16[60,2432]{1,0:T(8,128)(2,1)} %get-tuple-element.78), channel_id=1, source_target_pairs={{0,1},{1,0},{2,3},{3,2},{4,5},{5,4},{6,7},{7,6},{8,9},{9,8},{10,11... | collective-permute-start | bytes 875528 | tf_op jit(solution)/shard_map/ppermute | solution.py:22
  698.4 62.4 %collective-permute-start.77 = (bf16[192,608]{1,0:T(8,128)(2,1)S(1)}, bf16[192,608]{1,0:T(8,128)(2,1)S(1)}, u32[]{:S(2)}, u32[]{:S(2)}) collective-permute-start(bf16[192,608]{1,0:T(8,128)(2,1)S(1)} %fusion.149), channel_id=1, source_target_pairs={{16,0},{17,1},{18,2},{19,3},{20,4},{21,5},{22,6},{23,7},{24,8},{25... | collective-permute-start | bytes 700424 | tf_op jit(solution)/shard_map/ppermute | solution.py:243
  (214 other events, 2694.7 us)

commit v5 on v2

--- a/solution.py
+++ b/solution.py
@@ -209,13 +209,11 @@
                 pairs = xor_pairs(n_dp, d, live * n_dp)
                 pieces.append(lax.ppermute(block, ("section", "dp"), pairs))
                 terms.append(lax.ppermute(row_term[None, :], ("section", "dp"), pairs))
-            ordered = jnp.stack(pieces).astype(jnp.float32)
-            term_rows = jnp.concatenate(terms, axis=0)
             input_grad = jnp.zeros((row_count, col_width), jnp.float32)
             row_sum = jnp.zeros((row_count,), jnp.float32)
             for src in range(n_dp):
-                input_grad = input_grad + ordered[src]
-                row_sum = row_sum + term_rows[src]
+                input_grad = input_grad + pieces[src].astype(jnp.float32)
+                row_sum = row_sum + terms[src][0]
             row_mean = (row_sum / width)[:, None]
             grad_stream = grad_stream + inverse * (
                 input_grad * my_cols(scaled) - my_cols(normed) * row_mean

time: 744 us -> 737 us (level)
    unnamed x229 -> x233, local copies, waits for them, and re-layouts: 17 us -> 12.4 us
  transfers between devices with their start and end apart: 108 -> 108, of which waited for: 28 -> 29; matrix products, arithmetic and copies ran while one was open for 13% -> 13% of each run, Pallas kernels for 0% -> 0%
where the time goes in v5:
time: 737 us; the launch traced here: 726 us
  waiting for transfers between devices  278 us (38%)
  starting transfers between devices  190 us (26%)
  local copies, waits for them, and re-layouts  109 us (15%)
  matrix products  75.8 us (10%)
  other arithmetic  50.9 us (7%)
  between operations  23.3 us (3%)
    all_gather x4, waiting for transfers between devices, on_device(): lax.all_gather(teacher_weight[0, slot_no], 'mp', axis=0, tiled=True)  127 us
    ppermute x1, waiting for transfers between devices, on_device(): lax.ppermute(grad_stream.astype(jnp.bfloat16), 'section', [(live, live -...  90.7 us
    ppermute x50, starting transfers between devices, swap(): return lax.ppermute(x, axis, xor_pairs(n, d, base))  84.7 us
    ppermute x24, starting transfers between devices, on_device(): pieces.append(lax.ppermute(block, ('section', 'dp'), pairs))  45.5 us
    ppermute x24, starting transfers between devices, on_device(): terms.append(lax.ppermute(row_term[None, :], ('section', 'dp'), pairs))  45.4 us
    ppermute x50, waiting for transfers between devices, swap(): return lax.ppermute(x, axis, xor_pairs(n, d, base))  41.4 us
    dot_general x8, matrix products, on_device(): jnp.dot(normed_in, weights[slot_no], preferred_element_type=jnp.float32)  34.5 us
    dot_general x8, matrix products, on_device(): jnp.dot(pre_grad, weights[slot_no].T, preferred_element_type=jnp.float32)  26.6 us
  transfers between devices with their start and end apart: 108, of which 29 were waited for; matrix products, arithmetic and copies ran while one was open for 13% of the time, Pallas kernels for 0%

profile of v5, /device:TPU:0, one launch (start us, length us, event | category | flops | bytes accessed | tf_op | source)
XLA Modules:
  0.0 725.9 jit_solution(7359330931269782189)
XLA Ops:
  7.2 3.6 fusion.362
  22.1 6.2 broadcast_in_dim.190
  28.3 11.7 %fusion.361 = (f32[4,192,1,2432]{3,1,2,0:T(8,128)}, f32[4,192,1,2432]{3,1,2,0:T(8,128)}) fusion(f32[4,192,2,2432]{3,1,2,0:T(8,128)} %bitcast.338), kind=kLoop, calls=%fused_computation.584 | loop fusion | bytes 29884416 | tf_op jit(solution)/shard_map/slice | solution.py:117
  40.2 8.3 %dynamic-slice_bitcast_fusion = (f32[4,192,608]{2,1,0:T(8,128)S(1)}, f32[4,192,608]{2,1,0:T(8,128)}, f32[4,192,608]{2,1,0:T(8,128)}, f32[4,192,608]{2,1,0:T(8,128)}) fusion(f32[4,192,1,2432]{3,1,2,0:T(8,128)} %get-tuple-element.9, s32[]{:T(128)S(6)} %select_n.373, s32[]{:T(128)S(6)} %select_n.372, s32[]{:T(128)S(6)} %select_n.371, s32[]{:T(128)S(6)} %select_n.370), kind=kLoop, calls=%fused_computation.35 | loop fusion | bytes 14942224 | tf_op jit(solution)/shard_map/dynamic_slice | solution.py:34
  50.3 9.2 %concatenate.53 = f32[4,192,2432]{2,1,0:T(8,128)} concatenate(f32[4,192,608]{2,1,0:T(8,128)} %get-tuple-element.17, f32[4,192,608]{2,1,0:T(8,128)} %get-tuple-element.16, f32[4,192,608]{2,1,0:T(8,128)} %get-tuple-element.15, f32[4,192,608]{2,1,0:T(8,128)S(1)} %get-tuple-element.14), dimensions={2} | concatenate | bytes 14942208 | tf_op jit(solution)/shard_map/concatenate | solution.py:33
  73.6 4.7 collective-permute-done.8
  87.5 4.3 multiply_convert_fusion.23
  101.6 46.4 %all-gather.11.cloned.1.call-done = bf16[1,1,2432,608]{3,2,1,0:T(8,128)(2,1)} async-done(((bf16[1,1,608,608]{3,2,1,0:T(8,128)(2,1)}), bf16[1,1,2432,608]{3,2,1,0:T(8,128)(2,1)}) %all-gather.11.cloned.1.call-update) | async-done | bytes 2957328 | tf_op jit(solution)/shard_map/all_gather | solution.py:109
  158.2 4.1 multiply_convert_fusion.22
  171.5 39.7 %all-gather.13.cloned.1.call-done = bf16[1,1,2432,608]{3,2,1,0:T(8,128)(2,1)} async-done(((bf16[1,1,608,608]{3,2,1,0:T(8,128)(2,1)}), bf16[1,1,2432,608]{3,2,1,0:T(8,128)(2,1)}) %all-gather.13.cloned.1.call-update) | async-done | bytes 2957328 | tf_op jit(solution)/shard_map/all_gather | solution.py:109
  211.2 3.6 dynamic-slice_bitcast_fusion.11
  222.5 4.1 multiply_convert_fusion.21
  235.8 38.4 %all-gather.15.cloned.1.call-done = bf16[1,1,2432,608]{3,2,1,0:T(8,128)(2,1)} async-done(((bf16[1,1,608,608]{3,2,1,0:T(8,128)(2,1)}), bf16[1,1,2432,608]{3,2,1,0:T(8,128)(2,1)}) %all-gather.15.cloned.1.call-update) | async-done | bytes 2957328 | tf_op jit(solution)/shard_map/all_gather | solution.py:109
  274.3 3.5 dynamic-slice_bitcast_fusion.7
  285.2 4.1 multiply_convert_fusion.20
  300.8 4.3 collective-permute-done.21
  315.9 5.4 multiply_convert_fusion.19
  330.8 4.1 multiply_convert_fusion.18
  349.3 4.1 multiply_convert_fusion.17
  364.1 4.1 multiply_convert_fusion.16
  380.4 7.0 convolution_convert_fusion
  398.1 3.9 collective-permute-done.35
  402.1 4.7 collective-permute-done.36
  418.1 4.0 collective-permute-start.38
  424.6 3.7 collective-permute-done.39
  431.7 4.6 convolution_convert_fusion.8
  474.5 90.7 %collective-permute-done.65 = bf16[192,608]{1,0:T(8,128)(2,1)S(1)} collective-permute-done((bf16[192,608]{1,0:T(8,128)(2,1)S(1)}, bf16[192,608]{1,0:T(8,128)(2,1)S(1)}, u32[]{:S(2)}, u32[]{:S(2)}) %collective-permute-start.65) | collective-permute-done | bytes 233504 | tf_op jit(solution)/shard_map/ppermute | solution.py:222
  573.7 4.4 collective-permute-start.68
  584.2 3.8 collective-permute-start.71
  627.4 3.8 collective-permute-start.80
  637.2 3.8 collective-permute-start.83
  678.1 3.8 collective-permute-start.92
  (613 shorter events, 350.4 us)
Async XLA Ops:
  7.2 77.9 %all-gather.9.cloned.1.call-start = ((), (), s32[]{:S(2)}) async-start(), calls=%async_computation | async-start | bytes 3891200 | tf_op jit(solution)/shard_map/all_gather | solution.py:109
  10.9 137.1 %all-gather.11.cloned.1.call-start = ((), (), s32[]{:S(2)}) async-start(), calls=%async_computation.1 | async-start | bytes 3891200 | tf_op jit(solution)/shard_map/all_gather | solution.py:109
  11.6 199.5 %all-gather.13.cloned.1.call-start = ((), (), s32[]{:S(2)}) async-start(), calls=%async_computation.2 | async-start | bytes 3891200 | tf_op jit(solution)/shard_map/all_gather | solution.py:109
  12.4 261.9 %all-gather.15.cloned.1.call-start = ((), (), s32[]{:S(2)}) async-start(), calls=%async_computation.3 | async-start | bytes 3891200 | tf_op jit(solution)/shard_map/all_gather | solution.py:109
  13.0 46.4 %collective-permute-start = (bf16[304,16]{0,1:T(8,128)(2,1)}, bf16[304,16]{0,1:T(8,128)(2,1)}, u32[]{:S(2)}, u32[]{:S(2)}) collective-permute-start(bf16[304,16]{0,1:T(8,128)(2,1)} %convert_element_type.345), channel_id=1, source_target_pairs={{0,4},{4,0},{8,12},{12,8},{1,5},{5,1},{9,13},{13,9},{2,6},{6,2},{1... | collective-permute-start | bytes 29192 | tf_op jit(solution)/shard_map/ppermute | solution.py:22
  16.0 43.5 %collective-permute-start.1 = (bf16[304,16]{0,1:T(8,128)(2,1)}, bf16[304,16]{0,1:T(8,128)(2,1)}, u32[]{:S(2)}, u32[]{:S(2)}) collective-permute-start(bf16[304,16]{0,1:T(8,128)(2,1)} %convert_element_type.345), channel_id=1, source_target_pairs={{0,8},{4,12},{8,0},{12,4},{1,9},{5,13},{9,1},{13,5},{2,10},{6,14},... | collective-permute-start | bytes 29192 | tf_op jit(solution)/shard_map/ppermute | solution.py:22
  17.5 42.0 %collective-permute-start.2 = (bf16[304,16]{0,1:T(8,128)(2,1)}, bf16[304,16]{0,1:T(8,128)(2,1)}, u32[]{:S(2)}, u32[]{:S(2)}) collective-permute-start(bf16[304,16]{0,1:T(8,128)(2,1)} %convert_element_type.345), channel_id=1, source_target_pairs={{0,12},{4,8},{8,4},{12,0},{1,13},{5,9},{9,5},{13,1},{2,14},{6,10},... | collective-permute-start | bytes 29192 | tf_op jit(solution)/shard_map/ppermute | solution.py:22
  67.7 10.5 %collective-permute-start.8 = (bf16[304,64]{0,1:T(8,128)(2,1)S(1)}, bf16[304,64]{0,1:T(8,128)(2,1)S(1)}, u32[]{:S(2)}, u32[]{:S(2)}) collective-permute-start(bf16[304,64]{0,1:T(8,128)(2,1)S(1)} %pad_maximum_fusion.12), channel_id=1, source_target_pairs={{0,18},{1,19},{2,16},{3,17},{16,2},{17,3},{18,0},{19,1},{4,22},{5,... | collective-permute-start | bytes 116744 | tf_op jit(solution)/shard_map/ppermute | solution.py:22
  91.9 59.6 %collective-permute-start.10 = (bf16[192,608]{1,0:T(8,128)(2,1)S(1)}, bf16[192,608]{1,0:T(8,128)(2,1)S(1)}, u32[]{:S(2)}, u32[]{:S(2)}) collective-permute-start(bf16[192,608]{1,0:T(8,128)(2,1)S(1)} %get-tuple-element.100), channel_id=1, source_target_pairs={{0,4},{4,0},{8,12},{12,8},{1,5},{5,1},{9,13},{13,9},{2,6},{6,2},{1... | collective-permute-start | bytes 700424 | tf_op jit(solution)/shard_map/ppermute | solution.py:22
  95.2 56.2 %collective-permute-start.11 = (bf16[192,608]{1,0:T(8,128)(2,1)S(1)}, bf16[192,608]{1,0:T(8,128)(2,1)S(1)}, u32[]{:S(2)}, u32[]{:S(2)}) collective-permute-start(bf16[192,608]{1,0:T(8,128)(2,1)S(1)} %get-tuple-element.100), channel_id=1, source_target_pairs={{0,8},{4,12},{8,0},{12,4},{1,9},{5,13},{9,1},{13,5},{2,10},{6,14},... | collective-permute-start | bytes 700424 | tf_op jit(solution)/shard_map/ppermute | solution.py:22
  98.6 52.9 %collective-permute-start.12 = (bf16[192,608]{1,0:T(8,128)(2,1)S(1)}, bf16[192,608]{1,0:T(8,128)(2,1)}, u32[]{:S(2)}, u32[]{:S(2)}) collective-permute-start(bf16[192,608]{1,0:T(8,128)(2,1)S(1)} %get-tuple-element.100), channel_id=1, source_target_pairs={{0,12},{4,8},{8,4},{12,0},{1,13},{5,9},{9,5},{13,1},{2,14},{6,10},... | collective-permute-start | bytes 700424 | tf_op jit(solution)/shard_map/ppermute | solution.py:22
  162.3 52.5 %collective-permute-start.13 = (bf16[192,608]{1,0:T(8,128)(2,1)S(1)}, bf16[192,608]{1,0:T(8,128)(2,1)S(1)}, u32[]{:S(2)}, u32[]{:S(2)}) collective-permute-start(bf16[192,608]{1,0:T(8,128)(2,1)S(1)} %get-tuple-element.102), channel_id=1, source_target_pairs={{0,4},{4,0},{8,12},{12,8},{1,5},{5,1},{9,13},{13,9},{2,6},{6,2},{1... | collective-permute-start | bytes 700424 | tf_op jit(solution)/shard_map/ppermute | solution.py:22
  165.7 49.1 %collective-permute-start.14 = (bf16[192,608]{1,0:T(8,128)(2,1)S(1)}, bf16[192,608]{1,0:T(8,128)(2,1)S(1)}, u32[]{:S(2)}, u32[]{:S(2)}) collective-permute-start(bf16[192,608]{1,0:T(8,128)(2,1)S(1)} %get-tuple-element.102), channel_id=1, source_target_pairs={{0,8},{4,12},{8,0},{12,4},{1,9},{5,13},{9,1},{13,5},{2,10},{6,14},... | collective-permute-start | bytes 700424 | tf_op jit(solution)/shard_map/ppermute | solution.py:22
  169.1 45.7 %collective-permute-start.15 = (bf16[192,608]{1,0:T(8,128)(2,1)S(1)}, bf16[192,608]{1,0:T(8,128)(2,1)}, u32[]{:S(2)}, u32[]{:S(2)}) collective-permute-start(bf16[192,608]{1,0:T(8,128)(2,1)S(1)} %get-tuple-element.102), channel_id=1, source_target_pairs={{0,12},{4,8},{8,4},{12,0},{1,13},{5,9},{9,5},{13,1},{2,14},{6,10},... | collective-permute-start | bytes 700424 | tf_op jit(solution)/shard_map/ppermute | solution.py:22
  226.6 51.2 %collective-permute-start.16 = (bf16[192,608]{1,0:T(8,128)(2,1)S(1)}, bf16[192,608]{1,0:T(8,128)(2,1)S(1)}, u32[]{:S(2)}, u32[]{:S(2)}) collective-permute-start(bf16[192,608]{1,0:T(8,128)(2,1)S(1)} %get-tuple-element.104), channel_id=1, source_target_pairs={{0,4},{4,0},{8,12},{12,8},{1,5},{5,1},{9,13},{13,9},{2,6},{6,2},{1... | collective-permute-start | bytes 700424 | tf_op jit(solution)/shard_map/ppermute | solution.py:22
  230.0 47.8 %collective-permute-start.17 = (bf16[192,608]{1,0:T(8,128)(2,1)S(1)}, bf16[192,608]{1,0:T(8,128)(2,1)S(1)}, u32[]{:S(2)}, u32[]{:S(2)}) collective-permute-start(bf16[192,608]{1,0:T(8,128)(2,1)S(1)} %get-tuple-element.104), channel_id=1, source_target_pairs={{0,8},{4,12},{8,0},{12,4},{1,9},{5,13},{9,1},{13,5},{2,10},{6,14},... | collective-permute-start | bytes 700424 | tf_op jit(solution)/shard_map/ppermute | solution.py:22
  233.4 44.5 %collective-permute-start.18 = (bf16[192,608]{1,0:T(8,128)(2,1)S(1)}, bf16[192,608]{1,0:T(8,128)(2,1)}, u32[]{:S(2)}, u32[]{:S(2)}) collective-permute-start(bf16[192,608]{1,0:T(8,128)(2,1)S(1)} %get-tuple-element.104), channel_id=1, source_target_pairs={{0,12},{4,8},{8,4},{12,0},{1,13},{5,9},{9,5},{13,1},{2,14},{6,10},... | collective-permute-start | bytes 700424 | tf_op jit(solution)/shard_map/ppermute | solution.py:22
  392.0 14.8 %collective-permute-start.36 = (bf16[60,2432]{1,0:T(8,128)(2,1)}, bf16[60,2432]{1,0:T(8,128)(2,1)}, u32[]{:S(2)}, u32[]{:S(2)}) collective-permute-start(bf16[60,2432]{1,0:T(8,128)(2,1)} %get-tuple-element.48), channel_id=1, source_target_pairs={{0,2},{1,3},{2,0},{3,1},{4,6},{5,7},{6,4},{7,5},{8,10},{9,11},{10,... | collective-permute-start | bytes 875528 | tf_op jit(solution)/shard_map/ppermute | solution.py:22
  393.5 13.3 %collective-permute-start.37 = (bf16[60,2432]{1,0:T(8,128)(2,1)}, bf16[60,2432]{1,0:T(8,128)(2,1)}, u32[]{:S(2)}, u32[]{:S(2)}) collective-permute-start(bf16[60,2432]{1,0:T(8,128)(2,1)} %get-tuple-element.47), channel_id=1, source_target_pairs={{0,3},{1,2},{2,1},{3,0},{4,7},{5,6},{6,5},{7,4},{8,11},{9,10},{10,... | collective-permute-start | bytes 875528 | tf_op jit(solution)/shard_map/ppermute | solution.py:22
  473.2 92.0 %collective-permute-start.65 = (bf16[192,608]{1,0:T(8,128)(2,1)S(1)}, bf16[192,608]{1,0:T(8,128)(2,1)S(1)}, u32[]{:S(2)}, u32[]{:S(2)}) collective-permute-start(bf16[192,608]{1,0:T(8,128)(2,1)S(1)} %fusion.141), channel_id=1, source_target_pairs={{16,0},{17,1},{18,2},{19,3},{20,4},{21,5},{22,6},{23,7},{24,8},{25... | collective-permute-start | bytes 700424 | tf_op jit(solution)/shard_map/ppermute | solution.py:222
  568.8 21.7 %collective-permute-start.66 = (bf16[192,608]{1,0:T(8,128)(2,1)S(1)}, bf16[192,608]{1,0:T(8,128)(2,1)S(1)}, u32[]{:S(2)}, u32[]{:S(2)}) collective-permute-start(bf16[192,608]{1,0:T(8,128)(2,1)S(1)} %get-tuple-element.61), channel_id=1, source_target_pairs={{0,4},{4,0},{8,12},{12,8},{1,5},{5,1},{9,13},{13,9},{2,6},{6,2},{1... | collective-permute-start | bytes 700424 | tf_op jit(solution)/shard_map/ppermute | solution.py:210
  571.3 19.2 %collective-permute-start.67 = (bf16[192,608]{1,0:T(8,128)(2,1)S(1)}, bf16[192,608]{1,0:T(8,128)(2,1)S(1)}, u32[]{:S(2)}, u32[]{:S(2)}) collective-permute-start(bf16[192,608]{1,0:T(8,128)(2,1)S(1)} %get-tuple-element.63), channel_id=1, source_target_pairs={{0,8},{4,12},{8,0},{12,4},{1,9},{5,13},{9,1},{13,5},{2,10},{6,14},... | collective-permute-start | bytes 700424 | tf_op jit(solution)/shard_map/ppermute | solution.py:210
  573.7 16.9 %collective-permute-start.68 = (bf16[192,608]{1,0:T(8,128)(2,1)S(1)}, bf16[192,608]{1,0:T(8,128)(2,1)S(1)}, u32[]{:S(2)}, u32[]{:S(2)}) collective-permute-start(bf16[192,608]{1,0:T(8,128)(2,1)S(1)} %get-tuple-element.62), channel_id=1, source_target_pairs={{0,12},{4,8},{8,4},{12,0},{1,13},{5,9},{9,5},{13,1},{2,14},{6,10},... | collective-permute-start | bytes 700424 | tf_op jit(solution)/shard_map/ppermute | solution.py:210
  594.5 22.6 %collective-permute-start.72 = (bf16[192,608]{1,0:T(8,128)(2,1)S(1)}, bf16[192,608]{1,0:T(8,128)(2,1)S(1)}, u32[]{:S(2)}, u32[]{:S(2)}) collective-permute-start(bf16[192,608]{1,0:T(8,128)(2,1)S(1)} %get-tuple-element.58), channel_id=1, source_target_pairs={{0,4},{4,0},{8,12},{12,8},{1,5},{5,1},{9,13},{13,9},{2,6},{6,2},{1... | collective-permute-start | bytes 700424 | tf_op jit(solution)/shard_map/ppermute | solution.py:210
  597.3 19.8 %collective-permute-start.73 = (bf16[192,608]{1,0:T(8,128)(2,1)S(1)}, bf16[192,608]{1,0:T(8,128)(2,1)S(1)}, u32[]{:S(2)}, u32[]{:S(2)}) collective-permute-start(bf16[192,608]{1,0:T(8,128)(2,1)S(1)} %get-tuple-element.60), channel_id=1, source_target_pairs={{0,8},{4,12},{8,0},{12,4},{1,9},{5,13},{9,1},{13,5},{2,10},{6,14},... | collective-permute-start | bytes 700424 | tf_op jit(solution)/shard_map/ppermute | solution.py:210
  600.7 16.4 %collective-permute-start.74 = (bf16[192,608]{1,0:T(8,128)(2,1)S(1)}, bf16[192,608]{1,0:T(8,128)(2,1)S(1)}, u32[]{:S(2)}, u32[]{:S(2)}) collective-permute-start(bf16[192,608]{1,0:T(8,128)(2,1)S(1)} %get-tuple-element.59), channel_id=1, source_target_pairs={{0,12},{4,8},{8,4},{12,0},{1,13},{5,9},{9,5},{13,1},{2,14},{6,10},... | collective-permute-start | bytes 700424 | tf_op jit(solution)/shard_map/ppermute | solution.py:210
  621.9 21.6 %collective-permute-start.78 = (bf16[192,608]{1,0:T(8,128)(2,1)S(1)}, bf16[192,608]{1,0:T(8,128)(2,1)S(1)}, u32[]{:S(2)}, u32[]{:S(2)}) collective-permute-start(bf16[192,608]{1,0:T(8,128)(2,1)S(1)} %get-tuple-element.55), channel_id=1, source_target_pairs={{0,4},{4,0},{8,12},{12,8},{1,5},{5,1},{9,13},{13,9},{2,6},{6,2},{1... | collective-permute-start | bytes 700424 | tf_op jit(solution)/shard_map/ppermute | solution.py:210
  624.4 19.1 %collective-permute-start.79 = (bf16[192,608]{1,0:T(8,128)(2,1)S(1)}, bf16[192,608]{1,0:T(8,128)(2,1)S(1)}, u32[]{:S(2)}, u32[]{:S(2)}) collective-permute-start(bf16[192,608]{1,0:T(8,128)(2,1)S(1)} %get-tuple-element.57), channel_id=1, source_target_pairs={{0,8},{4,12},{8,0},{12,4},{1,9},{5,13},{9,1},{13,5},{2,10},{6,14},... | collective-permute-start | bytes 700424 | tf_op jit(solution)/shard_map/ppermute | solution.py:210
  627.4 16.2 %collective-permute-start.80 = (bf16[192,608]{1,0:T(8,128)(2,1)S(1)}, bf16[192,608]{1,0:T(8,128)(2,1)S(1)}, u32[]{:S(2)}, u32[]{:S(2)}) collective-permute-start(bf16[192,608]{1,0:T(8,128)(2,1)S(1)} %get-tuple-element.56), channel_id=1, source_target_pairs={{0,12},{4,8},{8,4},{12,0},{1,13},{5,9},{9,5},{13,1},{2,14},{6,10},... | collective-permute-start | bytes 700424 | tf_op jit(solution)/shard_map/ppermute | solution.py:210
  648.1 22.5 %collective-permute-start.84 = (bf16[192,608]{1,0:T(8,128)(2,1)}, bf16[192,608]{1,0:T(8,128)(2,1)}, u32[]{:S(2)}, u32[]{:S(2)}) collective-permute-start(bf16[192,608]{1,0:T(8,128)(2,1)} %get-tuple-element.52), channel_id=1, source_target_pairs={{0,4},{4,0},{8,12},{12,8},{1,5},{5,1},{9,13},{13,9},{2,6},{6,2},{1... | collective-permute-start | bytes 700424 | tf_op jit(solution)/shard_map/ppermute | solution.py:210
  651.0 19.6 %collective-permute-start.85 = (bf16[192,608]{1,0:T(8,128)(2,1)}, bf16[192,608]{1,0:T(8,128)(2,1)}, u32[]{:S(2)}, u32[]{:S(2)}) collective-permute-start(bf16[192,608]{1,0:T(8,128)(2,1)} %get-tuple-element.54), channel_id=1, source_target_pairs={{0,8},{4,12},{8,0},{12,4},{1,9},{5,13},{9,1},{13,5},{2,10},{6,14},... | collective-permute-start | bytes 700424 | tf_op jit(solution)/shard_map/ppermute | solution.py:210
  654.4 16.3 %collective-permute-start.86 = (bf16[192,608]{1,0:T(8,128)(2,1)}, bf16[192,608]{1,0:T(8,128)(2,1)}, u32[]{:S(2)}, u32[]{:S(2)}) collective-permute-start(bf16[192,608]{1,0:T(8,128)(2,1)} %get-tuple-element.53), channel_id=1, source_target_pairs={{0,12},{4,8},{8,4},{12,0},{1,13},{5,9},{9,5},{13,1},{2,14},{6,10},... | collective-permute-start | bytes 700424 | tf_op jit(solution)/shard_map/ppermute | solution.py:210
  (187 other events, 1628.2 us)
Sparse Core Ops, SparseCore 0:
  11.0 73.9 all-gather.8
  86.6 61.3 all-gather.10
  149.5 61.6 all-gather.12
  212.6 61.6 all-gather.14

commit v6 on v5

--- a/solution.py
+++ b/solution.py
@@ -160,15 +160,13 @@
     dispatch = (
         target[:, None] == jnp.arange(n_mp * capacity, dtype=jnp.int32)[None, :]
     ).astype(jnp.bfloat16)
+    dispatch = relative_blocks(dispatch, 1, n_mp, me_mp)
     send_feat = (
         jnp.dot(dispatch.T, tap_store, preferred_element_type=jnp.float32)
         .astype(jnp.bfloat16)
         .reshape(n_mp, capacity, width)
     )
-    items = [lax.dynamic_index_in_dim(send_feat, me_mp, 0, keepdims=False)]
-    for d in range(1, n_mp):
-        outgoing = lax.dynamic_index_in_dim(send_feat, me_mp ^ d, 0, keepdims=False)
-        items.append(swap(outgoing, "mp", n_mp, d))
+    items = [send_feat[0]] + [swap(send_feat[d], "mp", n_mp, d) for d in range(1, n_mp)]
     loss_scale = width / math.sqrt(row_count * n_mp)
     w_first = relative_blocks(
         lax.dynamic_index_in_dim(head_in[:, 0], sec, 0, keepdims=False), 0, n_dp, me_dp
@@ -179,9 +177,8 @@
     ).reshape(n_mp, capacity, width)
     head_cols = head_result[:, :, :col_width]
     back = [head_cols[0]] + [swap(head_cols[d], "mp", n_mp, d) for d in range(1, n_mp)]
-    by_owner = jnp.take(jnp.stack(back), me_mp ^ owner_range, axis=0)
     tap_grads = jnp.dot(
-        dispatch, by_owner.reshape(n_mp * capacity, col_width), preferred_element_type=jnp.float32
+        dispatch, jnp.concatenate(back, axis=0), preferred_element_type=jnp.float32
     )
 
     my_cols = lambda x: x[..., :col_width]

time: 737 us -> 730 us (level)
    dynamic_slice x7 -> x8, local copies, waits for them, and re-layouts: 22.9 us -> 23.7 us  [relative_blocks(): lax.dynamic_slice_in_dim(x, (me ^ d) * width, width, axis)]
  transfers between devices with their start and end apart: 108 -> 108, of which waited for: 29 -> 30; matrix products, arithmetic and copies ran while one was open for 13% -> 13% of each run, Pallas kernels for 0% -> 0%
where the time goes in v6:
time: 730 us; the launch traced here: 720 us
  waiting for transfers between devices  277 us (38%)
  starting transfers between devices  190 us (26%)
  local copies, waits for them, and re-layouts  104 us (14%)
  matrix products  74.5 us (10%)
  other arithmetic  50.1 us (7%)
  between operations  23.5 us (3%)
    all_gather x4, waiting for transfers between devices, on_device(): lax.all_gather(teacher_weight[0, slot_no], 'mp', axis=0, tiled=True)  127 us
    ppermute x1, waiting for transfers between devices, on_device(): lax.ppermute(grad_stream.astype(jnp.bfloat16), 'section', [(live, live -...  89.4 us
    ppermute x50, starting transfers between devices, swap(): return lax.ppermute(x, axis, xor_pairs(n, d, base))  85 us
    ppermute x24, starting transfers between devices, on_device(): terms.append(lax.ppermute(row_term[None, :], ('section', 'dp'), pairs))  45.8 us
    ppermute x24, starting transfers between devices, on_device(): pieces.append(lax.ppermute(block, ('section', 'dp'), pairs))  45 us
    ppermute x50, waiting for transfers between devices, swap(): return lax.ppermute(x, axis, xor_pairs(n, d, base))  42.4 us
    dot_general x8, matrix products, on_device(): jnp.dot(normed_in, weights[slot_no], preferred_element_type=jnp.float32)  34.6 us
    dot_general x8, matrix products, on_device(): jnp.dot(pre_grad, weights[slot_no].T, preferred_element_type=jnp.float32)  26.5 us
  transfers between devices with their start and end apart: 108, of which 30 were waited for; matrix products, arithmetic and copies ran while one was open for 13% of the time, Pallas kernels for 0%

profile of v6, /device:TPU:0, one launch (start us, length us, event | category | flops | bytes accessed | tf_op | source)
XLA Modules:
  0.0 719.5 jit_solution(4755565109099411594)
XLA Ops:
  7.2 3.6 fusion.365
  22.0 6.2 broadcast_in_dim.173
  28.2 11.7 %fusion.364 = (f32[4,192,1,2432]{3,1,2,0:T(8,128)}, f32[4,192,1,2432]{3,1,2,0:T(8,128)}) fusion(f32[4,192,2,2432]{3,1,2,0:T(8,128)} %bitcast.329), kind=kLoop, calls=%fused_computation.587 | loop fusion | bytes 29884416 | tf_op jit(solution)/shard_map/slice | solution.py:117
  40.2 8.3 %dynamic-slice_bitcast_fusion = (f32[4,192,608]{2,1,0:T(8,128)S(1)}, f32[4,192,608]{2,1,0:T(8,128)}, f32[4,192,608]{2,1,0:T(8,128)}, f32[4,192,608]{2,1,0:T(8,128)}) fusion(f32[4,192,1,2432]{3,1,2,0:T(8,128)} %get-tuple-element.9, s32[]{:T(128)S(6)} %select_n.377, s32[]{:T(128)S(6)} %select_n.376, s32[]{:T(128)S(6)} %select_n.375, s32[]{:T(128)S(6)} %select_n.374), kind=kLoop, calls=%fused_computation.34 | loop fusion | bytes 14942224 | tf_op jit(solution)/shard_map/dynamic_slice | solution.py:34
  50.2 9.2 %concatenate.60 = f32[4,192,2432]{2,1,0:T(8,128)} concatenate(f32[4,192,608]{2,1,0:T(8,128)} %get-tuple-element.17, f32[4,192,608]{2,1,0:T(8,128)} %get-tuple-element.16, f32[4,192,608]{2,1,0:T(8,128)} %get-tuple-element.15, f32[4,192,608]{2,1,0:T(8,128)S(1)} %get-tuple-element.14), dimensions={2} | concatenate | bytes 14942208 | tf_op jit(solution)/shard_map/concatenate | solution.py:33
  73.5 4.8 collective-permute-done.8
  87.4 4.4 multiply_convert_fusion.23
  101.3 46.6 %all-gather.11.cloned.1.call-done = bf16[1,1,2432,608]{3,2,1,0:T(8,128)(2,1)} async-done(((bf16[1,1,608,608]{3,2,1,0:T(8,128)(2,1)}), bf16[1,1,2432,608]{3,2,1,0:T(8,128)(2,1)}) %all-gather.11.cloned.1.call-update) | async-done | bytes 2957328 | tf_op jit(solution)/shard_map/all_gather | solution.py:109
  147.9 3.6 dynamic-slice_bitcast_fusion.15
  158.2 4.1 multiply_convert_fusion.22
  171.6 39.6 %all-gather.13.cloned.1.call-done = bf16[1,1,2432,608]{3,2,1,0:T(8,128)(2,1)} async-done(((bf16[1,1,608,608]{3,2,1,0:T(8,128)(2,1)}), bf16[1,1,2432,608]{3,2,1,0:T(8,128)(2,1)}) %all-gather.13.cloned.1.call-update) | async-done | bytes 2957328 | tf_op jit(solution)/shard_map/all_gather | solution.py:109
  222.3 4.2 multiply_convert_fusion.21
  235.8 38.5 %all-gather.15.cloned.1.call-done = bf16[1,1,2432,608]{3,2,1,0:T(8,128)(2,1)} async-done(((bf16[1,1,608,608]{3,2,1,0:T(8,128)(2,1)}), bf16[1,1,2432,608]{3,2,1,0:T(8,128)(2,1)}) %all-gather.15.cloned.1.call-update) | async-done | bytes 2957328 | tf_op jit(solution)/shard_map/all_gather | solution.py:109
  274.2 3.6 dynamic-slice_bitcast_fusion.7
  285.2 4.0 multiply_convert_fusion.20
  300.7 4.4 collective-permute-done.21
  315.8 5.3 multiply_convert_fusion.19
  335.3 4.2 multiply_convert_fusion.18
  349.7 4.2 multiply_convert_fusion.17
  370.3 4.1 multiply_convert_fusion.16
  380.6 6.1 convolution_convert_fusion
  393.7 4.1 collective-permute-done.35
  397.8 4.7 collective-permute-done.36
  413.9 4.0 collective-permute-start.38
  420.5 4.0 collective-permute-done.39
  427.6 4.5 convolution_convert_fusion.8
  470.2 89.4 %collective-permute-done.65 = bf16[192,608]{1,0:T(8,128)(2,1)S(1)} collective-permute-done((bf16[192,608]{1,0:T(8,128)(2,1)S(1)}, bf16[192,608]{1,0:T(8,128)(2,1)S(1)}, u32[]{:S(2)}, u32[]{:S(2)}) %collective-permute-start.65) | collective-permute-done | bytes 233504 | tf_op jit(solution)/shard_map/ppermute | solution.py:219
  568.1 4.2 collective-permute-start.68
  578.5 3.8 collective-permute-start.71
  621.6 3.8 collective-permute-start.80
  631.4 3.8 collective-permute-start.83
  671.4 3.8 collective-permute-start.92
  (619 shorter events, 345.3 us)
Async XLA Ops:
  7.2 77.8 %all-gather.9.cloned.1.call-start = ((), (), s32[]{:S(2)}) async-start(), calls=%async_computation | async-start | bytes 3891200 | tf_op jit(solution)/shard_map/all_gather | solution.py:109
  10.8 137.1 %all-gather.11.cloned.1.call-start = ((), (), s32[]{:S(2)}) async-start(), calls=%async_computation.1 | async-start | bytes 3891200 | tf_op jit(solution)/shard_map/all_gather | solution.py:109
  11.6 199.6 %all-gather.13.cloned.1.call-start = ((), (), s32[]{:S(2)}) async-start(), calls=%async_computation.2 | async-start | bytes 3891200 | tf_op jit(solution)/shard_map/all_gather | solution.py:109
  12.3 261.9 %all-gather.15.cloned.1.call-start = ((), (), s32[]{:S(2)}) async-start(), calls=%async_computation.3 | async-start | bytes 3891200 | tf_op jit(solution)/shard_map/all_gather | solution.py:109
  13.0 46.4 %collective-permute-start = (bf16[304,16]{0,1:T(8,128)(2,1)}, bf16[304,16]{0,1:T(8,128)(2,1)}, u32[]{:S(2)}, u32[]{:S(2)}) collective-permute-start(bf16[304,16]{0,1:T(8,128)(2,1)} %convert_element_type.348), channel_id=1, source_target_pairs={{0,4},{4,0},{8,12},{12,8},{1,5},{5,1},{9,13},{13,9},{2,6},{6,2},{1... | collective-permute-start | bytes 29192 | tf_op jit(solution)/shard_map/ppermute | solution.py:22
  15.9 43.4 %collective-permute-start.1 = (bf16[304,16]{0,1:T(8,128)(2,1)}, bf16[304,16]{0,1:T(8,128)(2,1)}, u32[]{:S(2)}, u32[]{:S(2)}) collective-permute-start(bf16[304,16]{0,1:T(8,128)(2,1)} %convert_element_type.348), channel_id=1, source_target_pairs={{0,8},{4,12},{8,0},{12,4},{1,9},{5,13},{9,1},{13,5},{2,10},{6,14},... | collective-permute-start | bytes 29192 | tf_op jit(solution)/shard_map/ppermute | solution.py:22
  17.4 41.9 %collective-permute-start.2 = (bf16[304,16]{0,1:T(8,128)(2,1)}, bf16[304,16]{0,1:T(8,128)(2,1)}, u32[]{:S(2)}, u32[]{:S(2)}) collective-permute-start(bf16[304,16]{0,1:T(8,128)(2,1)} %convert_element_type.348), channel_id=1, source_target_pairs={{0,12},{4,8},{8,4},{12,0},{1,13},{5,9},{9,5},{13,1},{2,14},{6,10},... | collective-permute-start | bytes 29192 | tf_op jit(solution)/shard_map/ppermute | solution.py:22
  91.8 59.7 %collective-permute-start.10 = (bf16[192,608]{1,0:T(8,128)(2,1)S(1)}, bf16[192,608]{1,0:T(8,128)(2,1)S(1)}, u32[]{:S(2)}, u32[]{:S(2)}) collective-permute-start(bf16[192,608]{1,0:T(8,128)(2,1)S(1)} %get-tuple-element.104), channel_id=1, source_target_pairs={{0,4},{4,0},{8,12},{12,8},{1,5},{5,1},{9,13},{13,9},{2,6},{6,2},{1... | collective-permute-start | bytes 700424 | tf_op jit(solution)/shard_map/ppermute | solution.py:22
  95.2 56.3 %collective-permute-start.11 = (bf16[192,608]{1,0:T(8,128)(2,1)S(1)}, bf16[192,608]{1,0:T(8,128)(2,1)S(1)}, u32[]{:S(2)}, u32[]{:S(2)}) collective-permute-start(bf16[192,608]{1,0:T(8,128)(2,1)S(1)} %get-tuple-element.104), channel_id=1, source_target_pairs={{0,8},{4,12},{8,0},{12,4},{1,9},{5,13},{9,1},{13,5},{2,10},{6,14},... | collective-permute-start | bytes 700424 | tf_op jit(solution)/shard_map/ppermute | solution.py:22
  98.6 52.9 %collective-permute-start.12 = (bf16[192,608]{1,0:T(8,128)(2,1)S(1)}, bf16[192,608]{1,0:T(8,128)(2,1)}, u32[]{:S(2)}, u32[]{:S(2)}) collective-permute-start(bf16[192,608]{1,0:T(8,128)(2,1)S(1)} %get-tuple-element.104), channel_id=1, source_target_pairs={{0,12},{4,8},{8,4},{12,0},{1,13},{5,9},{9,5},{13,1},{2,14},{6,10},... | collective-permute-start | bytes 700424 | tf_op jit(solution)/shard_map/ppermute | solution.py:22
  162.3 52.3 %collective-permute-start.13 = (bf16[192,608]{1,0:T(8,128)(2,1)S(1)}, bf16[192,608]{1,0:T(8,128)(2,1)S(1)}, u32[]{:S(2)}, u32[]{:S(2)}) collective-permute-start(bf16[192,608]{1,0:T(8,128)(2,1)S(1)} %get-tuple-element.106), channel_id=1, source_target_pairs={{0,4},{4,0},{8,12},{12,8},{1,5},{5,1},{9,13},{13,9},{2,6},{6,2},{1... | collective-permute-start | bytes 700424 | tf_op jit(solution)/shard_map/ppermute | solution.py:22
  165.8 48.9 %collective-permute-start.14 = (bf16[192,608]{1,0:T(8,128)(2,1)S(1)}, bf16[192,608]{1,0:T(8,128)(2,1)S(1)}, u32[]{:S(2)}, u32[]{:S(2)}) collective-permute-start(bf16[192,608]{1,0:T(8,128)(2,1)S(1)} %get-tuple-element.106), channel_id=1, source_target_pairs={{0,8},{4,12},{8,0},{12,4},{1,9},{5,13},{9,1},{13,5},{2,10},{6,14},... | collective-permute-start | bytes 700424 | tf_op jit(solution)/shard_map/ppermute | solution.py:22
  169.1 45.5 %collective-permute-start.15 = (bf16[192,608]{1,0:T(8,128)(2,1)S(1)}, bf16[192,608]{1,0:T(8,128)(2,1)}, u32[]{:S(2)}, u32[]{:S(2)}) collective-permute-start(bf16[192,608]{1,0:T(8,128)(2,1)S(1)} %get-tuple-element.106), channel_id=1, source_target_pairs={{0,12},{4,8},{8,4},{12,0},{1,13},{5,9},{9,5},{13,1},{2,14},{6,10},... | collective-permute-start | bytes 700424 | tf_op jit(solution)/shard_map/ppermute | solution.py:22
  226.5 51.2 %collective-permute-start.16 = (bf16[192,608]{1,0:T(8,128)(2,1)S(1)}, bf16[192,608]{1,0:T(8,128)(2,1)S(1)}, u32[]{:S(2)}, u32[]{:S(2)}) collective-permute-start(bf16[192,608]{1,0:T(8,128)(2,1)S(1)} %get-tuple-element.108), channel_id=1, source_target_pairs={{0,4},{4,0},{8,12},{12,8},{1,5},{5,1},{9,13},{13,9},{2,6},{6,2},{1... | collective-permute-start | bytes 700424 | tf_op jit(solution)/shard_map/ppermute | solution.py:22
  229.9 47.8 %collective-permute-start.17 = (bf16[192,608]{1,0:T(8,128)(2,1)S(1)}, bf16[192,608]{1,0:T(8,128)(2,1)S(1)}, u32[]{:S(2)}, u32[]{:S(2)}) collective-permute-start(bf16[192,608]{1,0:T(8,128)(2,1)S(1)} %get-tuple-element.108), channel_id=1, source_target_pairs={{0,8},{4,12},{8,0},{12,4},{1,9},{5,13},{9,1},{13,5},{2,10},{6,14},... | collective-permute-start | bytes 700424 | tf_op jit(solution)/shard_map/ppermute | solution.py:22
  233.3 44.5 %collective-permute-start.18 = (bf16[192,608]{1,0:T(8,128)(2,1)S(1)}, bf16[192,608]{1,0:T(8,128)(2,1)}, u32[]{:S(2)}, u32[]{:S(2)}) collective-permute-start(bf16[192,608]{1,0:T(8,128)(2,1)S(1)} %get-tuple-element.108), channel_id=1, source_target_pairs={{0,12},{4,8},{8,4},{12,0},{1,13},{5,9},{9,5},{13,1},{2,14},{6,10},... | collective-permute-start | bytes 700424 | tf_op jit(solution)/shard_map/ppermute | solution.py:22
  387.7 14.8 %collective-permute-start.36 = (bf16[60,2432]{1,0:T(8,128)(2,1)}, bf16[60,2432]{1,0:T(8,128)(2,1)}, u32[]{:S(2)}, u32[]{:S(2)}) collective-permute-start(bf16[60,2432]{1,0:T(8,128)(2,1)} %get-tuple-element.48), channel_id=1, source_target_pairs={{0,2},{1,3},{2,0},{3,1},{4,6},{5,7},{6,4},{7,5},{8,10},{9,11},{10,... | collective-permute-start | bytes 875528 | tf_op jit(solution)/shard_map/ppermute | solution.py:22
  389.2 13.3 %collective-permute-start.37 = (bf16[60,2432]{1,0:T(8,128)(2,1)}, bf16[60,2432]{1,0:T(8,128)(2,1)}, u32[]{:S(2)}, u32[]{:S(2)}) collective-permute-start(bf16[60,2432]{1,0:T(8,128)(2,1)} %get-tuple-element.47), channel_id=1, source_target_pairs={{0,3},{1,2},{2,1},{3,0},{4,7},{5,6},{6,5},{7,4},{8,11},{9,10},{10,... | collective-permute-start | bytes 875528 | tf_op jit(solution)/shard_map/ppermute | solution.py:22
  468.9 90.7 %collective-permute-start.65 = (bf16[192,608]{1,0:T(8,128)(2,1)S(1)}, bf16[192,608]{1,0:T(8,128)(2,1)S(1)}, u32[]{:S(2)}, u32[]{:S(2)}) collective-permute-start(bf16[192,608]{1,0:T(8,128)(2,1)S(1)} %fusion.141), channel_id=1, source_target_pairs={{16,0},{17,1},{18,2},{19,3},{20,4},{21,5},{22,6},{23,7},{24,8},{25... | collective-permute-start | bytes 700424 | tf_op jit(solution)/shard_map/ppermute | solution.py:219
  563.1 21.7 %collective-permute-start.66 = (bf16[192,608]{1,0:T(8,128)(2,1)S(1)}, bf16[192,608]{1,0:T(8,128)(2,1)S(1)}, u32[]{:S(2)}, u32[]{:S(2)}) collective-permute-start(bf16[192,608]{1,0:T(8,128)(2,1)S(1)} %get-tuple-element.61), channel_id=1, source_target_pairs={{0,4},{4,0},{8,12},{12,8},{1,5},{5,1},{9,13},{13,9},{2,6},{6,2},{1... | collective-permute-start | bytes 700424 | tf_op jit(solution)/shard_map/ppermute | solution.py:207
  565.8 19.1 %collective-permute-start.67 = (bf16[192,608]{1,0:T(8,128)(2,1)S(1)}, bf16[192,608]{1,0:T(8,128)(2,1)S(1)}, u32[]{:S(2)}, u32[]{:S(2)}) collective-permute-start(bf16[192,608]{1,0:T(8,128)(2,1)S(1)} %get-tuple-element.63), channel_id=1, source_target_pairs={{0,8},{4,12},{8,0},{12,4},{1,9},{5,13},{9,1},{13,5},{2,10},{6,14},... | collective-permute-start | bytes 700424 | tf_op jit(solution)/shard_map/ppermute | solution.py:207
  568.1 16.7 %collective-permute-start.68 = (bf16[192,608]{1,0:T(8,128)(2,1)S(1)}, bf16[192,608]{1,0:T(8,128)(2,1)S(1)}, u32[]{:S(2)}, u32[]{:S(2)}) collective-permute-start(bf16[192,608]{1,0:T(8,128)(2,1)S(1)} %get-tuple-element.62), channel_id=1, source_target_pairs={{0,12},{4,8},{8,4},{12,0},{1,13},{5,9},{9,5},{13,1},{2,14},{6,10},... | collective-permute-start | bytes 700424 | tf_op jit(solution)/shard_map/ppermute | solution.py:207
  588.8 22.5 %collective-permute-start.72 = (bf16[192,608]{1,0:T(8,128)(2,1)S(1)}, bf16[192,608]{1,0:T(8,128)(2,1)S(1)}, u32[]{:S(2)}, u32[]{:S(2)}) collective-permute-start(bf16[192,608]{1,0:T(8,128)(2,1)S(1)} %get-tuple-element.58), channel_id=1, source_target_pairs={{0,4},{4,0},{8,12},{12,8},{1,5},{5,1},{9,13},{13,9},{2,6},{6,2},{1... | collective-permute-start | bytes 700424 | tf_op jit(solution)/shard_map/ppermute | solution.py:207
  591.9 19.4 %collective-permute-start.73 = (bf16[192,608]{1,0:T(8,128)(2,1)S(1)}, bf16[192,608]{1,0:T(8,128)(2,1)S(1)}, u32[]{:S(2)}, u32[]{:S(2)}) collective-permute-start(bf16[192,608]{1,0:T(8,128)(2,1)S(1)} %get-tuple-element.60), channel_id=1, source_target_pairs={{0,8},{4,12},{8,0},{12,4},{1,9},{5,13},{9,1},{13,5},{2,10},{6,14},... | collective-permute-start | bytes 700424 | tf_op jit(solution)/shard_map/ppermute | solution.py:207
  595.0 16.3 %collective-permute-start.74 = (bf16[192,608]{1,0:T(8,128)(2,1)S(1)}, bf16[192,608]{1,0:T(8,128)(2,1)S(1)}, u32[]{:S(2)}, u32[]{:S(2)}) collective-permute-start(bf16[192,608]{1,0:T(8,128)(2,1)S(1)} %get-tuple-element.59), channel_id=1, source_target_pairs={{0,12},{4,8},{8,4},{12,0},{1,13},{5,9},{9,5},{13,1},{2,14},{6,10},... | collective-permute-start | bytes 700424 | tf_op jit(solution)/shard_map/ppermute | solution.py:207
  616.1 21.6 %collective-permute-start.78 = (bf16[192,608]{1,0:T(8,128)(2,1)S(1)}, bf16[192,608]{1,0:T(8,128)(2,1)S(1)}, u32[]{:S(2)}, u32[]{:S(2)}) collective-permute-start(bf16[192,608]{1,0:T(8,128)(2,1)S(1)} %get-tuple-element.55), channel_id=1, source_target_pairs={{0,4},{4,0},{8,12},{12,8},{1,5},{5,1},{9,13},{13,9},{2,6},{6,2},{1... | collective-permute-start | bytes 700424 | tf_op jit(solution)/shard_map/ppermute | solution.py:207
  618.8 18.9 %collective-permute-start.79 = (bf16[192,608]{1,0:T(8,128)(2,1)S(1)}, bf16[192,608]{1,0:T(8,128)(2,1)S(1)}, u32[]{:S(2)}, u32[]{:S(2)}) collective-permute-start(bf16[192,608]{1,0:T(8,128)(2,1)S(1)} %get-tuple-element.57), channel_id=1, source_target_pairs={{0,8},{4,12},{8,0},{12,4},{1,9},{5,13},{9,1},{13,5},{2,10},{6,14},... | collective-permute-start | bytes 700424 | tf_op jit(solution)/shard_map/ppermute | solution.py:207
  621.6 16.2 %collective-permute-start.80 = (bf16[192,608]{1,0:T(8,128)(2,1)S(1)}, bf16[192,608]{1,0:T(8,128)(2,1)S(1)}, u32[]{:S(2)}, u32[]{:S(2)}) collective-permute-start(bf16[192,608]{1,0:T(8,128)(2,1)S(1)} %get-tuple-element.56), channel_id=1, source_target_pairs={{0,12},{4,8},{8,4},{12,0},{1,13},{5,9},{9,5},{13,1},{2,14},{6,10},... | collective-permute-start | bytes 700424 | tf_op jit(solution)/shard_map/ppermute | solution.py:207
  642.4 15.5 %collective-permute-start.87 = (f32[1,192]{1,0:T(1,128)S(1)}, f32[1,192]{1,0:T(1,128)S(1)}, u32[]{:S(2)}, u32[]{:S(2)}) collective-permute-start(f32[1,192]{1,0:T(1,128)S(1)} %bitcast.361), channel_id=1, source_target_pairs={{0,4},{4,0},{8,12},{12,8},{1,5},{5,1},{9,13},{13,9},{2,6},{6,2},{1... | collective-permute-start | bytes 2312 | tf_op jit(solution)/shard_map/ppermute | solution.py:208
  645.5 18.8 %collective-permute-start.84 = (bf16[192,608]{1,0:T(8,128)(2,1)S(1)}, bf16[192,608]{1,0:T(8,128)(2,1)S(1)}, u32[]{:S(2)}, u32[]{:S(2)}) collective-permute-start(bf16[192,608]{1,0:T(8,128)(2,1)S(1)} %get-tuple-element.52), channel_id=1, source_target_pairs={{0,4},{4,0},{8,12},{12,8},{1,5},{5,1},{9,13},{13,9},{2,6},{6,2},{1... | collective-permute-start | bytes 700424 | tf_op jit(solution)/shard_map/ppermute | solution.py:207
  648.2 16.0 %collective-permute-start.85 = (bf16[192,608]{1,0:T(8,128)(2,1)S(1)}, bf16[192,608]{1,0:T(8,128)(2,1)S(1)}, u32[]{:S(2)}, u32[]{:S(2)}) collective-permute-start(bf16[192,608]{1,0:T(8,128)(2,1)S(1)} %get-tuple-element.54), channel_id=1, source_target_pairs={{0,8},{4,12},{8,0},{12,4},{1,9},{5,13},{9,1},{13,5},{2,10},{6,14},... | collective-permute-start | bytes 700424 | tf_op jit(solution)/shard_map/ppermute | solution.py:207
  651.3 12.9 %collective-permute-start.86 = (bf16[192,608]{1,0:T(8,128)(2,1)S(1)}, bf16[192,608]{1,0:T(8,128)(2,1)S(1)}, u32[]{:S(2)}, u32[]{:S(2)}) collective-permute-start(bf16[192,608]{1,0:T(8,128)(2,1)S(1)} %get-tuple-element.53), channel_id=1, source_target_pairs={{0,12},{4,8},{8,4},{12,0},{1,13},{5,9},{9,5},{13,1},{2,14},{6,10},... | collective-permute-start | bytes 700424 | tf_op jit(solution)/shard_map/ppermute | solution.py:207
  (192 other events, 1713.1 us)
Sparse Core Ops, SparseCore 0:
  11.0 73.9 all-gather.8
  86.6 61.3 all-gather.10
  149.5 61.6 all-gather.12
  212.6 61.6 all-gather.14

commit v7 on v6

--- a/solution.py
+++ b/solution.py
@@ -231,7 +231,6 @@
     for d in range(1, n_dp):
         block = lax.dynamic_slice_in_dim(latent_pre, (me_dp ^ d) * lat_part, lat_part, 1)
         got.append(lax.ppermute(block, ("section", "dp"), xor_pairs(n_dp, d, 0)))
-    got = jnp.take(jnp.stack(got), me_dp ^ jnp.arange(n_dp, dtype=jnp.int32), axis=0)
     lat_sum = got[0]
     for src in range(1, n_dp):
         lat_sum = lat_sum + got[src]
@@ -250,7 +249,6 @@
     for d in range(1, n_mp):
         outgoing = lax.dynamic_index_in_dim(part_grad, me_mp ^ d, 0, keepdims=False)
         got.append(swap(outgoing, "mp", n_mp, d))
-    got = jnp.take(jnp.stack(got), me_mp ^ jnp.arange(n_mp, dtype=jnp.int32), axis=0)
     grad_sum = got[0]
     for src in range(1, n_mp):
         grad_sum = grad_sum + got[src]

time: 730 us -> 730 us (level)
  no operation moved by 1% of the time
where the time goes in v7:
time: 730 us; the launch traced here: 719 us
  waiting for transfers between devices  281 us (38%)
  starting transfers between devices  188 us (26%)
  local copies, waits for them, and re-layouts  104 us (14%)
  matrix products  74.9 us (10%)
  other arithmetic  46.8 us (6%)
  between operations  23.8 us (3%)
    all_gather x4, waiting for transfers between devices, on_device(): lax.all_gather(teacher_weight[0, slot_no], 'mp', axis=0, tiled=True)  127 us
    ppermute x1, waiting for transfers between devices, on_device(): lax.ppermute(grad_stream.astype(jnp.bfloat16), 'section', [(live, live -...  89.4 us
    ppermute x50, starting transfers between devices, swap(): return lax.ppermute(x, axis, xor_pairs(n, d, base))  83.1 us
    ppermute x50, waiting for transfers between devices, swap(): return lax.ppermute(x, axis, xor_pairs(n, d, base))  46.1 us
    ppermute x24, starting transfers between devices, on_device(): terms.append(lax.ppermute(row_term[None, :], ('section', 'dp'), pairs))  45.8 us
    ppermute x24, starting transfers between devices, on_device(): pieces.append(lax.ppermute(block, ('section', 'dp'), pairs))  45 us
    dot_general x8, matrix products, on_device(): jnp.dot(normed_in, weights[slot_no], preferred_element_type=jnp.float32)  34.7 us
    dot_general x8, matrix products, on_device(): jnp.dot(pre_grad, weights[slot_no].T, preferred_element_type=jnp.float32)  26.7 us
  transfers between devices with their start and end apart: 108, of which 30 were waited for; matrix products, arithmetic and copies ran while one was open for 13% of the time, Pallas kernels for 0%

profile of v7, /device:TPU:0, one launch (start us, length us, event | category | flops | bytes accessed | tf_op | source)
XLA Modules:
  0.0 718.9 jit_solution(14516872880506228181)
XLA Ops:
  7.2 3.6 fusion.365
  19.8 6.3 broadcast_in_dim.151
  26.2 11.7 %fusion.364 = (f32[4,192,1,2432]{3,1,2,0:T(8,128)}, f32[4,192,1,2432]{3,1,2,0:T(8,128)}) fusion(f32[4,192,2,2432]{3,1,2,0:T(8,128)} %bitcast.319), kind=kLoop, calls=%fused_computation.575 | loop fusion | bytes 29884416 | tf_op jit(solution)/shard_map/slice | solution.py:117
  38.1 9.0 %dynamic-slice_bitcast_fusion = (f32[4,192,608]{2,1,0:T(8,128)}, f32[4,192,608]{2,1,0:T(8,128)}, f32[4,192,608]{2,1,0:T(8,128)}, f32[4,192,608]{2,1,0:T(8,128)}) fusion(f32[4,192,1,2432]{3,1,2,0:T(8,128)} %get-tuple-element.9, s32[]{:T(128)S(6)} %select_n.364, s32[]{:T(128)S(6)} %select_n.363, s32[]{:T(128)S(6)} %select_n.362, s32[]{:T(128)S(6)} %select_n.361), kind=kLoop, calls=%fused_computation.32 | loop fusion | bytes 14942224 | tf_op jit(solution)/shard_map/dynamic_slice | solution.py:34
  48.9 9.5 %concatenate.60 = f32[4,192,2432]{2,1,0:T(8,128)} concatenate(f32[4,192,608]{2,1,0:T(8,128)} %get-tuple-element.17, f32[4,192,608]{2,1,0:T(8,128)} %get-tuple-element.16, f32[4,192,608]{2,1,0:T(8,128)} %get-tuple-element.15, f32[4,192,608]{2,1,0:T(8,128)} %get-tuple-element.14), dimensions={2} | concatenate | bytes 14942208 | tf_op jit(solution)/shard_map/concatenate | solution.py:33
  71.5 6.6 collective-permute-done.8
  87.5 4.3 multiply_convert_fusion.23
  101.3 46.8 %all-gather.11.cloned.1.call-done = bf16[1,1,2432,608]{3,2,1,0:T(8,128)(2,1)} async-done(((bf16[1,1,608,608]{3,2,1,0:T(8,128)(2,1)}), bf16[1,1,2432,608]{3,2,1,0:T(8,128)(2,1)}) %all-gather.11.cloned.1.call-update) | async-done | bytes 2957328 | tf_op jit(solution)/shard_map/all_gather | solution.py:109
  148.1 3.6 dynamic-slice_bitcast_fusion.15
  158.4 4.2 multiply_convert_fusion.22
  171.8 39.5 %all-gather.13.cloned.1.call-done = bf16[1,1,2432,608]{3,2,1,0:T(8,128)(2,1)} async-done(((bf16[1,1,608,608]{3,2,1,0:T(8,128)(2,1)}), bf16[1,1,2432,608]{3,2,1,0:T(8,128)(2,1)}) %all-gather.13.cloned.1.call-update) | async-done | bytes 2957328 | tf_op jit(solution)/shard_map/all_gather | solution.py:109
  222.6 4.1 multiply_convert_fusion.21
  236.0 38.4 %all-gather.15.cloned.1.call-done = bf16[1,1,2432,608]{3,2,1,0:T(8,128)(2,1)} async-done(((bf16[1,1,608,608]{3,2,1,0:T(8,128)(2,1)}), bf16[1,1,2432,608]{3,2,1,0:T(8,128)(2,1)}) %all-gather.15.cloned.1.call-update) | async-done | bytes 2957328 | tf_op jit(solution)/shard_map/all_gather | solution.py:109
  274.4 3.6 dynamic-slice_bitcast_fusion.7
  285.5 4.1 multiply_convert_fusion.20
  301.0 4.4 collective-permute-done.21
  316.2 5.3 multiply_convert_fusion.19
  335.7 4.2 multiply_convert_fusion.18
  350.2 4.2 multiply_convert_fusion.17
  371.1 4.1 multiply_convert_fusion.16
  381.4 6.1 convolution_convert_fusion
  394.5 4.1 collective-permute-done.35
  398.6 4.7 collective-permute-done.36
  414.7 4.0 collective-permute-start.38
  421.3 4.1 collective-permute-done.39
  428.4 4.7 convolution_convert_fusion.8
  471.1 89.4 %collective-permute-done.65 = bf16[192,608]{1,0:T(8,128)(2,1)S(1)} collective-permute-done((bf16[192,608]{1,0:T(8,128)(2,1)S(1)}, bf16[192,608]{1,0:T(8,128)(2,1)S(1)}, u32[]{:S(2)}, u32[]{:S(2)}) %collective-permute-start.65) | collective-permute-done | bytes 233504 | tf_op jit(solution)/shard_map/ppermute | solution.py:219
  569.1 4.2 collective-permute-start.68
  579.4 3.8 collective-permute-start.71
  622.6 3.8 collective-permute-start.80
  632.4 3.8 collective-permute-start.83
  672.4 3.8 collective-permute-start.92
  (608 shorter events, 340.9 us)
Async XLA Ops:
  7.2 77.9 %all-gather.9.cloned.1.call-start = ((), (), s32[]{:S(2)}) async-start(), calls=%async_computation | async-start | bytes 3891200 | tf_op jit(solution)/shard_map/all_gather | solution.py:109
  10.9 137.3 %all-gather.11.cloned.1.call-start = ((), (), s32[]{:S(2)}) async-start(), calls=%async_computation.1 | async-start | bytes 3891200 | tf_op jit(solution)/shard_map/all_gather | solution.py:109
  11.6 199.7 %all-gather.13.cloned.1.call-start = ((), (), s32[]{:S(2)}) async-start(), calls=%async_computation.2 | async-start | bytes 3891200 | tf_op jit(solution)/shard_map/all_gather | solution.py:109
  12.4 262.1 %all-gather.15.cloned.1.call-start = ((), (), s32[]{:S(2)}) async-start(), calls=%async_computation.3 | async-start | bytes 3891200 | tf_op jit(solution)/shard_map/all_gather | solution.py:109
  12.4 45.9 %collective-permute-start = (bf16[304,16]{0,1:T(8,128)(2,1)S(1)}, bf16[304,16]{0,1:T(8,128)(2,1)S(1)}, u32[]{:S(2)}, u32[]{:S(2)}) collective-permute-start(bf16[304,16]{0,1:T(8,128)(2,1)S(1)} %convert_element_type.348), channel_id=1, source_target_pairs={{0,4},{4,0},{8,12},{12,8},{1,5},{5,1},{9,13},{13,9},{2,6},{6,2},{1... | collective-permute-start | bytes 29192 | tf_op jit(solution)/shard_map/ppermute | solution.py:22
  15.4 42.9 %collective-permute-start.1 = (bf16[304,16]{0,1:T(8,128)(2,1)S(1)}, bf16[304,16]{0,1:T(8,128)(2,1)S(1)}, u32[]{:S(2)}, u32[]{:S(2)}) collective-permute-start(bf16[304,16]{0,1:T(8,128)(2,1)S(1)} %convert_element_type.348), channel_id=1, source_target_pairs={{0,8},{4,12},{8,0},{12,4},{1,9},{5,13},{9,1},{13,5},{2,10},{6,14},... | collective-permute-start | bytes 29192 | tf_op jit(solution)/shard_map/ppermute | solution.py:22
  17.0 41.4 %collective-permute-start.2 = (bf16[304,16]{0,1:T(8,128)(2,1)S(1)}, bf16[304,16]{0,1:T(8,128)(2,1)S(1)}, u32[]{:S(2)}, u32[]{:S(2)}) collective-permute-start(bf16[304,16]{0,1:T(8,128)(2,1)S(1)} %convert_element_type.348), channel_id=1, source_target_pairs={{0,12},{4,8},{8,4},{12,0},{1,13},{5,9},{9,5},{13,1},{2,14},{6,10},... | collective-permute-start | bytes 29192 | tf_op jit(solution)/shard_map/ppermute | solution.py:22
  91.9 59.9 %collective-permute-start.10 = (bf16[192,608]{1,0:T(8,128)(2,1)S(1)}, bf16[192,608]{1,0:T(8,128)(2,1)S(1)}, u32[]{:S(2)}, u32[]{:S(2)}) collective-permute-start(bf16[192,608]{1,0:T(8,128)(2,1)S(1)} %get-tuple-element.103), channel_id=1, source_target_pairs={{0,4},{4,0},{8,12},{12,8},{1,5},{5,1},{9,13},{13,9},{2,6},{6,2},{1... | collective-permute-start | bytes 700424 | tf_op jit(solution)/shard_map/ppermute | solution.py:22
  95.2 56.5 %collective-permute-start.11 = (bf16[192,608]{1,0:T(8,128)(2,1)S(1)}, bf16[192,608]{1,0:T(8,128)(2,1)S(1)}, u32[]{:S(2)}, u32[]{:S(2)}) collective-permute-start(bf16[192,608]{1,0:T(8,128)(2,1)S(1)} %get-tuple-element.103), channel_id=1, source_target_pairs={{0,8},{4,12},{8,0},{12,4},{1,9},{5,13},{9,1},{13,5},{2,10},{6,14},... | collective-permute-start | bytes 700424 | tf_op jit(solution)/shard_map/ppermute | solution.py:22
  98.6 53.1 %collective-permute-start.12 = (bf16[192,608]{1,0:T(8,128)(2,1)S(1)}, bf16[192,608]{1,0:T(8,128)(2,1)}, u32[]{:S(2)}, u32[]{:S(2)}) collective-permute-start(bf16[192,608]{1,0:T(8,128)(2,1)S(1)} %get-tuple-element.103), channel_id=1, source_target_pairs={{0,12},{4,8},{8,4},{12,0},{1,13},{5,9},{9,5},{13,1},{2,14},{6,10},... | collective-permute-start | bytes 700424 | tf_op jit(solution)/shard_map/ppermute | solution.py:22
  162.6 52.3 %collective-permute-start.13 = (bf16[192,608]{1,0:T(8,128)(2,1)S(1)}, bf16[192,608]{1,0:T(8,128)(2,1)S(1)}, u32[]{:S(2)}, u32[]{:S(2)}) collective-permute-start(bf16[192,608]{1,0:T(8,128)(2,1)S(1)} %get-tuple-element.105), channel_id=1, source_target_pairs={{0,4},{4,0},{8,12},{12,8},{1,5},{5,1},{9,13},{13,9},{2,6},{6,2},{1... | collective-permute-start | bytes 700424 | tf_op jit(solution)/shard_map/ppermute | solution.py:22
  166.1 48.9 %collective-permute-start.14 = (bf16[192,608]{1,0:T(8,128)(2,1)S(1)}, bf16[192,608]{1,0:T(8,128)(2,1)S(1)}, u32[]{:S(2)}, u32[]{:S(2)}) collective-permute-start(bf16[192,608]{1,0:T(8,128)(2,1)S(1)} %get-tuple-element.105), channel_id=1, source_target_pairs={{0,8},{4,12},{8,0},{12,4},{1,9},{5,13},{9,1},{13,5},{2,10},{6,14},... | collective-permute-start | bytes 700424 | tf_op jit(solution)/shard_map/ppermute | solution.py:22
  169.4 45.5 %collective-permute-start.15 = (bf16[192,608]{1,0:T(8,128)(2,1)S(1)}, bf16[192,608]{1,0:T(8,128)(2,1)}, u32[]{:S(2)}, u32[]{:S(2)}) collective-permute-start(bf16[192,608]{1,0:T(8,128)(2,1)S(1)} %get-tuple-element.105), channel_id=1, source_target_pairs={{0,12},{4,8},{8,4},{12,0},{1,13},{5,9},{9,5},{13,1},{2,14},{6,10},... | collective-permute-start | bytes 700424 | tf_op jit(solution)/shard_map/ppermute | solution.py:22
  226.8 51.3 %collective-permute-start.16 = (bf16[192,608]{1,0:T(8,128)(2,1)S(1)}, bf16[192,608]{1,0:T(8,128)(2,1)S(1)}, u32[]{:S(2)}, u32[]{:S(2)}) collective-permute-start(bf16[192,608]{1,0:T(8,128)(2,1)S(1)} %get-tuple-element.107), channel_id=1, source_target_pairs={{0,4},{4,0},{8,12},{12,8},{1,5},{5,1},{9,13},{13,9},{2,6},{6,2},{1... | collective-permute-start | bytes 700424 | tf_op jit(solution)/shard_map/ppermute | solution.py:22
  230.2 47.9 %collective-permute-start.17 = (bf16[192,608]{1,0:T(8,128)(2,1)S(1)}, bf16[192,608]{1,0:T(8,128)(2,1)S(1)}, u32[]{:S(2)}, u32[]{:S(2)}) collective-permute-start(bf16[192,608]{1,0:T(8,128)(2,1)S(1)} %get-tuple-element.107), channel_id=1, source_target_pairs={{0,8},{4,12},{8,0},{12,4},{1,9},{5,13},{9,1},{13,5},{2,10},{6,14},... | collective-permute-start | bytes 700424 | tf_op jit(solution)/shard_map/ppermute | solution.py:22
  233.5 44.5 %collective-permute-start.18 = (bf16[192,608]{1,0:T(8,128)(2,1)S(1)}, bf16[192,608]{1,0:T(8,128)(2,1)}, u32[]{:S(2)}, u32[]{:S(2)}) collective-permute-start(bf16[192,608]{1,0:T(8,128)(2,1)S(1)} %get-tuple-element.107), channel_id=1, source_target_pairs={{0,12},{4,8},{8,4},{12,0},{1,13},{5,9},{9,5},{13,1},{2,14},{6,10},... | collective-permute-start | bytes 700424 | tf_op jit(solution)/shard_map/ppermute | solution.py:22
  388.5 14.8 %collective-permute-start.36 = (bf16[60,2432]{1,0:T(8,128)(2,1)}, bf16[60,2432]{1,0:T(8,128)(2,1)}, u32[]{:S(2)}, u32[]{:S(2)}) collective-permute-start(bf16[60,2432]{1,0:T(8,128)(2,1)} %get-tuple-element.48), channel_id=1, source_target_pairs={{0,2},{1,3},{2,0},{3,1},{4,6},{5,7},{6,4},{7,5},{8,10},{9,11},{10,... | collective-permute-start | bytes 875528 | tf_op jit(solution)/shard_map/ppermute | solution.py:22
  390.1 13.3 %collective-permute-start.37 = (bf16[60,2432]{1,0:T(8,128)(2,1)}, bf16[60,2432]{1,0:T(8,128)(2,1)}, u32[]{:S(2)}, u32[]{:S(2)}) collective-permute-start(bf16[60,2432]{1,0:T(8,128)(2,1)} %get-tuple-element.47), channel_id=1, source_target_pairs={{0,3},{1,2},{2,1},{3,0},{4,7},{5,6},{6,5},{7,4},{8,11},{9,10},{10,... | collective-permute-start | bytes 875528 | tf_op jit(solution)/shard_map/ppermute | solution.py:22
  469.8 90.7 %collective-permute-start.65 = (bf16[192,608]{1,0:T(8,128)(2,1)S(1)}, bf16[192,608]{1,0:T(8,128)(2,1)S(1)}, u32[]{:S(2)}, u32[]{:S(2)}) collective-permute-start(bf16[192,608]{1,0:T(8,128)(2,1)S(1)} %fusion.141), channel_id=1, source_target_pairs={{16,0},{17,1},{18,2},{19,3},{20,4},{21,5},{22,6},{23,7},{24,8},{25... | collective-permute-start | bytes 700424 | tf_op jit(solution)/shard_map/ppermute | solution.py:219
  564.1 21.7 %collective-permute-start.66 = (bf16[192,608]{1,0:T(8,128)(2,1)S(1)}, bf16[192,608]{1,0:T(8,128)(2,1)S(1)}, u32[]{:S(2)}, u32[]{:S(2)}) collective-permute-start(bf16[192,608]{1,0:T(8,128)(2,1)S(1)} %get-tuple-element.61), channel_id=1, source_target_pairs={{0,4},{4,0},{8,12},{12,8},{1,5},{5,1},{9,13},{13,9},{2,6},{6,2},{1... | collective-permute-start | bytes 700424 | tf_op jit(solution)/shard_map/ppermute | solution.py:207
  566.8 19.0 %collective-permute-start.67 = (bf16[192,608]{1,0:T(8,128)(2,1)S(1)}, bf16[192,608]{1,0:T(8,128)(2,1)S(1)}, u32[]{:S(2)}, u32[]{:S(2)}) collective-permute-start(bf16[192,608]{1,0:T(8,128)(2,1)S(1)} %get-tuple-element.63), channel_id=1, source_target_pairs={{0,8},{4,12},{8,0},{12,4},{1,9},{5,13},{9,1},{13,5},{2,10},{6,14},... | collective-permute-start | bytes 700424 | tf_op jit(solution)/shard_map/ppermute | solution.py:207
  569.1 16.7 %collective-permute-start.68 = (bf16[192,608]{1,0:T(8,128)(2,1)S(1)}, bf16[192,608]{1,0:T(8,128)(2,1)S(1)}, u32[]{:S(2)}, u32[]{:S(2)}) collective-permute-start(bf16[192,608]{1,0:T(8,128)(2,1)S(1)} %get-tuple-element.62), channel_id=1, source_target_pairs={{0,12},{4,8},{8,4},{12,0},{1,13},{5,9},{9,5},{13,1},{2,14},{6,10},... | collective-permute-start | bytes 700424 | tf_op jit(solution)/shard_map/ppermute | solution.py:207
  589.7 22.5 %collective-permute-start.72 = (bf16[192,608]{1,0:T(8,128)(2,1)S(1)}, bf16[192,608]{1,0:T(8,128)(2,1)S(1)}, u32[]{:S(2)}, u32[]{:S(2)}) collective-permute-start(bf16[192,608]{1,0:T(8,128)(2,1)S(1)} %get-tuple-element.58), channel_id=1, source_target_pairs={{0,4},{4,0},{8,12},{12,8},{1,5},{5,1},{9,13},{13,9},{2,6},{6,2},{1... | collective-permute-start | bytes 700424 | tf_op jit(solution)/shard_map/ppermute | solution.py:207
  592.8 19.4 %collective-permute-start.73 = (bf16[192,608]{1,0:T(8,128)(2,1)S(1)}, bf16[192,608]{1,0:T(8,128)(2,1)S(1)}, u32[]{:S(2)}, u32[]{:S(2)}) collective-permute-start(bf16[192,608]{1,0:T(8,128)(2,1)S(1)} %get-tuple-element.60), channel_id=1, source_target_pairs={{0,8},{4,12},{8,0},{12,4},{1,9},{5,13},{9,1},{13,5},{2,10},{6,14},... | collective-permute-start | bytes 700424 | tf_op jit(solution)/shard_map/ppermute | solution.py:207
  596.0 16.3 %collective-permute-start.74 = (bf16[192,608]{1,0:T(8,128)(2,1)S(1)}, bf16[192,608]{1,0:T(8,128)(2,1)S(1)}, u32[]{:S(2)}, u32[]{:S(2)}) collective-permute-start(bf16[192,608]{1,0:T(8,128)(2,1)S(1)} %get-tuple-element.59), channel_id=1, source_target_pairs={{0,12},{4,8},{8,4},{12,0},{1,13},{5,9},{9,5},{13,1},{2,14},{6,10},... | collective-permute-start | bytes 700424 | tf_op jit(solution)/shard_map/ppermute | solution.py:207
  617.1 21.6 %collective-permute-start.78 = (bf16[192,608]{1,0:T(8,128)(2,1)S(1)}, bf16[192,608]{1,0:T(8,128)(2,1)S(1)}, u32[]{:S(2)}, u32[]{:S(2)}) collective-permute-start(bf16[192,608]{1,0:T(8,128)(2,1)S(1)} %get-tuple-element.55), channel_id=1, source_target_pairs={{0,4},{4,0},{8,12},{12,8},{1,5},{5,1},{9,13},{13,9},{2,6},{6,2},{1... | collective-permute-start | bytes 700424 | tf_op jit(solution)/shard_map/ppermute | solution.py:207
  619.8 18.9 %collective-permute-start.79 = (bf16[192,608]{1,0:T(8,128)(2,1)S(1)}, bf16[192,608]{1,0:T(8,128)(2,1)S(1)}, u32[]{:S(2)}, u32[]{:S(2)}) collective-permute-start(bf16[192,608]{1,0:T(8,128)(2,1)S(1)} %get-tuple-element.57), channel_id=1, source_target_pairs={{0,8},{4,12},{8,0},{12,4},{1,9},{5,13},{9,1},{13,5},{2,10},{6,14},... | collective-permute-start | bytes 700424 | tf_op jit(solution)/shard_map/ppermute | solution.py:207
  622.6 16.2 %collective-permute-start.80 = (bf16[192,608]{1,0:T(8,128)(2,1)S(1)}, bf16[192,608]{1,0:T(8,128)(2,1)S(1)}, u32[]{:S(2)}, u32[]{:S(2)}) collective-permute-start(bf16[192,608]{1,0:T(8,128)(2,1)S(1)} %get-tuple-element.56), channel_id=1, source_target_pairs={{0,12},{4,8},{8,4},{12,0},{1,13},{5,9},{9,5},{13,1},{2,14},{6,10},... | collective-permute-start | bytes 700424 | tf_op jit(solution)/shard_map/ppermute | solution.py:207
  643.3 15.5 %collective-permute-start.87 = (f32[1,192]{1,0:T(1,128)S(1)}, f32[1,192]{1,0:T(1,128)S(1)}, u32[]{:S(2)}, u32[]{:S(2)}) collective-permute-start(f32[1,192]{1,0:T(1,128)S(1)} %bitcast.348), channel_id=1, source_target_pairs={{0,4},{4,0},{8,12},{12,8},{1,5},{5,1},{9,13},{13,9},{2,6},{6,2},{1... | collective-permute-start | bytes 2312 | tf_op jit(solution)/shard_map/ppermute | solution.py:208
  646.4 18.8 %collective-permute-start.84 = (bf16[192,608]{1,0:T(8,128)(2,1)S(1)}, bf16[192,608]{1,0:T(8,128)(2,1)S(1)}, u32[]{:S(2)}, u32[]{:S(2)}) collective-permute-start(bf16[192,608]{1,0:T(8,128)(2,1)S(1)} %get-tuple-element.52), channel_id=1, source_target_pairs={{0,4},{4,0},{8,12},{12,8},{1,5},{5,1},{9,13},{13,9},{2,6},{6,2},{1... | collective-permute-start | bytes 700424 | tf_op jit(solution)/shard_map/ppermute | solution.py:207
  649.2 16.1 %collective-permute-start.85 = (bf16[192,608]{1,0:T(8,128)(2,1)S(1)}, bf16[192,608]{1,0:T(8,128)(2,1)S(1)}, u32[]{:S(2)}, u32[]{:S(2)}) collective-permute-start(bf16[192,608]{1,0:T(8,128)(2,1)S(1)} %get-tuple-element.54), channel_id=1, source_target_pairs={{0,8},{4,12},{8,0},{12,4},{1,9},{5,13},{9,1},{13,5},{2,10},{6,14},... | collective-permute-start | bytes 700424 | tf_op jit(solution)/shard_map/ppermute | solution.py:207
  652.3 12.9 %collective-permute-start.86 = (bf16[192,608]{1,0:T(8,128)(2,1)S(1)}, bf16[192,608]{1,0:T(8,128)(2,1)S(1)}, u32[]{:S(2)}, u32[]{:S(2)}) collective-permute-start(bf16[192,608]{1,0:T(8,128)(2,1)S(1)} %get-tuple-element.53), channel_id=1, source_target_pairs={{0,12},{4,8},{8,4},{12,0},{1,13},{5,9},{9,5},{13,1},{2,14},{6,10},... | collective-permute-start | bytes 700424 | tf_op jit(solution)/shard_map/ppermute | solution.py:207
  (190 other events, 1841.3 us)
Sparse Core Ops, SparseCore 0:
  11.0 73.9 all-gather.8
  86.6 61.4 all-gather.10
  149.7 61.6 all-gather.12
  212.8 61.6 all-gather.14
